TPU v7x, 128 devices: a whole 4x4x4 slice. The times are simulated.
128 devices in a mesh: req: 16 (over y, x), cache: 8 (over z, core).
Axes of the slice: x: 4, y: 4, z: 4, core: 2. Of those that a mesh axis runs over, the one named last changes fastest.
Arguments:
- cand_x: bfloat16 [32768, 1024], P(('req', 'cache')), may hold values from -6 to 6
- cand_req: int32 [32768, 1], P(('req', 'cache')), may hold values from 0 to 127; in each aligned block of 256 rows (0 to 255, 256 to 511, ...) at most 4 rows name the same one
- hist_len: int32 [128], P(('req', 'cache')), may hold values from 1 to 2048, 131072 in all
- block_place: int32 [128, 128], P(('req', 'cache')), may hold values from 0 to 127, each once within a row
- kv_store: bfloat16 [128, 128, 1, 16, 2048], P(('req', 'cache')), may hold values from -6 to 6
- store_bucket: int32 [128, 128, 1, 16], P(('req', 'cache')), may hold values from 1 to 127
- w_proj: bfloat16 [1024, 2048], replicated, may hold values from -0.1875 to 0.1875
- w_out: bfloat16 [1024, 1024], replicated, may hold values from -0.1875 to 0.1875
- time_bias: float32 [8, 128], replicated, may hold values from -4 to 4
Outputs:
- scored: bfloat16 [32768, 1024], P(('req', 'cache'))
Inputs may be any that keep to these rules, and one draw needn't show every extreme that they name: `cand_req`: among the 256 candidate rows of one device at most 4 belong to one request, and some request of some device has exactly 4. `hist_len`: the lengths sum to 131072. `block_place`: each row is a permutation of 0 to 127.
All inputs are finite; a program needn't handle non-finite values. No bound on the sum of `hist_len` on one device may be relied on, other than what follows from the above.
Results may differ from a plain program's by a relative error of at most 0.0055.
Values may be sent and summed in bfloat16 or wider, within the bound.
No kernel may reach another device: no remote copies, remote signals or barrier semaphores. Data moves between devices by JAX's collectives and lax.ppermute only.
A program may use at most 128 MiB of HBM per device.

v0:
```python
import math

import jax
import jax.numpy as jnp
from jax import lax
from jax.sharding import PartitionSpec as P


def layer_norm(values):
    average = jnp.mean(values, axis=-1, keepdims=True)
    centred = values - average
    spread = jnp.mean(centred * centred, axis=-1, keepdims=True)
    return centred * lax.rsqrt(spread + 1e-05)


def prepare(inputs, w_proj):
    normed = layer_norm(inputs.astype(jnp.float32)).astype(jnp.bfloat16)
    return jax.nn.silu(jnp.dot(normed, w_proj, preferred_element_type=jnp.float32)).astype(
        jnp.bfloat16
    )


def send_back(update):
    return lax.all_to_all(update, ("req", "cache"), split_axis=0, concat_axis=0, tiled=True)


def shards(
    cand_x, cand_req, hist_len, block_place, kv_store, store_bucket, w_proj, w_out, time_bias
):
    devices = lax.axis_size(("req", "cache"))
    row_count = cand_x.shape[0]
    features = cand_x.shape[1]
    head_count = time_bias.shape[0]
    head_dim = features // head_count
    bucket_count = time_bias.shape[1]
    per_owner = kv_store.shape[2]
    block_ev = kv_store.shape[3]
    capacity = max(2, 2 * row_count // devices)
    arrived, arrived_bucket = (
        lax.all_to_all(kv_store, ("req", "cache"), split_axis=1, concat_axis=0, tiled=True),
        lax.all_to_all(store_bucket, ("req", "cache"), split_axis=1, concat_axis=0, tiled=True),
    )
    event_count = devices * per_owner * block_ev
    events = arrived.reshape(event_count, 2 * features)
    buckets = arrived_bucket.reshape(event_count)
    places = block_place[0]
    block_count = places.shape[0]
    block_ids = jnp.arange(block_count, dtype=jnp.int32)
    match = (places[:, None] == block_ids[None, :]).astype(jnp.int32)
    block_of_place = jnp.sum(match * block_ids[:, None], axis=0)
    position = (
        block_of_place[:, None] * block_ev + jnp.arange(block_ev, dtype=jnp.int32)[None, :]
    ).reshape(event_count)
    live = (position < hist_len[0]).astype(jnp.float32)
    bucket_table = (buckets[None, :] == jnp.arange(bucket_count, dtype=jnp.int32)[:, None]).astype(
        jnp.float32
    )
    bias = jnp.dot(time_bias, bucket_table, precision=lax.Precision.HIGHEST)
    score_scale = 1.0 / math.sqrt(head_dim)
    target = cand_req[:, 0]
    onehot = (target[:, None] == jnp.arange(devices, dtype=jnp.int32)[None, :]).astype(jnp.int32)
    earlier = jnp.cumsum(onehot, axis=0) - onehot
    slot_rank = jnp.sum(earlier * onehot, axis=1)
    flat_slot = target * capacity + slot_rank
    empty = jnp.zeros((devices * capacity, cand_x.shape[1]), cand_x.dtype)
    received = lax.all_to_all(
        empty.at[flat_slot].set(cand_x).reshape(devices, capacity, cand_x.shape[1]),
        ("req", "cache"),
        split_axis=0,
        concat_axis=0,
        tiled=True,
    )
    senders = received.shape[0]
    item_count = received.shape[1]
    flat_rows = received.reshape(senders * item_count, features)
    projected = prepare(flat_rows, w_proj)
    slot_count = projected.shape[0]
    gate_u = projected[:, :features]
    query = projected[:, features:]

    def one_head(head_index):
        start = head_index * head_dim
        query_head = lax.dynamic_slice_in_dim(query, start, head_dim, 1)
        key_head = lax.dynamic_slice_in_dim(events, start, head_dim, 1)
        value_head = lax.dynamic_slice_in_dim(events, features + start, head_dim, 1)
        bias_head = lax.dynamic_slice_in_dim(bias, head_index, 1, 0)
        scores = lax.dot_general(
            query_head, key_head, (((1,), (1,)), ((), ())), preferred_element_type=jnp.float32
        )
        weight = (jax.nn.silu(scores * score_scale + bias_head) * live[None, :]).astype(
            jnp.bfloat16
        )
        return jnp.dot(weight, value_head, preferred_element_type=jnp.float32)

    per_head = lax.map(one_head, jnp.arange(head_count, dtype=jnp.int32))
    attended = jnp.transpose(per_head, (1, 0, 2)).reshape(slot_count, features)
    hidden = (layer_norm(attended) * gate_u.astype(jnp.float32)).astype(jnp.bfloat16)
    update = (
        jnp.dot(hidden, w_out, preferred_element_type=jnp.float32)
        .astype(jnp.bfloat16)
        .reshape(senders, item_count, features)
    )
    returned = send_back(update)
    update = returned.reshape(devices * capacity, features)[flat_slot]
    return (cand_x.astype(jnp.float32) + update.astype(jnp.float32)).astype(jnp.bfloat16)


def solution(mesh):
    placed = (
        P(("req", "cache"), None),
        P(("req", "cache"), None),
        P(("req", "cache")),
        P(("req", "cache"), None),
        P(("req", "cache"), None, None, None, None),
        P(("req", "cache"), None, None, None),
        P(),
        P(),
        P(),
    )
    return jax.shard_map(
        shards, mesh=mesh, in_specs=placed, out_specs=P(("req", "cache"), None), check_vma=False
    )
```

profile of v0, /device:TPU:1, one launch (start us, length us, event | category | flops | bytes accessed | tf_op | source)
XLA Modules:
  0.0 257.6 jit_solution(16259972353692370718)
XLA Ops:
  0.0 1.6 copy.24
  1.6 11.5 %all-to-all-start.2 = ((s32[1,128,1,16]{3,2,0,1:T(1,128)}), s32[1,128,1,16]{3,2,0,1:T(1,128)S(1)}, u32[]{:S(2)}, u32[]{:S(2)}) async-start(s32[1,128,1,16]{3,2,0,1:T(1,128)} %copy.24), calls=%async_computation.2 | async-start | bytes 131072 | tf_op jit(solution)/shard_map/all_to_all | solution.py:41
  13.1 0.8 copy.21
  14.2 0.9 fusion.32
  15.0 0.7 compare_select_fusion
  15.7 2.4 scatter_custom_fusion
  18.1 1.2 reshape.108
  19.4 3.1 %all-to-all-done.2 = s32[1,128,1,16]{3,2,0,1:T(1,128)S(1)} async-done(((s32[1,128,1,16]{3,2,0,1:T(1,128)}), s32[1,128,1,16]{3,2,0,1:T(1,128)S(1)}, u32[]{:S(2)}, u32[]{:S(2)}) %all-to-all-start.2) | async-done | bytes 8224 | tf_op jit(solution)/shard_map/all_to_all | solution.py:41
  22.4 25.7 %all_to_all.28 = bf16[128,4,1024]{2,1,0:T(4,128)(2,1)S(1)} all-to-all(bf16[128,4,1024]{2,1,0:T(4,128)(2,1)} %reshape.108), channel_id=1, replica_groups=mesh['req'=16,'cache'=8] {'req','cache'}, dimensions={0} | all-to-all | bytes 2097152 | tf_op jit(solution)/shard_map/all_to_all | solution.py:66
  48.2 6.1 %all-to-all-start.1 = ((bf16[1,128,1,16,2048]{4,3,2,0,1:T(8,128)(2,1)}), bf16[1,128,1,16,2048]{4,3,2,0,1:T(8,128)(2,1)}, u32[]{:S(2)}, u32[]{:S(2)}) async-start(bf16[1,128,1,16,2048]{4,3,2,0,1:T(8,128)(2,1)} %bitcast.58), calls=%async_computation.1 | async-start | bytes 16777216 | tf_op jit(solution)/shard_map/all_to_all | solution.py:40
  54.9 0.7 reduce.8
  56.7 0.8 multiply_reduce_fusion
  57.7 1.5 reshape.113
  59.2 5.7 %multiply_convert_fusion.1 = bf16[512,2048]{1,0:T(8,128)(2,1)S(1)} fusion(bf16[1024,2048]{1,0:T(8,128)(2,1)} %param.17, f32[512,1024]{1,0:T(8,128)} %reshape.113, f32[512]{0:T(512)S(1)} %rsqrt.20, f32[512]{0:T(512)S(1)} %div.25), kind=kOutput, calls=%fused_computation.16 | convolution fusion | flops 2154299392 | bytes 8392704 | tf_op jit(solution)/shard_map/dot_general | solution.py:18
  64.9 1.4 copy-done.2
  66.4 89.5 %all-to-all-done.1 = bf16[1,128,1,16,2048]{4,3,2,0,1:T(8,128)(2,1)} async-done(((bf16[1,128,1,16,2048]{4,3,2,0,1:T(8,128)(2,1)}), bf16[1,128,1,16,2048]{4,3,2,0,1:T(8,128)(2,1)}, u32[]{:S(2)}, u32[]{:S(2)}) %all-to-all-start.1) | async-done | bytes 8388640 | tf_op jit(solution)/shard_map/all_to_all | solution.py:40
  155.9 58.1 %while.13 = (s32[]{:T(128)}, f32[8,512,128]{2,1,0:T(8,128)}, s32[8]{0:T(128)S(1)}, bf16[512,1024]{1,0:T(8,128)(2,1)S(1)}, bf16[2048,2048]{1,0:T(8,128)(2,1)}, /*...) while((s32[]{:T(128)}, f32[8,512,128]{2,1,0:T(8,128)}, ...), condition=%wide.region_8.9_spmd.clone, body=%wide.region_7.8_spmd.clone.sunk | while | flops 545265664 | bytes 1500472 | solution.py:95
  155.9 0.6 dynamic_slice.54
  159.0 0.7 fusion.47
  159.8 3.4 %fusion.48 = f32[8,512,128]{2,1,0:T(8,128)} fusion(f32[8,512,128]{2,1,0:T(8,128)} %get-tuple-element.196, s32[]{:T(128)} %get-tuple-element.195, f32[2048]{0:T(1024)S(1)} %reshape.147, f32[2048]{0:T(1024)S(1)} %bitcast.61, bf16[2048,2048]{1,0:T(8,128)(2,1)} %get-tuple-element.214, s32[]{:T(128)S(6)} %select_n.40, s32[]{:T(128)S(6)} %select_n.41, ...), kind=kOutput, calls=%fused_computation.6.clone.1 | convolution fusion | flops 545259520 | bytes 1458700 | tf_op jit(solution)/shard_map/while/body/eval_jaxpr/dot_general | solution.py:93
  163.2 0.6 dynamic_slice.54
  166.2 0.7 fusion.47
  167.1 3.4 %fusion.48 = f32[8,512,128]{2,1,0:T(8,128)} fusion(f32[8,512,128]{2,1,0:T(8,128)} %get-tuple-element.196, s32[]{:T(128)} %get-tuple-element.195, f32[2048]{0:T(1024)S(1)} %reshape.147, f32[2048]{0:T(1024)S(1)} %bitcast.61, bf16[2048,2048]{1,0:T(8,128)(2,1)} %get-tuple-element.214, s32[]{:T(128)S(6)} %select_n.40, s32[]{:T(128)S(6)} %select_n.41, ...), kind=kOutput, calls=%fused_computation.6.clone.1 | convolution fusion | flops 545259520 | bytes 1458700 | tf_op jit(solution)/shard_map/while/body/eval_jaxpr/dot_general | solution.py:93
  170.4 0.6 dynamic_slice.54
  173.5 0.7 fusion.47
  174.3 3.4 %fusion.48 = f32[8,512,128]{2,1,0:T(8,128)} fusion(f32[8,512,128]{2,1,0:T(8,128)} %get-tuple-element.196, s32[]{:T(128)} %get-tuple-element.195, f32[2048]{0:T(1024)S(1)} %reshape.147, f32[2048]{0:T(1024)S(1)} %bitcast.61, bf16[2048,2048]{1,0:T(8,128)(2,1)} %get-tuple-element.214, s32[]{:T(128)S(6)} %select_n.40, s32[]{:T(128)S(6)} %select_n.41, ...), kind=kOutput, calls=%fused_computation.6.clone.1 | convolution fusion | flops 545259520 | bytes 1458700 | tf_op jit(solution)/shard_map/while/body/eval_jaxpr/dot_general | solution.py:93
  177.7 0.6 dynamic_slice.54
  180.8 0.7 fusion.47
  181.6 3.4 %fusion.48 = f32[8,512,128]{2,1,0:T(8,128)} fusion(f32[8,512,128]{2,1,0:T(8,128)} %get-tuple-element.196, s32[]{:T(128)} %get-tuple-element.195, f32[2048]{0:T(1024)S(1)} %reshape.147, f32[2048]{0:T(1024)S(1)} %bitcast.61, bf16[2048,2048]{1,0:T(8,128)(2,1)} %get-tuple-element.214, s32[]{:T(128)S(6)} %select_n.40, s32[]{:T(128)S(6)} %select_n.41, ...), kind=kOutput, calls=%fused_computation.6.clone.1 | convolution fusion | flops 545259520 | bytes 1458700 | tf_op jit(solution)/shard_map/while/body/eval_jaxpr/dot_general | solution.py:93
  185.0 0.6 dynamic_slice.54
  188.0 0.7 fusion.47
  188.9 3.4 %fusion.48 = f32[8,512,128]{2,1,0:T(8,128)} fusion(f32[8,512,128]{2,1,0:T(8,128)} %get-tuple-element.196, s32[]{:T(128)} %get-tuple-element.195, f32[2048]{0:T(1024)S(1)} %reshape.147, f32[2048]{0:T(1024)S(1)} %bitcast.61, bf16[2048,2048]{1,0:T(8,128)(2,1)} %get-tuple-element.214, s32[]{:T(128)S(6)} %select_n.40, s32[]{:T(128)S(6)} %select_n.41, ...), kind=kOutput, calls=%fused_computation.6.clone.1 | convolution fusion | flops 545259520 | bytes 1458700 | tf_op jit(solution)/shard_map/while/body/eval_jaxpr/dot_general | solution.py:93
  192.2 0.6 dynamic_slice.54
  195.3 0.7 fusion.47
  196.1 3.4 %fusion.48 = f32[8,512,128]{2,1,0:T(8,128)} fusion(f32[8,512,128]{2,1,0:T(8,128)} %get-tuple-element.196, s32[]{:T(128)} %get-tuple-element.195, f32[2048]{0:T(1024)S(1)} %reshape.147, f32[2048]{0:T(1024)S(1)} %bitcast.61, bf16[2048,2048]{1,0:T(8,128)(2,1)} %get-tuple-element.214, s32[]{:T(128)S(6)} %select_n.40, s32[]{:T(128)S(6)} %select_n.41, ...), kind=kOutput, calls=%fused_computation.6.clone.1 | convolution fusion | flops 545259520 | bytes 1458700 | tf_op jit(solution)/shard_map/while/body/eval_jaxpr/dot_general | solution.py:93
  202.6 0.7 fusion.47
  203.4 3.4 %fusion.48 = f32[8,512,128]{2,1,0:T(8,128)} fusion(f32[8,512,128]{2,1,0:T(8,128)} %get-tuple-element.196, s32[]{:T(128)} %get-tuple-element.195, f32[2048]{0:T(1024)S(1)} %reshape.147, f32[2048]{0:T(1024)S(1)} %bitcast.61, bf16[2048,2048]{1,0:T(8,128)(2,1)} %get-tuple-element.214, s32[]{:T(128)S(6)} %select_n.40, s32[]{:T(128)S(6)} %select_n.41, ...), kind=kOutput, calls=%fused_computation.6.clone.1 | convolution fusion | flops 545259520 | bytes 1458700 | tf_op jit(solution)/shard_map/while/body/eval_jaxpr/dot_general | solution.py:93
  209.8 0.7 fusion.47
  210.6 3.4 %fusion.48 = f32[8,512,128]{2,1,0:T(8,128)} fusion(f32[8,512,128]{2,1,0:T(8,128)} %get-tuple-element.196, s32[]{:T(128)} %get-tuple-element.195, f32[2048]{0:T(1024)S(1)} %reshape.147, f32[2048]{0:T(1024)S(1)} %bitcast.61, bf16[2048,2048]{1,0:T(8,128)(2,1)} %get-tuple-element.214, s32[]{:T(128)S(6)} %select_n.40, s32[]{:T(128)S(6)} %select_n.41, ...), kind=kOutput, calls=%fused_computation.6.clone.1 | convolution fusion | flops 545259520 | bytes 1458700 | tf_op jit(solution)/shard_map/while/body/eval_jaxpr/dot_general | solution.py:93
  214.0 1.8 reduce_sum.61
  215.8 2.1 fusion.19
  218.0 2.6 convolution_convert_fusion
  220.6 1.2 reshape.111
  221.8 11.5 %all-to-all-start.3 = ((bf16[128,4,1024]{2,1,0:T(4,128)(2,1)}), bf16[128,4,1024]{2,1,0:T(4,128)(2,1)}, u32[]{:S(2)}, u32[]{:S(2)}) async-start(bf16[128,4,1024]{2,1,0:T(4,128)(2,1)} %reshape.111), calls=%async_computation.3 | async-start | bytes 2097152 | tf_op jit(solution)/shard_map/all_to_all | solution.py:24
  233.4 18.7 %all-to-all-done.3 = bf16[128,4,1024]{2,1,0:T(4,128)(2,1)} async-done(((bf16[128,4,1024]{2,1,0:T(4,128)(2,1)}), bf16[128,4,1024]{2,1,0:T(4,128)(2,1)}, u32[]{:S(2)}, u32[]{:S(2)}) %all-to-all-start.3) | async-done | bytes 1048608 | tf_op jit(solution)/shard_map/all_to_all | solution.py:24
  252.1 1.3 reshape.112
  253.4 2.0 gather_fusion
  255.4 2.2 add_convert_fusion
  (50 shorter events, 4.3 us)
Async XLA Ops:
  0.0 217.9 %copy-start = (bf16[1024,1024]{1,0:T(8,128)(2,1)S(1)}, bf16[1024,1024]{1,0:T(8,128)(2,1)}, u32[]{:S(2)}) copy-start(bf16[1024,1024]{1,0:T(8,128)(2,1)} %param.18) | copy-start | bytes 6291460
  1.6 20.9 %all-to-all-start.2 = ((s32[1,128,1,16]{3,2,0,1:T(1,128)}), s32[1,128,1,16]{3,2,0,1:T(1,128)S(1)}, u32[]{:S(2)}, u32[]{:S(2)}) async-start(s32[1,128,1,16]{3,2,0,1:T(1,128)} %copy.24), calls=%async_computation.2 | async-start | bytes 131072 | tf_op jit(solution)/shard_map/all_to_all | solution.py:41
  48.2 6.1 %copy-start.4 = (s32[1,128]{1,0:T(1,128)S(1)}, s32[1,128]{1,0:T(1,128)}, u32[]{:S(2)}) copy-start(s32[1,128]{1,0:T(1,128)} %param.14) | copy-start | bytes 1540
  48.2 7.5 %copy-start.3 = (f32[8,128]{1,0:T(8,128)S(1)}, f32[8,128]{1,0:T(8,128)}, u32[]{:S(2)}) copy-start(f32[8,128]{1,0:T(8,128)} %param.19) | copy-start | bytes 12292
  48.2 107.7 %all-to-all-start.1 = ((bf16[1,128,1,16,2048]{4,3,2,0,1:T(8,128)(2,1)}), bf16[1,128,1,16,2048]{4,3,2,0,1:T(8,128)(2,1)}, u32[]{:S(2)}, u32[]{:S(2)}) async-start(bf16[1,128,1,16,2048]{4,3,2,0,1:T(8,128)(2,1)} %bitcast.58), calls=%async_computation.1 | async-start | bytes 16777216 | tf_op jit(solution)/shard_map/all_to_all | solution.py:40
  64.9 1.4 copy-start.2
  215.8 2.2 copy-start.1
  221.8 30.2 %all-to-all-start.3 = ((bf16[128,4,1024]{2,1,0:T(4,128)(2,1)}), bf16[128,4,1024]{2,1,0:T(4,128)(2,1)}, u32[]{:S(2)}, u32[]{:S(2)}) async-start(bf16[128,4,1024]{2,1,0:T(4,128)(2,1)} %reshape.111), calls=%async_computation.3 | async-start | bytes 2097152 | tf_op jit(solution)/shard_map/all_to_all | solution.py:24
where the time goes:
time: 259 us; the launch traced here: 258 us
  waiting for transfers between devices  111 us (43%)
  matrix products  35.7 us (14%)
  starting transfers between devices  29.1 us (11%)
  blocking collectives  25.7 us (10%)
  local copies, waits for them, and re-layouts  20 us (8%)
  loops' own time  19.7 us (8%)
  other arithmetic  15.8 us (6%)
    all_to_all x1, waiting for transfers between devices, shards(): lax.all_to_all(kv_store, ('req', 'cache'), split_axis=1, concat_axis=0, t...  89.5 us
    dot_general x8, matrix products, one_head(): return jnp.dot(weight, value_head, preferred_element_type=jnp.float32)  27 us
    all_to_all x1, blocking collectives, shards(): lax.all_to_all(empty.at[flat_slot].set(cand_x).reshape(devices, capacity,...  25.7 us
    another operation x1, loops' own time, shards(): per_head = lax.map(one_head, jnp.arange(head_count, dtype=jnp.int32))  19.7 us
    all_to_all x1, waiting for transfers between devices, send_back(): lax.all_to_all(update, ('req', 'cache'), split_axis=0, concat_axis=0, til...  18.7 us
    all_to_all x1, starting transfers between devices, send_back(): lax.all_to_all(update, ('req', 'cache'), split_axis=0, concat_axis=0, til...  11.5 us
    all_to_all x1, starting transfers between devices, shards(): lax.all_to_all(store_bucket, ('req', 'cache'), split_axis=1, concat_axis=...  11.5 us
    all_to_all x1, starting transfers between devices, shards(): lax.all_to_all(kv_store, ('req', 'cache'), split_axis=1, concat_axis=0, t...  6.09 us
  transfers between devices with their start and end apart: 3, of which 3 were waited for; matrix products, arithmetic and copies ran while one was open for 7% of the time, Pallas kernels for 0%

commit v1 on v0

v1 whole, which is shorter than its diff:
```python
import functools
import math

import jax
import jax.numpy as jnp
from jax import lax
from jax.experimental import pallas as pl
from jax.experimental.pallas import tpu as pltpu
from jax.sharding import PartitionSpec as P


def layer_norm(values):
    average = jnp.mean(values, axis=-1, keepdims=True)
    centred = values - average
    spread = jnp.mean(centred * centred, axis=-1, keepdims=True)
    return centred * lax.rsqrt(spread + 1e-05)


def prepare(inputs, w_proj):
    normed = layer_norm(inputs.astype(jnp.float32)).astype(jnp.bfloat16)
    return jax.nn.silu(jnp.dot(normed, w_proj, preferred_element_type=jnp.float32)).astype(
        jnp.bfloat16
    )


def attend_kernel(q_ref, k_ref, v_ref, bias_ref, live_ref, o_ref, *, scale, chunk):
    head = pl.program_id(0)
    query = q_ref[...]
    bias_row = bias_ref[pl.ds(head, 1), :]
    live_row = live_ref[...]
    event_count = k_ref.shape[0]
    acc = jnp.zeros(o_ref.shape, jnp.float32)
    for c in range(event_count // chunk):
        lo = c * chunk
        key = k_ref[pl.ds(lo, chunk), :]
        value = v_ref[pl.ds(lo, chunk), :]
        scores = lax.dot_general(
            query, key, (((1,), (1,)), ((), ())), preferred_element_type=jnp.float32
        )
        scores = scores * scale + bias_row[:, lo : lo + chunk]
        silu = scores / (1.0 + jnp.exp(-scores))
        weight = jnp.where(live_row[:, lo : lo + chunk] > 0.0, silu, 0.0).astype(jnp.bfloat16)
        acc = acc + jnp.dot(weight, value, preferred_element_type=jnp.float32)
    o_ref[...] = acc


def attend(projected, events, bias, live, head_count, head_dim, scale):
    slot_count = projected.shape[0]
    event_count = events.shape[0]
    features = head_count * head_dim
    slot_tile = 256 if slot_count % 256 == 0 else slot_count
    chunk = 512 if event_count % 512 == 0 else event_count
    kernel = functools.partial(attend_kernel, scale=scale, chunk=chunk)
    return pl.pallas_call(
        kernel,
        grid=(head_count, slot_count // slot_tile),
        in_specs=[
            pl.BlockSpec((slot_tile, head_dim), lambda h, i: (i, head_count + h)),
            pl.BlockSpec((event_count, head_dim), lambda h, i: (0, h)),
            pl.BlockSpec((event_count, head_dim), lambda h, i: (0, head_count + h)),
            pl.BlockSpec(bias.shape, lambda h, i: (0, 0)),
            pl.BlockSpec(live.shape, lambda h, i: (0, 0)),
        ],
        out_specs=pl.BlockSpec((slot_tile, head_dim), lambda h, i: (i, h)),
        out_shape=jax.ShapeDtypeStruct((slot_count, features), jnp.float32),
    )(projected, events, events, bias, live)


def shards(
    cand_x, cand_req, hist_len, block_place, kv_store, store_bucket, w_proj, w_out, time_bias
):
    axes = ("req", "cache")
    devices = lax.axis_size(axes)
    row_count = cand_x.shape[0]
    features = cand_x.shape[1]
    head_count = time_bias.shape[0]
    head_dim = features // head_count
    bucket_count = time_bias.shape[1]
    per_owner = kv_store.shape[2]
    block_ev = kv_store.shape[3]
    capacity = max(2, 2 * row_count // devices)
    arrived = lax.all_to_all(kv_store, axes, split_axis=1, concat_axis=0, tiled=True)
    event_count = devices * per_owner * block_ev
    events = arrived.reshape(event_count, 2 * features)

    target = cand_req[:, 0]
    onehot = (target[:, None] == jnp.arange(devices, dtype=jnp.int32)[None, :]).astype(jnp.int32)
    earlier = jnp.cumsum(onehot, axis=0) - onehot
    slot_rank = jnp.sum(earlier * onehot, axis=1)
    flat_slot = target * capacity + slot_rank
    empty = jnp.zeros((devices * capacity, features), cand_x.dtype)
    slotted = empty.at[flat_slot].set(cand_x).reshape(devices, capacity * features)
    bucket_send = store_bucket.reshape(devices, per_owner * block_ev).astype(cand_x.dtype)
    received = lax.all_to_all(
        jnp.concatenate([slotted, bucket_send], axis=1), axes, split_axis=0, concat_axis=0, tiled=True
    )
    senders = received.shape[0]
    flat_rows = received[:, : capacity * features].reshape(senders * capacity, features)
    buckets = received[:, capacity * features :].astype(jnp.int32).reshape(event_count)

    places = block_place[0]
    block_count = places.shape[0]
    block_ids = jnp.arange(block_count, dtype=jnp.int32)
    match = (places[:, None] == block_ids[None, :]).astype(jnp.int32)
    block_of_place = jnp.sum(match * block_ids[:, None], axis=0)
    position = (
        block_of_place[:, None] * block_ev + jnp.arange(block_ev, dtype=jnp.int32)[None, :]
    ).reshape(1, event_count)
    live = (position < hist_len[0]).astype(jnp.float32)
    bucket_table = (buckets[None, :] == jnp.arange(bucket_count, dtype=jnp.int32)[:, None]).astype(
        jnp.float32
    )
    bias = jnp.dot(time_bias, bucket_table, precision=lax.Precision.HIGHEST)
    score_scale = 1.0 / math.sqrt(head_dim)

    projected = prepare(flat_rows, w_proj)
    slot_count = projected.shape[0]
    gate_u = projected[:, :features]
    attended = attend(projected, events, bias, live, head_count, head_dim, score_scale)
    hidden = (layer_norm(attended) * gate_u.astype(jnp.float32)).astype(jnp.bfloat16)
    update = (
        jnp.dot(hidden, w_out, preferred_element_type=jnp.float32)
        .astype(jnp.bfloat16)
        .reshape(senders, capacity, features)
    )
    returned = lax.all_to_all(update, axes, split_axis=0, concat_axis=0, tiled=True)
    update = returned.reshape(devices * capacity, features)[flat_slot]
    return (cand_x.astype(jnp.float32) + update.astype(jnp.float32)).astype(jnp.bfloat16)


def solution(mesh):
    placed = (
        P(("req", "cache"), None),
        P(("req", "cache"), None),
        P(("req", "cache")),
        P(("req", "cache"), None),
        P(("req", "cache"), None, None, None, None),
        P(("req", "cache"), None, None, None),
        P(),
        P(),
        P(),
    )
    return jax.shard_map(
        shards, mesh=mesh, in_specs=placed, out_specs=P(("req", "cache"), None), check_vma=False
    )
```

time: 259 us -> 222 us (0.86)
  matrix products: 35.7 us -> 10.1 us
  Pallas kernels: 0 us -> 22.2 us
  loops' own time: 19.7 us -> 0 us
  waiting for transfers between devices: 111 us -> 91.4 us
  starting transfers between devices: 29.1 us -> 17.4 us
  local copies, waits for them, and re-layouts: 20 us -> 30.9 us
  blocking collectives: 25.7 us -> 31.2 us
    dot_general x8 -> x0, matrix products: 27 us -> none  [one_head(): return jnp.dot(weight, value_head, preferred_element_type=jnp.float32)]
    pallas_call x0 -> x1, Pallas kernels: none -> 22.2 us  [attend(): pl.pallas_call(kernel, grid=(head_count, slot_count // slot_tile), in_spe...]
    all_to_all x3 -> x2, waiting for transfers between devices: 111 us -> 91.4 us  [the longest x1 72.8 us: shards(): lax.all_to_all(kv_store, axes, split_axis=1, concat_axis=0, tiled=True)]
    another operation x1 -> x0, loops' own time: 19.7 us -> none  [shards(): per_head = lax.map(one_head, jnp.arange(head_count, dtype=jnp.int32))]
    all_to_all x3 -> x2, starting transfers between devices: 29.1 us -> 17.4 us  [the longest x1 11.4 us: shards(): lax.all_to_all(update, axes, split_axis=0, concat_axis=0, tiled=True)]
    convert_element_type x8 -> x1, other arithmetic: 5.81 us -> 0.08 us  [shards(): live = (position < hist_len[0]).astype(jnp.float32)]
    all_to_all x1, blocking collectives: 25.7 us -> 31.2 us  [shards(): lax.all_to_all(jnp.concatenate([slotted, bucket_send], axis=1), axes, spl...]
    all_to_all x1 -> x2, local copies, waits for them, and re-layouts: 0.49 us -> 5.59 us  [shards(): lax.all_to_all(jnp.concatenate([slotted, bucket_send], axis=1), axes, spl...]
  transfers between devices with their start and end apart: 3 -> 2, of which waited for: 3 -> 2; matrix products, arithmetic and copies ran while one was open for 7% -> 13% of each run, Pallas kernels for 0% -> 0%
where the time goes in v1:
time: 222 us; the launch traced here: 221 us
  waiting for transfers between devices  91.4 us (41%)
  blocking collectives  31.2 us (14%)
  local copies, waits for them, and re-layouts  30.9 us (14%)
  Pallas kernels  22.2 us (10%)
  starting transfers between devices  17.4 us (8%)
  other arithmetic  16.7 us (8%)
  matrix products  10.1 us (5%)
    all_to_all x1, waiting for transfers between devices, shards(): lax.all_to_all(kv_store, axes, split_axis=1, concat_axis=0, tiled=True)  72.8 us
    all_to_all x1, blocking collectives, shards(): lax.all_to_all(jnp.concatenate([slotted, bucket_send], axis=1), axes, spl...  31.2 us
    pallas_call x1, Pallas kernels, attend(): pl.pallas_call(kernel, grid=(head_count, slot_count // slot_tile), in_spe...  22.2 us
    all_to_all x1, waiting for transfers between devices, shards(): lax.all_to_all(update, axes, split_axis=0, concat_axis=0, tiled=True)  18.7 us
    all_to_all x1, starting transfers between devices, shards(): lax.all_to_all(update, axes, split_axis=0, concat_axis=0, tiled=True)  11.4 us
    unnamed x16, local copies, waits for them, and re-layouts  7.01 us
    dot_general x1, matrix products, prepare(): jnp.dot(normed, w_proj, preferred_element_type=jnp.float32)  6.47 us
    all_to_all x1, starting transfers between devices, shards(): lax.all_to_all(kv_store, axes, split_axis=1, concat_axis=0, tiled=True)  6.08 us
  transfers between devices with their start and end apart: 2, of which 2 were waited for; matrix products, arithmetic and copies ran while one was open for 13% of the time, Pallas kernels for 0%

profile of v1, /device:TPU:1, one launch (start us, length us, event | category | flops | bytes accessed | tf_op | source)
XLA Modules:
  0.0 220.9 jit_solution(15377902289617898380)
XLA Ops:
  0.0 0.0 copy-start
  0.0 0.9 copy.34
  0.9 0.2 fusion.9
  1.2 0.9 fusion.11
  2.1 0.7 compare_select_fusion
  2.8 2.4 %scatter_custom_fusion = bf16[512,1024]{1,0:T(8,128)(2,1)S(1)} fusion(s32[256]{0:T(256)S(1)} %bitcast.41, bf16[256,1024]{1,0:T(8,128)(2,1)} %param.9, bf16[]{:T(256)} %constant.9.clone.1), kind=kCustom, calls=%fused_computation.20 | custom fusion | bytes 1049088 | tf_op jit(solution)/shard_map/scatter | solution.py:92
  5.2 0.0 copy-start.3
  5.2 1.5 reshape.105
  6.7 2.3 %copy.36 = bf16[128,4096]{0,1:T(8,128)(2,1)} copy(bf16[128,4096]{1,0:T(8,128)(2,1)} %reshape.105) | data formatting | bytes 2097152 | tf_op jit(solution)/shard_map/reshape | solution.py:92
  9.0 0.0 copy-done.3
  9.0 1.3 maximum_bitcast_fusion
  10.3 0.5 broadcast.108
  10.8 2.1 reduce
  12.9 1.7 copy.42
  14.6 1.6 reshape.130
  16.2 31.2 %all_to_all.26 = bf16[128,2,2056]{2,1,0:T(2,128)(2,1)S(1)} all-to-all(bf16[128,2,2056]{2,1,0:T(2,128)(2,1)} %reshape.130), channel_id=1, replica_groups=mesh['req'=16,'cache'=8] {'req','cache'}, dimensions={0} | all-to-all | bytes 2105344 | tf_op jit(solution)/shard_map/all_to_all | solution.py:94
  47.4 0.0 copy-start.5
  47.4 6.1 %all-to-all-start.1 = ((bf16[1,128,1,16,2048]{4,3,2,0,1:T(8,128)(2,1)}), bf16[1,128,1,16,2048]{4,3,2,0,1:T(8,128)(2,1)}, u32[]{:S(2)}, u32[]{:S(2)}) async-start(bf16[1,128,1,16,2048]{4,3,2,0,1:T(8,128)(2,1)} %bitcast.32), calls=%async_computation.1 | async-start | bytes 16777216 | tf_op jit(solution)/shard_map/all_to_all | solution.py:82
  54.1 0.0 copy-done.5
  54.2 0.1 select_reduce_fusion
  54.3 0.1 fusion.14
  54.4 0.7 reshape.111.live_ref
  55.0 3.6 %reshape.131 = bf16[128,1,4112]{2,1,0:T(2,128)(2,1)} reshape(bf16[128,2,2056]{2,1,0:T(2,128)(2,1)S(1)} %all_to_all.26) | data formatting | bytes 2105344
  58.6 5.1 %copy.38 = bf16[128,1,4112]{0,2,1:T(8,128)(2,1)S(1)} copy(bf16[128,1,4112]{2,1,0:T(2,128)(2,1)} %reshape.131) | data formatting | bytes 2105344 | tf_op jit(solution)/shard_map/all_to_all | solution.py:94
  63.7 1.4 slice_convert_fusion
  65.2 3.0 %copy.39 = f32[128,4096]{1,0:T(8,128)} copy(f32[128,4096]{0,1:T(8,128)} %slice_convert_fusion) | data formatting | bytes 4194304 | tf_op jit(solution)/shard_map/convert_element_type | solution.py:20
  68.1 2.8 %reshape.109 = f32[512,1024]{1,0:T(8,128)} reshape(f32[128,4096]{1,0:T(8,128)} %copy.39) | data formatting | bytes 4194304 | tf_op jit(solution)/shard_map/convert_element_type | solution.py:20
  71.0 0.1 copy.41
  71.1 0.1 reshape.110
  71.1 1.8 reduce_sum.58
  73.0 2.1 multiply_reduce_fusion.1
  75.0 0.0 copy-done.4
  75.1 1.1 convolution_bitcast_fusion.bias_ref
  76.1 0.0 copy-done.2
  76.1 6.5 %multiply_convert_fusion.q_ref = bf16[512,2048]{1,0:T(8,128)(2,1)} fusion(bf16[1024,2048]{1,0:T(8,128)(2,1)} %param.15, f32[512,1024]{1,0:T(8,128)S(1)} %copy-done.2, f32[512]{0:T(512)S(1)} %add_rsqrt_fusion.1, f32[512]{0:T(512)S(1)} %broadcast_multiply_fusion.1), kind=kOutput, calls=%fused_computation.2 | convolution fusion | flops 2154299392 | bytes 8392704 | tf_op jit(solution)/shard_map/dot_general | solution.py:21
  82.6 72.8 %all-to-all-done.1 = bf16[1,128,1,16,2048]{4,3,2,0,1:T(8,128)(2,1)} async-done(((bf16[1,128,1,16,2048]{4,3,2,0,1:T(8,128)(2,1)}), bf16[1,128,1,16,2048]{4,3,2,0,1:T(8,128)(2,1)}, u32[]{:S(2)}, u32[]{:S(2)}) %all-to-all-start.1) | async-done | bytes 8388640 | tf_op jit(solution)/shard_map/all_to_all | solution.py:82
  155.3 22.2 %shard_map.91 = f32[512,1024]{1,0:T(8,128)} custom-call(bf16[512,2048]{1,0:T(8,128)(2,1)} %multiply_convert_fusion.q_ref, bf16[2048,2048]{1,0:T(8,128)(2,1)} %bitcast.11.k_ref.v_ref, bf16[2048,2048]{1,0:T(8,128)(2,1)} %bitcast.11.k_ref.v_ref, f32[8,2048]{1,0:T(8,128)} %convolution_bitcast_fusion.bias_ref, f32[1,2048]{1,0:T(1,128)} %reshape.111.live_ref), custom_call_target="tpu_custom_call" | custom-call | tf_op jit(solution)/shard_map/pallas_call | solution.py:54
  177.6 1.8 reduce_sum.61
  179.4 2.1 multiply_reduce_fusion
  181.5 0.0 copy-done
  181.5 0.1 copy-done.1
  181.6 2.6 %convolution_convert_fusion = bf16[512,1024]{1,0:T(8,128)(2,1)S(1)} fusion(bf16[1024,1024]{1,0:T(8,128)(2,1)S(1)} %copy-done, f32[512,1024]{1,0:T(8,128)S(1)} %copy-done.1, bf16[512,2048]{1,0:T(8,128)(2,1)} %multiply_convert_fusion.q_ref, f32[512]{0:T(512)S(1)} %add_rsqrt_fusion, f32[512]{0:T(512)S(1)} %broadcast_multiply_fusion), kind=kOutput, calls=%fused_computation.8 | convolution fusion | flops 1076887552 | bytes 6295552 | tf_op jit(solution)/shard_map/dot_general | solution.py:122
  184.1 1.2 reshape.107
  185.4 11.4 %all-to-all-start.2 = ((bf16[128,4,1024]{2,1,0:T(4,128)(2,1)}), bf16[128,4,1024]{2,1,0:T(4,128)(2,1)}, u32[]{:S(2)}, u32[]{:S(2)}) async-start(bf16[128,4,1024]{2,1,0:T(4,128)(2,1)} %reshape.107), calls=%async_computation.2 | async-start | bytes 2097152 | tf_op jit(solution)/shard_map/all_to_all | solution.py:126
  196.8 18.7 %all-to-all-done.2 = bf16[128,4,1024]{2,1,0:T(4,128)(2,1)} async-done(((bf16[128,4,1024]{2,1,0:T(4,128)(2,1)}), bf16[128,4,1024]{2,1,0:T(4,128)(2,1)}, u32[]{:S(2)}, u32[]{:S(2)}) %all-to-all-start.2) | async-done | bytes 1048608 | tf_op jit(solution)/shard_map/all_to_all | solution.py:126
  215.4 1.3 reshape.108
  216.8 2.0 gather_fusion
  218.7 2.2 add_convert_fusion
  (17 shorter events, 0.1 us)
Async XLA Ops:
  0.0 181.5 %copy-start = (bf16[1024,1024]{1,0:T(8,128)(2,1)S(1)}, bf16[1024,1024]{1,0:T(8,128)(2,1)}, u32[]{:S(2)}) copy-start(bf16[1024,1024]{1,0:T(8,128)(2,1)} %param.16) | copy-start | bytes 6291460
  5.2 3.8 %copy-start.3 = (s32[1,128,1,16]{1,3,2,0:T(8,128)S(1)}, s32[1,128,1,16]{1,3,2,0:T(8,128)}, u32[]{:S(2)}) copy-start(s32[1,128,1,16]{1,3,2,0:T(8,128)} %param.14) | copy-start | bytes 24580
  47.4 6.7 %copy-start.5 = (s32[1,128]{1,0:T(1,128)S(1)}, s32[1,128]{1,0:T(1,128)}, u32[]{:S(2)}) copy-start(s32[1,128]{1,0:T(1,128)} %param.12) | copy-start | bytes 1540
  47.4 107.9 %all-to-all-start.1 = ((bf16[1,128,1,16,2048]{4,3,2,0,1:T(8,128)(2,1)}), bf16[1,128,1,16,2048]{4,3,2,0,1:T(8,128)(2,1)}, u32[]{:S(2)}, u32[]{:S(2)}) async-start(bf16[1,128,1,16,2048]{4,3,2,0,1:T(8,128)(2,1)} %bitcast.32), calls=%async_computation.1 | async-start | bytes 16777216 | tf_op jit(solution)/shard_map/all_to_all | solution.py:82
  71.1 3.9 %copy-start.4 = (f32[8,128]{1,0:T(8,128)S(1)}, f32[8,128]{1,0:T(8,128)}, u32[]{:S(2)}) copy-start(f32[8,128]{1,0:T(8,128)} %param.17) | copy-start | bytes 12292
  72.9 3.2 %copy-start.2 = (f32[512,1024]{1,0:T(8,128)S(1)}, f32[512,1024]{1,0:T(8,128)}, u32[]{:S(2)}) copy-start(f32[512,1024]{1,0:T(8,128)} %reshape.109) | copy-start | bytes 6291460
  179.4 2.2 %copy-start.1 = (f32[512,1024]{1,0:T(8,128)S(1)}, f32[512,1024]{1,0:T(8,128)}, u32[]{:S(2)}) copy-start(f32[512,1024]{1,0:T(8,128)} %shard_map.91) | copy-start | bytes 6291460
  185.4 30.0 %all-to-all-start.2 = ((bf16[128,4,1024]{2,1,0:T(4,128)(2,1)}), bf16[128,4,1024]{2,1,0:T(4,128)(2,1)}, u32[]{:S(2)}, u32[]{:S(2)}) async-start(bf16[128,4,1024]{2,1,0:T(4,128)(2,1)} %reshape.107), calls=%async_computation.2 | async-start | bytes 2097152 | tf_op jit(solution)/shard_map/all_to_all | solution.py:126

commit v2 on v1

v2 whole, which is shorter than its diff:
```python
import functools
import math

import jax
import jax.numpy as jnp
from jax import lax
from jax.experimental import pallas as pl
from jax.experimental.pallas import tpu as pltpu
from jax.sharding import PartitionSpec as P


def layer_norm(values):
    average = jnp.mean(values, axis=-1, keepdims=True)
    centred = values - average
    spread = jnp.mean(centred * centred, axis=-1, keepdims=True)
    return centred * lax.rsqrt(spread + 1e-05)


def prepare(inputs, w_proj):
    normed = layer_norm(inputs.astype(jnp.float32)).astype(jnp.bfloat16)
    return jax.nn.silu(jnp.dot(normed, w_proj, preferred_element_type=jnp.float32)).astype(
        jnp.bfloat16
    )


def attend_kernel(q_ref, k_ref, v_ref, bias_ref, live_ref, o_ref, *, half_scale, chunk):
    head = pl.program_id(0)
    query = q_ref[...]
    bias_row = bias_ref[pl.ds(head, 1), :]
    event_count = k_ref.shape[0]
    acc = jnp.zeros(o_ref.shape, jnp.float32)
    for c in range(event_count // chunk):
        lo = c * chunk
        key = k_ref[pl.ds(lo, chunk), :]
        value = v_ref[pl.ds(lo, chunk), :]
        value = jnp.where(live_ref[pl.ds(lo, chunk), :] > 0.0, value, jnp.zeros_like(value))
        scores = lax.dot_general(
            query, key, (((1,), (1,)), ((), ())), preferred_element_type=jnp.float32
        )
        half = scores * half_scale + bias_row[:, lo : lo + chunk]
        weight = (half + half * jnp.tanh(half)).astype(jnp.bfloat16)
        acc = acc + jnp.dot(weight, value, preferred_element_type=jnp.float32)
    o_ref[...] = acc


def attend(projected, events, half_bias, live, head_count, head_dim, half_scale):
    slot_count = projected.shape[0]
    event_count = events.shape[0]
    features = head_count * head_dim
    chunk = 512 if event_count % 512 == 0 else event_count
    kernel = functools.partial(attend_kernel, half_scale=half_scale, chunk=chunk)
    return pl.pallas_call(
        kernel,
        grid=(head_count,),
        in_specs=[
            pl.BlockSpec((slot_count, head_dim), lambda h: (0, head_count + h)),
            pl.BlockSpec((event_count, head_dim), lambda h: (0, h)),
            pl.BlockSpec((event_count, head_dim), lambda h: (0, head_count + h)),
            pl.BlockSpec(half_bias.shape, lambda h: (0, 0)),
            pl.BlockSpec(live.shape, lambda h: (0, 0)),
        ],
        out_specs=pl.BlockSpec((slot_count, head_dim), lambda h: (0, h)),
        out_shape=jax.ShapeDtypeStruct((slot_count, features), jnp.float32),
    )(projected, events, events, half_bias, live)


def shards(
    cand_x, cand_req, hist_len, block_place, kv_store, store_bucket, w_proj, w_out, time_bias
):
    axes = ("req", "cache")
    devices = lax.axis_size(axes)
    row_count = cand_x.shape[0]
    features = cand_x.shape[1]
    head_count = time_bias.shape[0]
    head_dim = features // head_count
    bucket_count = time_bias.shape[1]
    per_owner = kv_store.shape[2]
    block_ev = kv_store.shape[3]
    capacity = max(2, 2 * row_count // devices)
    event_count = devices * per_owner * block_ev
    kv_send = kv_store.reshape(devices, per_owner * block_ev, 2 * features)

    target = cand_req[:, 0]
    onehot = (target[:, None] == jnp.arange(devices, dtype=jnp.int32)[None, :]).astype(jnp.int32)
    earlier = jnp.cumsum(onehot, axis=0) - onehot
    slot_rank = jnp.sum(earlier * onehot, axis=1)
    flat_slot = target * capacity + slot_rank
    empty = jnp.zeros((devices * capacity, features), cand_x.dtype)
    rows_per = per_owner * block_ev
    slotted = empty.at[flat_slot].set(cand_x).reshape(devices, rows_per, capacity * features // rows_per)
    bucket_send = store_bucket.reshape(devices, rows_per, 1).astype(cand_x.dtype)
    received = lax.all_to_all(
        jnp.concatenate([kv_send, slotted, bucket_send], axis=2),
        axes,
        split_axis=0,
        concat_axis=0,
        tiled=True,
    )
    senders = received.shape[0]
    width = received.shape[2]
    events = received.reshape(event_count, width)
    flat_rows = received[:, :, 2 * features : width - 1].reshape(senders * capacity, features)
    buckets = received[:, :, width - 1].astype(jnp.int32).reshape(event_count)

    places = block_place[0]
    block_count = places.shape[0]
    block_ids = jnp.arange(block_count, dtype=jnp.int32)
    match = (places[:, None] == block_ids[None, :]).astype(jnp.int32)
    block_of_place = jnp.sum(match * block_ids[:, None], axis=0)
    position = (
        block_of_place[:, None] * block_ev + jnp.arange(block_ev, dtype=jnp.int32)[None, :]
    ).reshape(event_count, 1)
    live = (position < hist_len[0]).astype(jnp.float32)
    bucket_table = (buckets[None, :] == jnp.arange(bucket_count, dtype=jnp.int32)[:, None]).astype(
        jnp.float32
    )
    half_bias = 0.5 * jnp.dot(time_bias, bucket_table, precision=lax.Precision.HIGHEST)
    half_scale = 0.5 / math.sqrt(head_dim)

    projected = prepare(flat_rows, w_proj)
    slot_count = projected.shape[0]
    gate_u = projected[:, :features]
    attended = attend(projected, events, half_bias, live, head_count, head_dim, half_scale)
    hidden = (layer_norm(attended) * gate_u.astype(jnp.float32)).astype(jnp.bfloat16)
    update = (
        jnp.dot(hidden, w_out, preferred_element_type=jnp.float32)
        .astype(jnp.bfloat16)
        .reshape(senders, capacity, features)
    )
    returned = lax.all_to_all(update, axes, split_axis=0, concat_axis=0, tiled=True)
    update = returned.reshape(devices * capacity, features)[flat_slot]
    return (cand_x.astype(jnp.float32) + update.astype(jnp.float32)).astype(jnp.bfloat16)


def solution(mesh):
    placed = (
        P(("req", "cache"), None),
        P(("req", "cache"), None),
        P(("req", "cache")),
        P(("req", "cache"), None),
        P(("req", "cache"), None, None, None, None),
        P(("req", "cache"), None, None, None),
        P(),
        P(),
        P(),
    )
    return jax.shard_map(
        shards, mesh=mesh, in_specs=placed, out_specs=P(("req", "cache"), None), check_vma=False
    )
```

time: 222 us -> 233 us (1.050)
  waiting for transfers between devices: 91.4 us -> 137 us
  blocking collectives: 31.2 us -> 0 us
  local copies, waits for them, and re-layouts: 30.9 us -> 16.8 us
  other arithmetic: 16.7 us -> 27.1 us
  starting transfers between devices: 17.4 us -> 24 us
  Pallas kernels: 22.2 us -> 16 us
    all_to_all x1, waiting for transfers between devices: 72.8 us -> 119 us  [shards(): lax.all_to_all(jnp.concatenate([kv_send, slotted, bucket_send], axis=2),...]
    all_to_all x1 -> x0, blocking collectives: 31.2 us -> none  [shards(): lax.all_to_all(jnp.concatenate([slotted, bucket_send], axis=1), axes, spl...]
    concatenate x0 -> x1, other arithmetic: none -> 9.15 us  [shards(): jnp.concatenate([kv_send, slotted, bucket_send], axis=2)]
    unnamed x16 -> x11, local copies, waits for them, and re-layouts: 7.01 us -> 0.13 us
    pallas_call x1, Pallas kernels: 22.2 us -> 16 us  [attend(): pl.pallas_call(kernel, grid=(head_count,), in_specs=[pl.BlockSpec((slot_c...]
    all_to_all x1, starting transfers between devices: 6.08 us -> 11.9 us  [shards(): lax.all_to_all(jnp.concatenate([kv_send, slotted, bucket_send], axis=2),...]
    all_to_all x2 -> x0, local copies, waits for them, and re-layouts: 5.59 us -> none  [shards(): lax.all_to_all(jnp.concatenate([slotted, bucket_send], axis=1), axes, spl...]
    all_to_all x2 -> x0, other arithmetic: 3.39 us -> none  [shards(): lax.all_to_all(jnp.concatenate([slotted, bucket_send], axis=1), axes, spl...]
  transfers between devices with their start and end apart: 2 -> 2, of which waited for: 2 -> 2; matrix products, arithmetic and copies ran while one was open for 13% -> 1% of each run, Pallas kernels for 0% -> 0%
where the time goes in v2:
time: 233 us
  waiting for transfers between devices  137 us (59%)
  other arithmetic  27.1 us (12%)
  starting transfers between devices  24 us (10%)
  local copies, waits for them, and re-layouts  16.8 us (7%)
  Pallas kernels  16 us (7%)
  matrix products  10.6 us (5%)
    all_to_all x1, waiting for transfers between devices, shards(): lax.all_to_all(jnp.concatenate([kv_send, slotted, bucket_send], axis=2),...  119 us
    all_to_all x1, waiting for transfers between devices, shards(): lax.all_to_all(update, axes, split_axis=0, concat_axis=0, tiled=True)  18.7 us
    pallas_call x1, Pallas kernels, attend(): pl.pallas_call(kernel, grid=(head_count,), in_specs=[pl.BlockSpec((slot_c...  16 us
    all_to_all x1, starting transfers between devices, shards(): lax.all_to_all(update, axes, split_axis=0, concat_axis=0, tiled=True)  12.1 us
    all_to_all x1, starting transfers between devices, shards(): lax.all_to_all(jnp.concatenate([kv_send, slotted, bucket_send], axis=2),...  11.9 us
    concatenate x1, other arithmetic, shards(): jnp.concatenate([kv_send, slotted, bucket_send], axis=2)  9.15 us
    dot_general x1, matrix products, prepare(): jnp.dot(normed, w_proj, preferred_element_type=jnp.float32)  7 us
  transfers between devices with their start and end apart: 2, of which 2 were waited for; matrix products, arithmetic and copies ran while one was open for 1% of the time, Pallas kernels for 0%

profile of v2, /device:TPU:1, one launch (start us, length us, event | category | flops | bytes accessed | tf_op | source)
XLA Modules:
  0.0 232.7 jit_solution(11579458595655810026)
XLA Ops:
  0.0 0.0 copy-start
  0.0 0.0 copy-start.2
  0.0 0.9 copy.18
  1.0 0.2 fusion.11
  1.3 0.9 fusion.13
  2.1 0.7 compare_select_fusion
  2.8 3.2 %scatter_custom_fusion = bf16[512,1024]{1,0:T(8,128)(2,1)} fusion(s32[256]{0:T(256)S(1)} %bitcast.38, bf16[256,1024]{1,0:T(8,128)(2,1)} %param.9, bf16[]{:T(256)} %constant.10.clone.1), kind=kCustom, calls=%fused_computation.23 | custom fusion | bytes 1049088 | tf_op jit(solution)/shard_map/scatter | solution.py:90
  6.0 1.7 reshape.129
  7.7 0.0 copy-done.2
  7.7 1.2 copy.20
  8.9 9.2 %pad_maximum_fusion = bf16[128,16,2305]{2,1,0:T(8,128)(2,1)} fusion(bf16[128,16,1]{2,1,0:T(8,128)(2,1)} %copy.20, bf16[128,16,256]{2,1,0:T(8,128)(2,1)S(1)} %reshape.129, bf16[128,16,2048]{2,1,0:T(8,128)(2,1)} %bitcast.30), kind=kLoop, calls=%fused_computation.2 | loop fusion | flops 28323840 | bytes 18882560 | tf_op jit(solution)/shard_map/concatenate | solution.py:93
  18.1 0.0 copy-start.4
  18.1 11.9 %all-to-all-start = ((bf16[128,16,2305]{2,1,0:T(8,128)(2,1)}), bf16[128,16,2305]{2,1,0:T(8,128)(2,1)}, u32[]{:S(2)}, u32[]{:S(2)}) async-start(bf16[128,16,2305]{2,1,0:T(8,128)(2,1)} %pad_maximum_fusion), calls=%async_computation | async-start | bytes 19922944 | tf_op jit(solution)/shard_map/all_to_all | solution.py:92
  30.6 0.0 copy-done.4
  30.6 0.1 select_reduce_fusion
  30.8 0.1 fusion.16
  30.8 1.6 reshape.152.live_ref
  32.4 118.7 %all-to-all-done = bf16[128,16,2305]{2,1,0:T(8,128)(2,1)} async-done(((bf16[128,16,2305]{2,1,0:T(8,128)(2,1)}), bf16[128,16,2305]{2,1,0:T(8,128)(2,1)}, u32[]{:S(2)}, u32[]{:S(2)}) %all-to-all-start) | async-done | bytes 9441312 | tf_op jit(solution)/shard_map/all_to_all | solution.py:92
  151.1 1.6 fusion.7
  152.7 0.1 reduce_sum.73
  152.8 0.1 reduce_sum.74
  153.0 0.1 div.19
  153.1 0.1 copy.21
  153.2 0.1 copy.22
  153.3 1.9 multiply_reduce_fusion.1
  155.2 0.1 reduce_sum.76
  155.3 0.1 reduce_sum.77
  155.4 2.8 %slice_convert_fusion = f32[128,16,256]{2,1,0:T(8,128)} fusion(bf16[128,16,2305]{2,1,0:T(8,128)(2,1)} %all-to-all-done), kind=kLoop, calls=%fused_computation.13 | loop fusion | flops 524288 | bytes 3145728 | tf_op jit(solution)/shard_map/convert_element_type | solution.py:20
  158.3 0.0 copy-start.3
  158.3 2.9 %reshape.133 = f32[512,1024]{1,0:T(8,128)} reshape(f32[128,16,256]{2,1,0:T(8,128)} %slice_convert_fusion) | data formatting | bytes 4194304 | tf_op jit(solution)/shard_map/convert_element_type | solution.py:20
  161.2 3.3 %convert_reduce_fusion = s32[128,16]{1,0:T(8,128)S(1)} fusion(bf16[128,16,2305]{2,1,0:T(8,128)(2,1)} %all-to-all-done), kind=kLoop, calls=%fused_computation.14 | loop fusion | flops 2048 | bytes 12288 | tf_op jit(solution)/shard_map/convert_element_type | solution.py:103
  164.5 0.1 reshape.134
  164.6 0.0 copy-done.3
  164.6 1.1 fusion.bias_ref
  165.6 7.0 %multiply_convert_fusion.q_ref = bf16[512,2048]{1,0:T(8,128)(2,1)} fusion(bf16[1024,2048]{1,0:T(8,128)(2,1)} %param.15, f32[512,1024]{1,0:T(8,128)} %reshape.133, f32[512]{0:T(512)S(1)} %add_rsqrt_fusion.1, f32[512]{0:T(512)S(1)} %broadcast_multiply_fusion.1), kind=kOutput, calls=%fused_computation.3 | convolution fusion | flops 2154299392 | bytes 8392704 | tf_op jit(solution)/shard_map/dot_general | solution.py:21
  172.6 16.0 %shard_map.91 = f32[512,1024]{1,0:T(8,128)} custom-call(bf16[512,2048]{1,0:T(8,128)(2,1)} %multiply_convert_fusion.q_ref, bf16[2048,2305]{1,0:T(8,128)(2,1)} %bitcast.10.k_ref.v_ref, bf16[2048,2305]{1,0:T(8,128)(2,1)} %bitcast.10.k_ref.v_ref, f32[8,2048]{1,0:T(8,128)} %fusion.bias_ref, f32[2048,1]{1,0:T(8,128)} %reshape.152.live_ref), custom_call_target="tpu_custom_call" | custom-call | tf_op jit(solution)/shard_map/pallas_call | solution.py:52
  188.6 1.8 reduce_sum.79
  190.4 0.0 copy-start.1
  190.4 2.1 multiply_reduce_fusion
  192.5 0.0 copy-done
  192.5 0.1 copy-done.1
  192.6 2.6 %convolution_convert_fusion = bf16[512,1024]{1,0:T(8,128)(2,1)S(1)} fusion(bf16[1024,1024]{1,0:T(8,128)(2,1)S(1)} %copy-done, f32[512,1024]{1,0:T(8,128)S(1)} %copy-done.1, bf16[512,2048]{1,0:T(8,128)(2,1)} %multiply_convert_fusion.q_ref, f32[512]{0:T(512)S(1)} %add_rsqrt_fusion, f32[512]{0:T(512)S(1)} %broadcast_multiply_fusion), kind=kOutput, calls=%fused_computation.10 | convolution fusion | flops 1076887552 | bytes 6295552 | tf_op jit(solution)/shard_map/dot_general | solution.py:126
  195.2 1.2 reshape.131
  196.4 12.1 %all-to-all-start.1 = ((bf16[128,4,1024]{2,1,0:T(4,128)(2,1)}), bf16[128,4,1024]{2,1,0:T(4,128)(2,1)}, u32[]{:S(2)}, u32[]{:S(2)}) async-start(bf16[128,4,1024]{2,1,0:T(4,128)(2,1)} %reshape.131), calls=%async_computation.1 | async-start | bytes 2097152 | tf_op jit(solution)/shard_map/all_to_all | solution.py:130
  208.6 18.7 %all-to-all-done.1 = bf16[128,4,1024]{2,1,0:T(4,128)(2,1)} async-done(((bf16[128,4,1024]{2,1,0:T(4,128)(2,1)}), bf16[128,4,1024]{2,1,0:T(4,128)(2,1)}, u32[]{:S(2)}, u32[]{:S(2)}) %all-to-all-start.1) | async-done | bytes 1048608 | tf_op jit(solution)/shard_map/all_to_all | solution.py:130
  227.2 1.3 reshape.132
  228.6 2.0 gather_fusion
  230.5 2.2 add_convert_fusion
  (14 shorter events, 0.1 us)
Async XLA Ops:
  0.0 192.5 %copy-start = (bf16[1024,1024]{1,0:T(8,128)(2,1)S(1)}, bf16[1024,1024]{1,0:T(8,128)(2,1)}, u32[]{:S(2)}) copy-start(bf16[1024,1024]{1,0:T(8,128)(2,1)} %param.16) | copy-start | bytes 6291460
  0.0 7.7 %copy-start.2 = (s32[1,128,1,16]{1,3,2,0:T(8,128)S(1)}, s32[1,128,1,16]{1,3,2,0:T(8,128)}, u32[]{:S(2)}) copy-start(s32[1,128,1,16]{1,3,2,0:T(8,128)} %param.14) | copy-start | bytes 24580
  18.1 12.6 %copy-start.4 = (s32[1,128]{1,0:T(1,128)S(1)}, s32[1,128]{1,0:T(1,128)}, u32[]{:S(2)}) copy-start(s32[1,128]{1,0:T(1,128)} %param.12) | copy-start | bytes 1540
  18.1 133.1 %all-to-all-start = ((bf16[128,16,2305]{2,1,0:T(8,128)(2,1)}), bf16[128,16,2305]{2,1,0:T(8,128)(2,1)}, u32[]{:S(2)}, u32[]{:S(2)}) async-start(bf16[128,16,2305]{2,1,0:T(8,128)(2,1)} %pad_maximum_fusion), calls=%async_computation | async-start | bytes 19922944 | tf_op jit(solution)/shard_map/all_to_all | solution.py:92
  158.3 6.3 %copy-start.3 = (f32[8,128]{1,0:T(8,128)S(1)}, f32[8,128]{1,0:T(8,128)}, u32[]{:S(2)}) copy-start(f32[8,128]{1,0:T(8,128)} %param.17) | copy-start | bytes 12292
  190.4 2.2 copy-start.1
  196.4 30.8 %all-to-all-start.1 = ((bf16[128,4,1024]{2,1,0:T(4,128)(2,1)}), bf16[128,4,1024]{2,1,0:T(4,128)(2,1)}, u32[]{:S(2)}, u32[]{:S(2)}) async-start(bf16[128,4,1024]{2,1,0:T(4,128)(2,1)} %reshape.131), calls=%async_computation.1 | async-start | bytes 2097152 | tf_op jit(solution)/shard_map/all_to_all | solution.py:130

commit v3 on v2

--- a/solution.py
+++ b/solution.py
@@ -78,7 +78,11 @@
     block_ev = kv_store.shape[3]
     capacity = max(2, 2 * row_count // devices)
     event_count = devices * per_owner * block_ev
-    kv_send = kv_store.reshape(devices, per_owner * block_ev, 2 * features)
+    arrived = lax.all_to_all(kv_store, axes, split_axis=1, concat_axis=0, tiled=True)
+    events = arrived.reshape(event_count, 2 * features)
+    every_bucket = lax.all_gather(store_bucket, axes, axis=0, tiled=True)
+    me = lax.axis_index(axes)
+    buckets = lax.dynamic_index_in_dim(every_bucket, me, axis=1, keepdims=False).reshape(event_count)
 
     target = cand_req[:, 0]
     onehot = (target[:, None] == jnp.arange(devices, dtype=jnp.int32)[None, :]).astype(jnp.int32)
@@ -86,21 +90,15 @@
     slot_rank = jnp.sum(earlier * onehot, axis=1)
     flat_slot = target * capacity + slot_rank
     empty = jnp.zeros((devices * capacity, features), cand_x.dtype)
-    rows_per = per_owner * block_ev
-    slotted = empty.at[flat_slot].set(cand_x).reshape(devices, rows_per, capacity * features // rows_per)
-    bucket_send = store_bucket.reshape(devices, rows_per, 1).astype(cand_x.dtype)
     received = lax.all_to_all(
-        jnp.concatenate([kv_send, slotted, bucket_send], axis=2),
+        empty.at[flat_slot].set(cand_x).reshape(devices, capacity, features),
         axes,
         split_axis=0,
         concat_axis=0,
         tiled=True,
     )
     senders = received.shape[0]
-    width = received.shape[2]
-    events = received.reshape(event_count, width)
-    flat_rows = received[:, :, 2 * features : width - 1].reshape(senders * capacity, features)
-    buckets = received[:, :, width - 1].astype(jnp.int32).reshape(event_count)
+    flat_rows = received.reshape(senders * capacity, features)
 
     places = block_place[0]
     block_count = places.shape[0]

time: 233 us -> 252 us (1.082)
  blocking collectives: 0 us -> 30.5 us
  other arithmetic: 27.1 us -> 9.39 us
  between operations: 0.85 us -> 14.2 us
  starting transfers between devices: 24 us -> 12.1 us
  waiting for transfers between devices: 137 us -> 143 us
    all_gather x0 -> x1, waiting for transfers between devices: none -> 123 us  [shards(): every_bucket = lax.all_gather(store_bucket, axes, axis=0, tiled=True)]
    all_to_all x1, waiting for transfers between devices: 119 us -> 0.01 us  [shards(): lax.all_to_all(kv_store, axes, split_axis=1, concat_axis=0, tiled=True)]
    all_to_all x0 -> x1, blocking collectives: none -> 30.5 us  [shards(): lax.all_to_all(empty.at[flat_slot].set(cand_x).reshape(devices, capacity,...]
    concatenate x1 -> x0, other arithmetic: 9.15 us -> none  [shards(): jnp.concatenate([kv_send, slotted, bucket_send], axis=2)]
    all_to_all x1, starting transfers between devices: 12.1 us -> 5.8 us  [shards(): lax.all_to_all(update, axes, split_axis=0, concat_axis=0, tiled=True)]
    convert_element_type x3 -> x0, other arithmetic: 6.12 us -> none  [the longest x1 3.28 us: shards(): buckets = received[:, :, width - 1].astype(jnp.int32).reshape(event_count)]
    all_to_all x1, starting transfers between devices: 11.9 us -> 6.09 us  [shards(): lax.all_to_all(kv_store, axes, split_axis=1, concat_axis=0, tiled=True)]
    dynamic_slice x0 -> x1, local copies, waits for them, and re-layouts: none -> 3.75 us  [shards(): lax.dynamic_index_in_dim(every_bucket, me, axis=1, keepdims=False)]
  transfers between devices with their start and end apart: 2 -> 3, of which waited for: 2 -> 2; matrix products, arithmetic and copies ran while one was open for 1% -> 7% of each run, Pallas kernels for 0% -> 0%
where the time goes in v3:
time: 252 us
  waiting for transfers between devices  143 us (57%)
  blocking collectives  30.5 us (12%)
  local copies, waits for them, and re-layouts  16.3 us (6%)
  Pallas kernels  16 us (6%)
  between operations  14.2 us (6%)
  starting transfers between devices  12.1 us (5%)
  matrix products  10.8 us (4%)
  other arithmetic  9.39 us (4%)
    all_gather x1, waiting for transfers between devices, shards(): every_bucket = lax.all_gather(store_bucket, axes, axis=0, tiled=True)  123 us
    all_to_all x1, blocking collectives, shards(): lax.all_to_all(empty.at[flat_slot].set(cand_x).reshape(devices, capacity,...  30.5 us
    all_to_all x1, waiting for transfers between devices, shards(): lax.all_to_all(update, axes, split_axis=0, concat_axis=0, tiled=True)  18.7 us
    pallas_call x1, Pallas kernels, attend(): pl.pallas_call(kernel, grid=(head_count,), in_specs=[pl.BlockSpec((slot_c...  16 us
    dot_general x1, matrix products, prepare(): jnp.dot(normed, w_proj, preferred_element_type=jnp.float32)  7.09 us
    all_to_all x1, starting transfers between devices, shards(): lax.all_to_all(kv_store, axes, split_axis=1, concat_axis=0, tiled=True)  6.09 us
    all_to_all x1, starting transfers between devices, shards(): lax.all_to_all(update, axes, split_axis=0, concat_axis=0, tiled=True)  5.8 us
  transfers between devices with their start and end apart: 3, of which 2 were waited for; matrix products, arithmetic and copies ran while one was open for 7% of the time, Pallas kernels for 0%

profile of v3, /device:TPU:1, one launch (start us, length us, event | category | flops | bytes accessed | tf_op | source)
XLA Modules:
  0.0 251.8 jit_solution(14563578382978201069)
XLA Ops:
  6.5 0.0 copy-start
  6.5 0.9 copy.18
  7.5 0.2 fusion.10
  7.8 0.9 fusion.12
  8.6 0.7 compare_select_fusion
  9.3 2.4 scatter_custom_fusion
  11.7 1.2 reshape.122
  13.0 30.5 %all_to_all.19 = bf16[128,4,1024]{2,1,0:T(4,128)(2,1)S(1)} all-to-all(bf16[128,4,1024]{2,1,0:T(4,128)(2,1)} %reshape.122), channel_id=1, replica_groups=mesh['req'=16,'cache'=8] {'req','cache'}, dimensions={0} | all-to-all | bytes 2097152 | tf_op jit(solution)/shard_map/all_to_all | solution.py:93
  43.5 0.0 copy-start.3
  43.5 6.1 %all-to-all-start.1 = ((bf16[1,128,1,16,2048]{4,3,2,0,1:T(8,128)(2,1)}), bf16[1,128,1,16,2048]{4,3,2,0,1:T(8,128)(2,1)}, u32[]{:S(2)}, u32[]{:S(2)}) async-start(bf16[1,128,1,16,2048]{4,3,2,0,1:T(8,128)(2,1)} %bitcast.27), calls=%async_computation.1 | async-start | bytes 16777216 | tf_op jit(solution)/shard_map/all_to_all | solution.py:81
  49.6 0.2 all-gather.2.cloned.1.call-start
  49.8 0.5 all-gather.2.cloned.1.call-update
  51.0 0.0 copy-done.3
  51.0 0.1 select_reduce_fusion
  51.1 0.1 fusion.15
  51.2 1.6 reshape.144.live_ref
  52.8 0.5 convert_reduce_fusion
  53.3 0.1 div.19
  53.4 0.8 multiply_reduce_fusion.1
  54.3 0.1 rsqrt.20
  54.4 1.4 reshape.126
  55.8 0.0 copy-start.2
  55.8 7.1 %multiply_convert_fusion.q_ref = bf16[512,2048]{1,0:T(8,128)(2,1)} fusion(bf16[1024,2048]{1,0:T(8,128)(2,1)} %param.15, f32[512,1024]{1,0:T(8,128)} %reshape.126, f32[512]{0:T(512)S(1)} %rsqrt.20, f32[512]{0:T(512)S(1)} %div.19), kind=kOutput, calls=%fused_computation.2 | convolution fusion | flops 2154299392 | bytes 8392704 | tf_op jit(solution)/shard_map/dot_general | solution.py:21
  62.9 123.4 %all-gather.2.cloned.1.call-done = s32[128,128,1,16]{1,3,2,0:T(8,128)} async-done(((s32[1,128,1,16]{1,3,2,0:T(8,128)}), s32[128,128,1,16]{1,3,2,0:T(8,128)}) %all-gather.2.cloned.1.call-update) | async-done | bytes 1048592 | tf_op jit(solution)/shard_map/all_gather | solution.py:83
  186.2 3.8 %dynamic-slice_reduce_fusion = s32[128,16]{1,0:T(8,128)S(1)} fusion(s32[128,128,1,16]{1,3,2,0:T(8,128)} %all-gather.2.cloned.1.call-done, s32[]{:T(128)S(6)} %select_n.10), kind=kLoop, calls=%fused_computation.17 | loop fusion | bytes 16388 | tf_op jit(solution)/shard_map/jit(dynamic_index_in_dim)/dynamic_slice | solution.py:85
  190.0 0.1 eq.63
  190.1 0.0 copy-done.2
  190.1 1.1 fusion.bias_ref
  191.1 0.0 all-to-all-done.1
  191.1 16.0 %shard_map.91 = f32[512,1024]{1,0:T(8,128)} custom-call(bf16[512,2048]{1,0:T(8,128)(2,1)} %multiply_convert_fusion.q_ref, bf16[2048,2048]{1,0:T(8,128)(2,1)} %bitcast.8.k_ref.v_ref, bf16[2048,2048]{1,0:T(8,128)(2,1)} %bitcast.8.k_ref.v_ref, f32[8,2048]{1,0:T(8,128)} %fusion.bias_ref, f32[2048,1]{1,0:T(8,128)} %reshape.144.live_ref), custom_call_target="tpu_custom_call" | custom-call | tf_op jit(solution)/shard_map/pallas_call | solution.py:52
  207.1 1.8 reduce_sum.61
  208.9 0.0 copy-start.1
  208.9 2.1 multiply_reduce_fusion
  211.0 0.0 copy-done
  211.0 0.1 copy-done.1
  211.1 2.6 %convolution_convert_fusion = bf16[512,1024]{1,0:T(8,128)(2,1)S(1)} fusion(bf16[1024,1024]{1,0:T(8,128)(2,1)S(1)} %copy-done, f32[512,1024]{1,0:T(8,128)S(1)} %copy-done.1, bf16[512,2048]{1,0:T(8,128)(2,1)} %multiply_convert_fusion.q_ref, f32[512]{0:T(512)S(1)} %add_rsqrt_fusion.1, f32[512]{0:T(512)S(1)} %broadcast_multiply_fusion.1), kind=kOutput, calls=%fused_computation.9 | convolution fusion | flops 1076887552 | bytes 6295552 | tf_op jit(solution)/shard_map/dot_general | solution.py:124
  213.7 1.2 reshape.124
  215.0 5.8 %all-to-all-start.2 = ((bf16[128,4,1024]{2,1,0:T(4,128)(2,1)}), bf16[128,4,1024]{2,1,0:T(4,128)(2,1)}, u32[]{:S(2)}, u32[]{:S(2)}) async-start(bf16[128,4,1024]{2,1,0:T(4,128)(2,1)} %reshape.124), calls=%async_computation.2 | async-start | bytes 2097152 | tf_op jit(solution)/shard_map/all_to_all | solution.py:128
  220.8 18.7 %all-to-all-done.2 = bf16[128,4,1024]{2,1,0:T(4,128)(2,1)} async-done(((bf16[128,4,1024]{2,1,0:T(4,128)(2,1)}), bf16[128,4,1024]{2,1,0:T(4,128)(2,1)}, u32[]{:S(2)}, u32[]{:S(2)}) %all-to-all-start.2) | async-done | bytes 1048608 | tf_op jit(solution)/shard_map/all_to_all | solution.py:128
  239.4 1.3 reshape.125
  240.8 2.0 gather_fusion
  242.7 2.2 add_convert_fusion
  (12 shorter events, 0.1 us)
Async XLA Ops:
  6.5 204.5 %copy-start = (bf16[1024,1024]{1,0:T(8,128)(2,1)S(1)}, bf16[1024,1024]{1,0:T(8,128)(2,1)}, u32[]{:S(2)}) copy-start(bf16[1024,1024]{1,0:T(8,128)(2,1)} %param.16) | copy-start | bytes 6291460
  43.5 7.5 %copy-start.3 = (s32[1,128]{1,0:T(1,128)S(1)}, s32[1,128]{1,0:T(1,128)}, u32[]{:S(2)}) copy-start(s32[1,128]{1,0:T(1,128)} %param.12) | copy-start | bytes 1540
  43.5 147.6 %all-to-all-start.1 = ((bf16[1,128,1,16,2048]{4,3,2,0,1:T(8,128)(2,1)}), bf16[1,128,1,16,2048]{4,3,2,0,1:T(8,128)(2,1)}, u32[]{:S(2)}, u32[]{:S(2)}) async-start(bf16[1,128,1,16,2048]{4,3,2,0,1:T(8,128)(2,1)} %bitcast.27), calls=%async_computation.1 | async-start | bytes 16777216 | tf_op jit(solution)/shard_map/all_to_all | solution.py:81
  49.6 136.6 %all-gather.2.cloned.1.call-start = ((), (), s32[]{:S(2)}) async-start(), calls=%async_computation.3 | async-start | bytes 1056768 | tf_op jit(solution)/shard_map/all_gather | solution.py:83
  55.8 134.3 %copy-start.2 = (f32[8,128]{1,0:T(8,128)S(1)}, f32[8,128]{1,0:T(8,128)}, u32[]{:S(2)}) copy-start(f32[8,128]{1,0:T(8,128)} %param.17) | copy-start | bytes 12292
  208.9 2.2 copy-start.1
  215.0 24.5 %all-to-all-start.2 = ((bf16[128,4,1024]{2,1,0:T(4,128)(2,1)}), bf16[128,4,1024]{2,1,0:T(4,128)(2,1)}, u32[]{:S(2)}, u32[]{:S(2)}) async-start(bf16[128,4,1024]{2,1,0:T(4,128)(2,1)} %reshape.124), calls=%async_computation.2 | async-start | bytes 2097152 | tf_op jit(solution)/shard_map/all_to_all | solution.py:128
Sparse Core Ops, SparseCore 0:
  53.2 132.9 all-gather.1

commit v4 on v3

--- a/solution.py
+++ b/solution.py
@@ -64,6 +64,16 @@
     )(projected, events, events, half_bias, live)
 
 
+def exchange(values):
+    outer = lax.axis_size("req")
+    inner = lax.axis_size("cache")
+    rest = values.shape[1:]
+    values = values.reshape((outer, inner) + rest)
+    values = lax.all_to_all(values, "cache", split_axis=1, concat_axis=1, tiled=True)
+    values = lax.all_to_all(values, "req", split_axis=0, concat_axis=0, tiled=True)
+    return values.reshape((outer * inner,) + rest)
+
+
 def shards(
     cand_x, cand_req, hist_len, block_place, kv_store, store_bucket, w_proj, w_out, time_bias
 ):
@@ -80,9 +90,6 @@
     event_count = devices * per_owner * block_ev
     arrived = lax.all_to_all(kv_store, axes, split_axis=1, concat_axis=0, tiled=True)
     events = arrived.reshape(event_count, 2 * features)
-    every_bucket = lax.all_gather(store_bucket, axes, axis=0, tiled=True)
-    me = lax.axis_index(axes)
-    buckets = lax.dynamic_index_in_dim(every_bucket, me, axis=1, keepdims=False).reshape(event_count)
 
     target = cand_req[:, 0]
     onehot = (target[:, None] == jnp.arange(devices, dtype=jnp.int32)[None, :]).astype(jnp.int32)
@@ -90,15 +97,15 @@
     slot_rank = jnp.sum(earlier * onehot, axis=1)
     flat_slot = target * capacity + slot_rank
     empty = jnp.zeros((devices * capacity, features), cand_x.dtype)
-    received = lax.all_to_all(
-        empty.at[flat_slot].set(cand_x).reshape(devices, capacity, features),
-        axes,
-        split_axis=0,
-        concat_axis=0,
-        tiled=True,
-    )
+    slotted = empty.at[flat_slot].set(cand_x).reshape(devices, capacity, features)
+    rows_per = per_owner * block_ev
+    bucket_lanes = rows_per // capacity
+    bucket_send = store_bucket.reshape(devices, capacity, bucket_lanes).astype(cand_x.dtype)
+    bucket_send = jnp.pad(bucket_send, ((0, 0), (0, 0), (0, 128 - bucket_lanes)))
+    received = exchange(jnp.concatenate([slotted, bucket_send], axis=2))
     senders = received.shape[0]
-    flat_rows = received.reshape(senders * capacity, features)
+    flat_rows = received[:, :, :features].reshape(senders * capacity, features)
+    buckets = received[:, :, features : features + bucket_lanes].astype(jnp.int32).reshape(event_count)
 
     places = block_place[0]
     block_count = places.shape[0]
@@ -125,7 +132,7 @@
         .astype(jnp.bfloat16)
         .reshape(senders, capacity, features)
     )
-    returned = lax.all_to_all(update, axes, split_axis=0, concat_axis=0, tiled=True)
+    returned = exchange(update)
     update = returned.reshape(devices * capacity, features)[flat_slot]
     return (cand_x.astype(jnp.float32) + update.astype(jnp.float32)).astype(jnp.bfloat16)
 

time: 252 us -> 243 us (0.964)
  waiting for transfers between devices: 143 us -> 98 us
  blocking collectives: 30.5 us -> 67.4 us
  between operations: 14.2 us -> 0.87 us
  local copies, waits for them, and re-layouts: 16.3 us -> 22.9 us
    all_gather x1 -> x0, waiting for transfers between devices: 123 us -> none  [shards(): every_bucket = lax.all_gather(store_bucket, axes, axis=0, tiled=True)]
    all_to_all x1, waiting for transfers between devices: 0.01 us -> 82.3 us  [shards(): lax.all_to_all(kv_store, axes, split_axis=1, concat_axis=0, tiled=True)]
    all_to_all x1 -> x3, blocking collectives: 30.5 us -> 67.4 us  [the longest x2 43.5 us: exchange(): lax.all_to_all(values, 'cache', split_axis=1, concat_axis=1, tiled=True)]
    convert_element_type x1 -> x2, local copies, waits for them, and re-layouts: 1.39 us -> 5.69 us  [prepare(): normed = layer_norm(inputs.astype(jnp.float32)).astype(jnp.bfloat16)]
    reshape x3 -> x0, local copies, waits for them, and re-layouts: 3.82 us -> none  [the longest x1 1.34 us: shards(): update = returned.reshape(devices * capacity, features)[flat_slot]]
    dynamic_slice x1 -> x0, local copies, waits for them, and re-layouts: 3.75 us -> none  [shards(): lax.dynamic_index_in_dim(every_bucket, me, axis=1, keepdims=False)]
    all_to_all x0 -> x3, local copies, waits for them, and re-layouts: none -> 3.56 us  [the longest x2 2.2 us: exchange(): lax.all_to_all(values, 'cache', split_axis=1, concat_axis=1, tiled=True)]
    another operation x3 -> x6, local copies, waits for them, and re-layouts: 0.02 us -> 3.19 us  [the longest x2 1.84 us: exchange(): values = values.reshape((outer, inner) + rest)]
  transfers between devices with their start and end apart: 3 -> 2, of which waited for: 2 -> 2; matrix products, arithmetic and copies ran while one was open for 7% -> 8% of each run, Pallas kernels for 0% -> 0%
where the time goes in v4:
time: 243 us; the launch traced here: 241 us
  waiting for transfers between devices  98 us (40%)
  blocking collectives  67.4 us (28%)
  local copies, waits for them, and re-layouts  22.9 us (9%)
  Pallas kernels  16 us (7%)
  starting transfers between devices  14.5 us (6%)
  matrix products  11.7 us (5%)
  other arithmetic  9.58 us (4%)
    all_to_all x1, waiting for transfers between devices, shards(): lax.all_to_all(kv_store, axes, split_axis=1, concat_axis=0, tiled=True)  82.3 us
    all_to_all x2, blocking collectives, exchange(): lax.all_to_all(values, 'cache', split_axis=1, concat_axis=1, tiled=True)  43.5 us
    all_to_all x1, blocking collectives, exchange(): lax.all_to_all(values, 'req', split_axis=0, concat_axis=0, tiled=True)  23.9 us
    pallas_call x1, Pallas kernels, attend(): pl.pallas_call(kernel, grid=(head_count,), in_specs=[pl.BlockSpec((slot_c...  16 us
    all_to_all x1, waiting for transfers between devices, exchange(): lax.all_to_all(values, 'req', split_axis=0, concat_axis=0, tiled=True)  15.7 us
    all_to_all x1, starting transfers between devices, exchange(): lax.all_to_all(values, 'req', split_axis=0, concat_axis=0, tiled=True)  7.41 us
    dot_general x1, matrix products, prepare(): jnp.dot(normed, w_proj, preferred_element_type=jnp.float32)  7.08 us
    all_to_all x1, starting transfers between devices, shards(): lax.all_to_all(kv_store, axes, split_axis=1, concat_axis=0, tiled=True)  7.05 us
  transfers between devices with their start and end apart: 2, of which 2 were waited for; matrix products, arithmetic and copies ran while one was open for 8% of the time, Pallas kernels for 0%

profile of v4, /device:TPU:1, one launch (start us, length us, event | category | flops | bytes accessed | tf_op | source)
XLA Modules:
  0.0 240.9 jit_solution(5279420655095883568)
XLA Ops:
  0.0 0.0 copy-start
  0.0 0.9 copy.85
  1.0 0.2 fusion.11
  1.3 0.9 fusion.13
  2.1 0.7 compare_select_fusion
  2.8 3.2 %scatter_custom_fusion = bf16[512,1024]{1,0:T(8,128)(2,1)} fusion(s32[256]{0:T(256)S(1)} %bitcast.45, bf16[256,1024]{1,0:T(8,128)(2,1)} %param.9, bf16[]{:T(256)} %constant.10.clone.1), kind=kCustom, calls=%fused_computation.23 | custom fusion | bytes 1049088 | tf_op jit(solution)/shard_map/scatter | solution.py:100
  6.0 1.5 concatenate.8
  7.4 0.0 copy-done.2
  7.5 0.2 copy.102
  7.7 0.1 copy.89
  7.8 0.6 pad_maximum_fusion
  8.4 23.1 %all_to_all.29 = bf16[16,8,4,1152]{3,2,0,1:T(4,128)(2,1)S(1)} all-to-all(bf16[16,8,4,1152]{3,2,0,1:T(4,128)(2,1)S(1)} %pad_maximum_fusion), channel_id=1, replica_groups=mesh['req'=16,'cache'=8] {'cache'}, dimensions={1} | all-to-all | bytes 2359296 | tf_op jit(solution)/shard_map/all_to_all | solution.py:72
  31.5 0.7 copy.90
  32.2 23.9 %all_to_all.30 = bf16[16,8,4,1152]{3,1,2,0:T(8,128)(2,1)} all-to-all(bf16[16,8,4,1152]{3,1,2,0:T(8,128)(2,1)S(1)} %copy.90), channel_id=1, replica_groups=mesh['req'=16,'cache'=8] {'req'}, dimensions={0} | all-to-all | bytes 2359296 | tf_op jit(solution)/shard_map/all_to_all | solution.py:73
  56.1 7.0 %all-to-all-start.2 = ((bf16[1,128,1,16,2048]{4,3,2,0,1:T(8,128)(2,1)}), bf16[1,128,1,16,2048]{4,3,2,0,1:T(8,128)(2,1)}, u32[]{:S(2)}, u32[]{:S(2)}) async-start(bf16[1,128,1,16,2048]{4,3,2,0,1:T(8,128)(2,1)} %bitcast.37), calls=%async_computation.2 | async-start | bytes 16777216 | tf_op jit(solution)/shard_map/all_to_all | solution.py:91
  63.8 0.0 copy-done.4
  63.8 0.1 select_reduce_fusion
  63.9 0.1 fusion.16
  64.0 1.6 reshape.143.live_ref
  65.7 1.4 copy.108
  67.0 0.2 fusion.7
  67.2 0.1 copy.93
  67.4 0.4 multiply_reduce_fusion.1
  67.8 0.1 copy.94
  67.9 0.1 rsqrt.20
  68.0 0.1 div.19
  68.1 0.3 slice_convert_fusion
  68.4 2.7 %copy.92 = f32[128,4,1024]{2,1,0:T(4,128)} copy(f32[128,4,1024]{2,0,1:T(8,128)S(1)} %slice_convert_fusion) | data formatting | bytes 4194304 | tf_op jit(solution)/shard_map/convert_element_type | solution.py:20
  71.1 2.9 %reshape.124 = f32[512,1024]{1,0:T(8,128)} reshape(f32[128,4,1024]{2,1,0:T(4,128)} %copy.92) | data formatting | bytes 4194304 | tf_op jit(solution)/shard_map/convert_element_type | solution.py:20
  74.1 0.2 copy.97
  74.3 0.3 reshape.125
  74.5 1.1 fusion.bias_ref
  75.6 7.1 %multiply_convert_fusion.q_ref = bf16[512,2048]{1,0:T(8,128)(2,1)} fusion(bf16[1024,2048]{1,0:T(8,128)(2,1)} %param.15, f32[512,1024]{1,0:T(8,128)} %reshape.124, f32[512]{0:T(512)S(1)} %rsqrt.20, f32[512]{0:T(512)S(1)} %div.19), kind=kOutput, calls=%fused_computation.2 | convolution fusion | flops 2154299392 | bytes 8392704 | tf_op jit(solution)/shard_map/dot_general | solution.py:21
  82.7 82.3 %all-to-all-done.2 = bf16[1,128,1,16,2048]{4,3,2,0,1:T(8,128)(2,1)} async-done(((bf16[1,128,1,16,2048]{4,3,2,0,1:T(8,128)(2,1)}), bf16[1,128,1,16,2048]{4,3,2,0,1:T(8,128)(2,1)}, u32[]{:S(2)}, u32[]{:S(2)}) %all-to-all-start.2) | async-done | bytes 8388640 | tf_op jit(solution)/shard_map/all_to_all | solution.py:91
  165.0 16.0 %shard_map.91 = f32[512,1024]{1,0:T(8,128)} custom-call(bf16[512,2048]{1,0:T(8,128)(2,1)} %multiply_convert_fusion.q_ref, bf16[2048,2048]{1,0:T(8,128)(2,1)} %bitcast.11.k_ref.v_ref, bf16[2048,2048]{1,0:T(8,128)(2,1)} %bitcast.11.k_ref.v_ref, f32[8,2048]{1,0:T(8,128)} %fusion.bias_ref, f32[2048,1]{1,0:T(8,128)} %reshape.143.live_ref), custom_call_target="tpu_custom_call" | custom-call | tf_op jit(solution)/shard_map/pallas_call | solution.py:52
  181.0 1.8 reduce_sum.61
  182.8 2.1 multiply_reduce_fusion
  184.9 0.1 copy-done.1
  185.0 3.6 %convolution_convert_fusion = bf16[512,1024]{1,0:T(8,128)(2,1)} fusion(bf16[1024,1024]{1,0:T(8,128)(2,1)S(1)} %copy-done, f32[512,1024]{1,0:T(8,128)S(1)} %copy-done.1, bf16[512,2048]{1,0:T(8,128)(2,1)} %multiply_convert_fusion.q_ref, f32[512]{0:T(512)S(1)} %add_rsqrt_fusion, f32[512]{0:T(512)S(1)} %broadcast_multiply_fusion), kind=kOutput, calls=%fused_computation.9 | convolution fusion | flops 1076887552 | bytes 6295552 | tf_op jit(solution)/shard_map/dot_general | solution.py:131
  188.5 1.5 reshape_reshape.6
  190.0 0.4 copy.99
  190.4 20.3 %all_to_all.31 = bf16[16,8,4,1024]{3,2,0,1:T(4,128)(2,1)S(1)} all-to-all(bf16[16,8,4,1024]{3,2,0,1:T(4,128)(2,1)S(1)} %copy.99), channel_id=1, replica_groups=mesh['req'=16,'cache'=8] {'cache'}, dimensions={1} | all-to-all | bytes 2097152 | tf_op jit(solution)/shard_map/all_to_all | solution.py:72
  210.7 1.5 copy.100
  212.3 7.4 %all-to-all-start.4 = ((bf16[16,8,4,1024]{3,2,1,0:T(4,128)(2,1)}), bf16[16,8,4,1024]{3,2,1,0:T(4,128)(2,1)}, u32[]{:S(2)}, u32[]{:S(2)}) async-start(bf16[16,8,4,1024]{3,2,1,0:T(4,128)(2,1)} %copy.100), calls=%async_computation.4 | async-start | bytes 2097152 | tf_op jit(solution)/shard_map/all_to_all | solution.py:73
  219.7 15.7 %all-to-all-done.4 = bf16[16,8,4,1024]{3,2,1,0:T(4,128)(2,1)} async-done(((bf16[16,8,4,1024]{3,2,1,0:T(4,128)(2,1)}), bf16[16,8,4,1024]{3,2,1,0:T(4,128)(2,1)}, u32[]{:S(2)}, u32[]{:S(2)}) %all-to-all-start.4) | async-done | bytes 1048608 | tf_op jit(solution)/shard_map/all_to_all | solution.py:73
  235.4 1.3 reshape_reshape.7
  236.8 2.0 gather_fusion
  238.7 2.2 add_convert_fusion
  (21 shorter events, 0.2 us)
Async XLA Ops:
  0.0 184.9 %copy-start = (bf16[1024,1024]{1,0:T(8,128)(2,1)S(1)}, bf16[1024,1024]{1,0:T(8,128)(2,1)}, u32[]{:S(2)}) copy-start(bf16[1024,1024]{1,0:T(8,128)(2,1)} %param.16) | copy-start | bytes 6291460
  0.0 7.4 %copy-start.2 = (s32[1,128,1,16]{1,3,2,0:T(8,128)S(1)}, s32[1,128,1,16]{1,3,2,0:T(8,128)}, u32[]{:S(2)}) copy-start(s32[1,128,1,16]{1,3,2,0:T(8,128)} %param.14) | copy-start | bytes 24580
  56.1 7.7 %copy-start.4 = (s32[1,128]{1,0:T(1,128)S(1)}, s32[1,128]{1,0:T(1,128)}, u32[]{:S(2)}) copy-start(s32[1,128]{1,0:T(1,128)} %param.12) | copy-start | bytes 1540
  56.1 108.9 %all-to-all-start.2 = ((bf16[1,128,1,16,2048]{4,3,2,0,1:T(8,128)(2,1)}), bf16[1,128,1,16,2048]{4,3,2,0,1:T(8,128)(2,1)}, u32[]{:S(2)}, u32[]{:S(2)}) async-start(bf16[1,128,1,16,2048]{4,3,2,0,1:T(8,128)(2,1)} %bitcast.37), calls=%async_computation.2 | async-start | bytes 16777216 | tf_op jit(solution)/shard_map/all_to_all | solution.py:91
  71.1 3.4 %copy-start.3 = (f32[8,128]{1,0:T(8,128)S(1)}, f32[8,128]{1,0:T(8,128)}, u32[]{:S(2)}) copy-start(f32[8,128]{1,0:T(8,128)} %param.17) | copy-start | bytes 12292
  182.7 2.2 copy-start.1
  212.3 23.1 %all-to-all-start.4 = ((bf16[16,8,4,1024]{3,2,1,0:T(4,128)(2,1)}), bf16[16,8,4,1024]{3,2,1,0:T(4,128)(2,1)}, u32[]{:S(2)}, u32[]{:S(2)}) async-start(bf16[16,8,4,1024]{3,2,1,0:T(4,128)(2,1)} %copy.100), calls=%async_computation.4 | async-start | bytes 2097152 | tf_op jit(solution)/shard_map/all_to_all | solution.py:73

commit v5 on v2

--- a/solution.py
+++ b/solution.py
@@ -53,7 +53,7 @@
         kernel,
         grid=(head_count,),
         in_specs=[
-            pl.BlockSpec((slot_count, head_dim), lambda h: (0, head_count + h)),
+            pl.BlockSpec((slot_count, head_dim), lambda h: (0, h)),
             pl.BlockSpec((event_count, head_dim), lambda h: (0, h)),
             pl.BlockSpec((event_count, head_dim), lambda h: (0, head_count + h)),
             pl.BlockSpec(half_bias.shape, lambda h: (0, 0)),
@@ -77,18 +77,24 @@
     per_owner = kv_store.shape[2]
     block_ev = kv_store.shape[3]
     capacity = max(2, 2 * row_count // devices)
-    event_count = devices * per_owner * block_ev
-    kv_send = kv_store.reshape(devices, per_owner * block_ev, 2 * features)
+    rows_per = per_owner * block_ev
+    event_count = devices * rows_per
+
+    projected = prepare(cand_x, w_proj)
+    gate_u = projected[:, :features]
+    query = projected[:, features:]
 
     target = cand_req[:, 0]
     onehot = (target[:, None] == jnp.arange(devices, dtype=jnp.int32)[None, :]).astype(jnp.int32)
     earlier = jnp.cumsum(onehot, axis=0) - onehot
     slot_rank = jnp.sum(earlier * onehot, axis=1)
     flat_slot = target * capacity + slot_rank
-    empty = jnp.zeros((devices * capacity, features), cand_x.dtype)
-    rows_per = per_owner * block_ev
-    slotted = empty.at[flat_slot].set(cand_x).reshape(devices, rows_per, capacity * features // rows_per)
+    empty = jnp.zeros((devices * capacity, features), query.dtype)
+    query_width = capacity * features // rows_per
+    slotted = empty.at[flat_slot].set(query).reshape(devices, rows_per, query_width)
+    kv_send = kv_store.reshape(devices, rows_per, 2 * features)
     bucket_send = store_bucket.reshape(devices, rows_per, 1).astype(cand_x.dtype)
+    bucket_send = jnp.pad(bucket_send, ((0, 0), (0, 0), (0, 127)))
     received = lax.all_to_all(
         jnp.concatenate([kv_send, slotted, bucket_send], axis=2),
         axes,
@@ -99,8 +105,10 @@
     senders = received.shape[0]
     width = received.shape[2]
     events = received.reshape(event_count, width)
-    flat_rows = received[:, :, 2 * features : width - 1].reshape(senders * capacity, features)
-    buckets = received[:, :, width - 1].astype(jnp.int32).reshape(event_count)
+    slot_query = received[:, :, 2 * features : 2 * features + query_width].reshape(
+        senders * capacity, features
+    )
+    buckets = received[:, :, 2 * features + query_width].astype(jnp.int32).reshape(event_count)
 
     places = block_place[0]
     block_count = places.shape[0]
@@ -117,18 +125,12 @@
     half_bias = 0.5 * jnp.dot(time_bias, bucket_table, precision=lax.Precision.HIGHEST)
     half_scale = 0.5 / math.sqrt(head_dim)
 
-    projected = prepare(flat_rows, w_proj)
-    slot_count = projected.shape[0]
-    gate_u = projected[:, :features]
-    attended = attend(projected, events, half_bias, live, head_count, head_dim, half_scale)
-    hidden = (layer_norm(attended) * gate_u.astype(jnp.float32)).astype(jnp.bfloat16)
-    update = (
-        jnp.dot(hidden, w_out, preferred_element_type=jnp.float32)
-        .astype(jnp.bfloat16)
-        .reshape(senders, capacity, features)
-    )
-    returned = lax.all_to_all(update, axes, split_axis=0, concat_axis=0, tiled=True)
-    update = returned.reshape(devices * capacity, features)[flat_slot]
+    attended = attend(slot_query, events, half_bias, live, head_count, head_dim, half_scale)
+    normal = layer_norm(attended).astype(jnp.bfloat16).reshape(senders, capacity, features)
+    returned = lax.all_to_all(normal, axes, split_axis=0, concat_axis=0, tiled=True)
+    normal = returned.reshape(devices * capacity, features)[flat_slot]
+    hidden = (normal.astype(jnp.float32) * gate_u.astype(jnp.float32)).astype(jnp.bfloat16)
+    update = jnp.dot(hidden, w_out, preferred_element_type=jnp.float32).astype(jnp.bfloat16)
     return (cand_x.astype(jnp.float32) + update.astype(jnp.float32)).astype(jnp.bfloat16)
 
 

time: 233 us -> 228 us (0.979)
  other arithmetic: 27.1 us -> 22.6 us
  matrix products: 10.6 us -> 7.74 us
  starting transfers between devices: 24 us -> 26.7 us
    convert_element_type x3 -> x1, local copies, waits for them, and re-layouts: 4.23 us -> 0.08 us  [shards(): received[:, :, 2 * features + query_width].astype(jnp.int32)]
    dot_general x1, matrix products: 7 us -> 3.81 us  [prepare(): jnp.dot(normed, w_proj, preferred_element_type=jnp.float32)]
    convert_element_type x3 -> x2, other arithmetic: 8.31 us -> 5.14 us  [the longest x1 3.28 us: shards(): received[:, :, 2 * features + query_width].astype(jnp.int32)]
    all_to_all x1, starting transfers between devices: 12.1 us -> 14.8 us  [shards(): lax.all_to_all(normal, axes, split_axis=0, concat_axis=0, tiled=True)]
    reshape x3 -> x4, local copies, waits for them, and re-layouts: 4.29 us -> 5.77 us  [the longest x1 1.7 us: shards(): empty.at[flat_slot].set(query).reshape(devices, rows_per, query_width)]
where the time goes in v5:
time: 228 us
  waiting for transfers between devices  137 us (60%)
  starting transfers between devices  26.7 us (12%)
  other arithmetic  22.6 us (10%)
  local copies, waits for them, and re-layouts  16.4 us (7%)
  Pallas kernels  16 us (7%)
  matrix products  7.74 us (3%)
    all_to_all x1, waiting for transfers between devices, shards(): lax.all_to_all(jnp.concatenate([kv_send, slotted, bucket_send], axis=2),...  119 us
    all_to_all x1, waiting for transfers between devices, shards(): lax.all_to_all(normal, axes, split_axis=0, concat_axis=0, tiled=True)  18.7 us
    pallas_call x1, Pallas kernels, attend(): pl.pallas_call(kernel, grid=(head_count,), in_specs=[pl.BlockSpec((slot_c...  16 us
    all_to_all x1, starting transfers between devices, shards(): lax.all_to_all(normal, axes, split_axis=0, concat_axis=0, tiled=True)  14.8 us
    all_to_all x1, starting transfers between devices, shards(): lax.all_to_all(jnp.concatenate([kv_send, slotted, bucket_send], axis=2),...  11.9 us
    concatenate x1, other arithmetic, shards(): jnp.concatenate([kv_send, slotted, bucket_send], axis=2)  9.09 us
  transfers between devices with their start and end apart: 2, of which 2 were waited for; matrix products, arithmetic and copies ran while one was open for 1% of the time, Pallas kernels for 0%

profile of v5, /device:TPU:1, one launch (start us, length us, event | category | flops | bytes accessed | tf_op | source)
XLA Modules:
  0.0 227.7 jit_solution(13010530867852444376)
XLA Ops:
  0.0 0.0 copy-start
  0.0 1.3 convert_reduce_fusion
  1.3 1.3 fusion.7
  2.7 0.8 copy.16
  3.5 0.2 fusion.20
  3.8 0.9 fusion.22
  4.6 0.7 compare_select_fusion
  5.3 0.0 copy-start.2
  5.3 3.8 %multiply_convert_fusion.1 = bf16[256,2048]{1,0:T(8,128)(2,1)S(1)} fusion(bf16[1024,2048]{1,0:T(8,128)(2,1)} %param.15, bf16[256,1024]{1,0:T(8,128)(2,1)} %param.9, f32[256]{0:T(256)S(1)} %add_rsqrt_fusion.1, f32[256]{0:T(256)S(1)} %broadcast_multiply_fusion.1), kind=kOutput, calls=%fused_computation.9 | convolution fusion | flops 1077411840 | bytes 5769216 | tf_op jit(solution)/shard_map/dot_general | solution.py:21
  9.1 0.0 copy-start.1
  9.2 1.0 copy-done.1
  10.1 2.7 %scatter_custom_fusion = bf16[512,1024]{1,0:T(8,128)(2,1)} fusion(s32[256]{0:T(256)S(1)} %bitcast.36, bf16[256,2048]{1,0:T(8,128)(2,1)S(1)} %multiply_convert_fusion.1, bf16[]{:T(256)} %constant.10.clone.1), kind=kCustom, calls=%fused_computation.25 | custom fusion | bytes 1572866 | tf_op jit(solution)/shard_map/scatter | solution.py:94
  12.8 1.7 reshape.121
  14.5 0.0 copy-done.2
  14.5 1.2 copy.20
  15.8 9.1 %fusion.1 = bf16[128,16,2432]{2,1,0:T(8,128)(2,1)} fusion(bf16[128,16,1]{2,1,0:T(8,128)(2,1)} %copy.20, bf16[128,16,256]{2,1,0:T(8,128)(2,1)S(1)} %reshape.121, bf16[128,16,2048]{2,1,0:T(8,128)(2,1)} %bitcast.29), kind=kLoop, calls=%fused_computation.4 | loop fusion | flops 39845888 | bytes 19402752 | tf_op jit(solution)/shard_map/concatenate | solution.py:99
  24.8 0.0 copy-start.4
  24.8 11.9 %all-to-all-start = ((bf16[128,16,2432]{2,1,0:T(8,128)(2,1)}), bf16[128,16,2432]{2,1,0:T(8,128)(2,1)}, u32[]{:S(2)}, u32[]{:S(2)}) async-start(bf16[128,16,2432]{2,1,0:T(8,128)(2,1)} %fusion.1), calls=%async_computation | async-start | bytes 19922944 | tf_op jit(solution)/shard_map/all_to_all | solution.py:98
  36.7 0.0 copy-start.3
  37.4 0.0 copy-done.4
  37.4 0.1 select_reduce_fusion
  37.5 0.1 fusion.25
  37.6 1.6 reshape.144.live_ref
  39.2 118.8 %all-to-all-done = bf16[128,16,2432]{2,1,0:T(8,128)(2,1)} async-done(((bf16[128,16,2432]{2,1,0:T(8,128)(2,1)}), bf16[128,16,2432]{2,1,0:T(8,128)(2,1)}, u32[]{:S(2)}, u32[]{:S(2)}) %all-to-all-start) | async-done | bytes 9961504 | tf_op jit(solution)/shard_map/all_to_all | solution.py:98
  158.0 1.3 slice.28
  159.3 1.5 reshape.122.q_ref
  160.7 3.3 %convert_reduce_fusion.1 = s32[128,16]{1,0:T(8,128)S(1)} fusion(bf16[128,16,2432]{2,1,0:T(8,128)(2,1)} %all-to-all-done), kind=kLoop, calls=%fused_computation.20 | loop fusion | flops 2048 | bytes 12288 | tf_op jit(solution)/shard_map/convert_element_type | solution.py:111
  164.0 0.1 reshape.126
  164.1 0.0 copy-done.3
  164.1 1.1 fusion.2.bias_ref
  165.2 16.0 %shard_map.91 = f32[512,1024]{1,0:T(8,128)} custom-call(bf16[512,1024]{1,0:T(8,128)(2,1)} %reshape.122.q_ref, bf16[2048,2432]{1,0:T(8,128)(2,1)} %bitcast.9.k_ref.v_ref, bf16[2048,2432]{1,0:T(8,128)(2,1)} %bitcast.9.k_ref.v_ref, f32[8,2048]{1,0:T(8,128)} %fusion.2.bias_ref, f32[2048,1]{1,0:T(8,128)} %reshape.144.live_ref), custom_call_target="tpu_custom_call" | custom-call | tf_op jit(solution)/shard_map/pallas_call | solution.py:52
  181.2 1.8 reduce_sum.61
  183.0 1.9 multiply_reduce_fusion
  184.9 1.9 multiply_convert_fusion
  186.8 1.2 reshape.124
  188.0 14.8 %all-to-all-start.1 = ((bf16[128,4,1024]{2,1,0:T(4,128)(2,1)}), bf16[128,4,1024]{2,1,0:T(4,128)(2,1)}, u32[]{:S(2)}, u32[]{:S(2)}) async-start(bf16[128,4,1024]{2,1,0:T(4,128)(2,1)} %reshape.124), calls=%async_computation.1 | async-start | bytes 2097152 | tf_op jit(solution)/shard_map/all_to_all | solution.py:130
  202.9 18.7 %all-to-all-done.1 = bf16[128,4,1024]{2,1,0:T(4,128)(2,1)} async-done(((bf16[128,4,1024]{2,1,0:T(4,128)(2,1)}), bf16[128,4,1024]{2,1,0:T(4,128)(2,1)}, u32[]{:S(2)}, u32[]{:S(2)}) %all-to-all-start.1) | async-done | bytes 1048608 | tf_op jit(solution)/shard_map/all_to_all | solution.py:130
  221.6 1.3 reshape.125
  222.9 2.0 gather_fusion
  224.9 0.0 copy-done
  224.9 2.9 %fusion.4 = bf16[256,1024]{1,0:T(8,128)(2,1)} fusion(bf16[1024,1024]{1,0:T(8,128)(2,1)S(1)} %copy-done, bf16[256,1024]{1,0:T(8,128)(2,1)} %param.9, bf16[256,1024]{1,0:T(8,128)(2,1)} %gather_fusion, bf16[256,2048]{1,0:T(8,128)(2,1)} %copy-done.1), kind=kOutput, calls=%fused_computation.15 | convolution fusion | flops 539230208 | bytes 4194304 | tf_op jit(solution)/shard_map/dot_general | solution.py:133
  (13 shorter events, 0.1 us)
Async XLA Ops:
  0.0 224.9 %copy-start = (bf16[1024,1024]{1,0:T(8,128)(2,1)S(1)}, bf16[1024,1024]{1,0:T(8,128)(2,1)}, u32[]{:S(2)}) copy-start(bf16[1024,1024]{1,0:T(8,128)(2,1)} %param.16) | copy-start | bytes 6291460
  5.3 9.2 %copy-start.2 = (s32[1,128,1,16]{1,3,2,0:T(8,128)S(1)}, s32[1,128,1,16]{1,3,2,0:T(8,128)}, u32[]{:S(2)}) copy-start(s32[1,128,1,16]{1,3,2,0:T(8,128)} %param.14) | copy-start | bytes 24580
  9.1 1.0 copy-start.1
  24.8 12.6 %copy-start.4 = (s32[1,128]{1,0:T(1,128)S(1)}, s32[1,128]{1,0:T(1,128)}, u32[]{:S(2)}) copy-start(s32[1,128]{1,0:T(1,128)} %param.12) | copy-start | bytes 1540
  24.8 133.1 %all-to-all-start = ((bf16[128,16,2432]{2,1,0:T(8,128)(2,1)}), bf16[128,16,2432]{2,1,0:T(8,128)(2,1)}, u32[]{:S(2)}, u32[]{:S(2)}) async-start(bf16[128,16,2432]{2,1,0:T(8,128)(2,1)} %fusion.1), calls=%async_computation | async-start | bytes 19922944 | tf_op jit(solution)/shard_map/all_to_all | solution.py:98
  36.7 127.4 %copy-start.3 = (f32[8,128]{1,0:T(8,128)S(1)}, f32[8,128]{1,0:T(8,128)}, u32[]{:S(2)}) copy-start(f32[8,128]{1,0:T(8,128)} %param.17) | copy-start | bytes 12292
  188.0 33.5 %all-to-all-start.1 = ((bf16[128,4,1024]{2,1,0:T(4,128)(2,1)}), bf16[128,4,1024]{2,1,0:T(4,128)(2,1)}, u32[]{:S(2)}, u32[]{:S(2)}) async-start(bf16[128,4,1024]{2,1,0:T(4,128)(2,1)} %reshape.124), calls=%async_computation.1 | async-start | bytes 2097152 | tf_op jit(solution)/shard_map/all_to_all | solution.py:130

commit v6 on v4

--- a/solution.py
+++ b/solution.py
@@ -64,16 +64,6 @@
     )(projected, events, events, half_bias, live)
 
 
-def exchange(values):
-    outer = lax.axis_size("req")
-    inner = lax.axis_size("cache")
-    rest = values.shape[1:]
-    values = values.reshape((outer, inner) + rest)
-    values = lax.all_to_all(values, "cache", split_axis=1, concat_axis=1, tiled=True)
-    values = lax.all_to_all(values, "req", split_axis=0, concat_axis=0, tiled=True)
-    return values.reshape((outer * inner,) + rest)
-
-
 def shards(
     cand_x, cand_req, hist_len, block_place, kv_store, store_bucket, w_proj, w_out, time_bias
 ):
@@ -89,7 +79,6 @@
     capacity = max(2, 2 * row_count // devices)
     event_count = devices * per_owner * block_ev
     arrived = lax.all_to_all(kv_store, axes, split_axis=1, concat_axis=0, tiled=True)
-    events = arrived.reshape(event_count, 2 * features)
 
     target = cand_req[:, 0]
     onehot = (target[:, None] == jnp.arange(devices, dtype=jnp.int32)[None, :]).astype(jnp.int32)
@@ -102,7 +91,10 @@
     bucket_lanes = rows_per // capacity
     bucket_send = store_bucket.reshape(devices, capacity, bucket_lanes).astype(cand_x.dtype)
     bucket_send = jnp.pad(bucket_send, ((0, 0), (0, 0), (0, 128 - bucket_lanes)))
-    received = exchange(jnp.concatenate([slotted, bucket_send], axis=2))
+    send = jnp.concatenate([slotted, bucket_send], axis=2)
+    arrived, send = lax.optimization_barrier((arrived, send))
+    events = arrived.reshape(event_count, 2 * features)
+    received = lax.all_to_all(send, axes, split_axis=0, concat_axis=0, tiled=True)
     senders = received.shape[0]
     flat_rows = received[:, :, :features].reshape(senders * capacity, features)
     buckets = received[:, :, features : features + bucket_lanes].astype(jnp.int32).reshape(event_count)
@@ -132,7 +124,7 @@
         .astype(jnp.bfloat16)
         .reshape(senders, capacity, features)
     )
-    returned = exchange(update)
+    returned = lax.all_to_all(update, axes, split_axis=0, concat_axis=0, tiled=True)
     update = returned.reshape(devices * capacity, features)[flat_slot]
     return (cand_x.astype(jnp.float32) + update.astype(jnp.float32)).astype(jnp.bfloat16)
 

time: 243 us -> 215 us (0.88)
  blocking collectives: 67.4 us -> 0 us
  waiting for transfers between devices: 98 us -> 131 us
  starting transfers between devices: 14.5 us -> 28.8 us
  local copies, waits for them, and re-layouts: 22.9 us -> 15.3 us
    all_to_all x3 -> x0, blocking collectives: 67.4 us -> none  [the longest x2 43.5 us: exchange(): lax.all_to_all(values, 'cache', split_axis=1, concat_axis=1, tiled=True)]
    all_to_all x1 -> x2, waiting for transfers between devices: 15.7 us -> 36.7 us  [the longest x1 18.8 us: shards(): lax.all_to_all(update, axes, split_axis=0, concat_axis=0, tiled=True)]
    all_to_all x1, waiting for transfers between devices: 82.3 us -> 94.3 us  [shards(): lax.all_to_all(kv_store, axes, split_axis=1, concat_axis=0, tiled=True)]
    all_to_all x1 -> x2, starting transfers between devices: 7.41 us -> 16.9 us  [the longest x1 11.1 us: shards(): lax.all_to_all(send, axes, split_axis=0, concat_axis=0, tiled=True)]
    all_to_all x1, starting transfers between devices: 7.05 us -> 12 us  [shards(): lax.all_to_all(kv_store, axes, split_axis=1, concat_axis=0, tiled=True)]
    reshape x0 -> x3, local copies, waits for them, and re-layouts: none -> 4.04 us  [the longest x1 1.46 us: shards(): empty.at[flat_slot].set(cand_x).reshape(devices, capacity, features)]
    all_to_all x3 -> x0, local copies, waits for them, and re-layouts: 3.56 us -> none  [the longest x2 2.2 us: exchange(): lax.all_to_all(values, 'cache', split_axis=1, concat_axis=1, tiled=True)]
    another operation x6 -> x3, local copies, waits for them, and re-layouts: 3.19 us -> 0.02 us  [the longest x2 1.84 us: exchange(): values = values.reshape((outer, inner) + rest)]
  transfers between devices with their start and end apart: 2 -> 3, of which waited for: 2 -> 3; matrix products, arithmetic and copies ran while one was open for 8% -> 4% of each run, Pallas kernels for 0% -> 0%
where the time goes in v6:
time: 215 us; the launch traced here: 214 us
  waiting for transfers between devices  131 us (61%)
  starting transfers between devices  28.8 us (13%)
  Pallas kernels  16 us (7%)
  local copies, waits for them, and re-layouts  15.3 us (7%)
  other arithmetic  11.8 us (5%)
  matrix products  10.7 us (5%)
    all_to_all x1, waiting for transfers between devices, shards(): lax.all_to_all(kv_store, axes, split_axis=1, concat_axis=0, tiled=True)  94.3 us
    all_to_all x1, waiting for transfers between devices, shards(): lax.all_to_all(update, axes, split_axis=0, concat_axis=0, tiled=True)  18.8 us
    all_to_all x1, waiting for transfers between devices, shards(): lax.all_to_all(send, axes, split_axis=0, concat_axis=0, tiled=True)  17.9 us
    pallas_call x1, Pallas kernels, attend(): pl.pallas_call(kernel, grid=(head_count,), in_specs=[pl.BlockSpec((slot_c...  16 us
    all_to_all x1, starting transfers between devices, shards(): lax.all_to_all(kv_store, axes, split_axis=1, concat_axis=0, tiled=True)  12 us
    all_to_all x1, starting transfers between devices, shards(): lax.all_to_all(send, axes, split_axis=0, concat_axis=0, tiled=True)  11.1 us
    dot_general x1, matrix products, prepare(): jnp.dot(normed, w_proj, preferred_element_type=jnp.float32)  7.08 us
    all_to_all x1, starting transfers between devices, shards(): lax.all_to_all(update, axes, split_axis=0, concat_axis=0, tiled=True)  5.77 us
  transfers between devices with their start and end apart: 3, of which 3 were waited for; matrix products, arithmetic and copies ran while one was open for 4% of the time, Pallas kernels for 0%

profile of v6, /device:TPU:1, one launch (start us, length us, event | category | flops | bytes accessed | tf_op | source)
XLA Modules:
  0.0 214.4 jit_solution(1193769902722484430)
XLA Ops:
  0.0 0.0 copy-start
  0.0 0.0 copy-start.3
  0.0 0.0 copy-start.2
  0.0 12.0 %all-to-all-start = ((bf16[1,128,1,16,2048]{4,3,2,0,1:T(8,128)(2,1)}), bf16[1,128,1,16,2048]{4,3,2,0,1:T(8,128)(2,1)}, u32[]{:S(2)}, u32[]{:S(2)}) async-start(bf16[1,128,1,16,2048]{4,3,2,0,1:T(8,128)(2,1)} %bitcast.30), calls=%async_computation | async-start | bytes 16777216 | tf_op jit(solution)/shard_map/all_to_all | solution.py:81
  12.0 0.0 copy-done.3
  12.0 0.0 copy-done.2
  12.0 0.1 copy.22
  12.1 0.2 fusion.13
  12.4 0.2 copy.24
  12.6 0.2 fusion.15
  12.8 3.2 %scatter_custom_fusion = bf16[512,1024]{1,0:T(8,128)(2,1)} fusion(s32[256]{0:T(256)S(1)} %bitcast.38, bf16[256,1024]{1,0:T(8,128)(2,1)} %param.9, bf16[]{:T(256)} %constant.10.clone.1), kind=kCustom, calls=%fused_computation.24 | custom fusion | bytes 1049088 | tf_op jit(solution)/shard_map/scatter | solution.py:89
  16.1 1.5 reshape.122
  17.5 0.0 copy-start.6
  17.5 1.7 fusion.2
  19.2 94.3 %all-to-all-done = bf16[1,128,1,16,2048]{4,3,2,0,1:T(8,128)(2,1)} async-done(((bf16[1,128,1,16,2048]{4,3,2,0,1:T(8,128)(2,1)}), bf16[1,128,1,16,2048]{4,3,2,0,1:T(8,128)(2,1)}, u32[]{:S(2)}, u32[]{:S(2)}) %all-to-all-start) | async-done | bytes 8388640 | tf_op jit(solution)/shard_map/all_to_all | solution.py:81
  113.5 11.1 %all-to-all-start.1 = ((bf16[128,4,1152]{2,1,0:T(4,128)(2,1)}), bf16[128,4,1152]{2,1,0:T(4,128)(2,1)S(1)}, u32[]{:S(2)}, u32[]{:S(2)}) async-start(bf16[128,4,1152]{2,1,0:T(4,128)(2,1)} %fusion.2), calls=%async_computation.1 | async-start | bytes 2359296 | tf_op jit(solution)/shard_map/all_to_all | solution.py:97
  125.2 0.0 copy-done.6
  125.2 0.1 select_reduce_fusion
  125.3 0.1 fusion.18
  125.4 1.6 reshape.145.live_ref
  127.0 17.9 %all-to-all-done.1 = bf16[128,4,1152]{2,1,0:T(4,128)(2,1)S(1)} async-done(((bf16[128,4,1152]{2,1,0:T(4,128)(2,1)}), bf16[128,4,1152]{2,1,0:T(4,128)(2,1)S(1)}, u32[]{:S(2)}, u32[]{:S(2)}) %all-to-all-start.1) | async-done | bytes 1179680 | tf_op jit(solution)/shard_map/all_to_all | solution.py:97
  145.0 0.5 fusion.9
  145.5 0.1 div.19
  145.6 0.8 multiply_reduce_fusion.1
  146.4 0.7 rsqrt.20
  147.1 0.1 slice_convert_fusion.1
  147.2 0.3 reshape.127
  147.5 2.0 slice_convert_fusion
  149.5 0.0 copy-start.5
  149.5 0.0 copy-start.4
  149.5 2.9 %reshape.126 = f32[512,1024]{1,0:T(8,128)} reshape(f32[128,4,1024]{2,1,0:T(4,128)} %slice_convert_fusion) | data formatting | bytes 4194304 | tf_op jit(solution)/shard_map/convert_element_type | solution.py:20
  152.4 0.0 copy-done.5
  152.4 1.1 fusion.1.bias_ref
  153.5 0.0 copy-done.4
  153.5 7.1 %multiply_convert_fusion.q_ref = bf16[512,2048]{1,0:T(8,128)(2,1)} fusion(bf16[1024,2048]{1,0:T(8,128)(2,1)} %param.15, f32[512,1024]{1,0:T(8,128)} %reshape.126, f32[512]{0:T(512)S(1)} %copy-done.4, f32[512]{0:T(512)S(1)} %div.19), kind=kOutput, calls=%fused_computation.2 | convolution fusion | flops 2154299392 | bytes 8392704 | tf_op jit(solution)/shard_map/dot_general | solution.py:21
  160.6 16.0 %shard_map.91 = f32[512,1024]{1,0:T(8,128)} custom-call(bf16[512,2048]{1,0:T(8,128)(2,1)} %multiply_convert_fusion.q_ref, bf16[2048,2048]{1,0:T(8,128)(2,1)} %bitcast.10.k_ref.v_ref, bf16[2048,2048]{1,0:T(8,128)(2,1)} %bitcast.10.k_ref.v_ref, f32[8,2048]{1,0:T(8,128)} %fusion.1.bias_ref, f32[2048,1]{1,0:T(8,128)} %reshape.145.live_ref), custom_call_target="tpu_custom_call" | custom-call | tf_op jit(solution)/shard_map/pallas_call | solution.py:52
  176.5 1.8 reduce_sum.61
  178.3 0.0 copy-start.1
  178.3 2.1 multiply_reduce_fusion
  180.4 0.0 copy-done
  180.4 0.1 copy-done.1
  180.5 2.6 %convolution_convert_fusion = bf16[512,1024]{1,0:T(8,128)(2,1)S(1)} fusion(bf16[1024,1024]{1,0:T(8,128)(2,1)S(1)} %copy-done, f32[512,1024]{1,0:T(8,128)S(1)} %copy-done.1, bf16[512,2048]{1,0:T(8,128)(2,1)} %multiply_convert_fusion.q_ref, f32[512]{0:T(512)S(1)} %add_rsqrt_fusion.1, f32[512]{0:T(512)S(1)} %broadcast_multiply_fusion.1), kind=kOutput, calls=%fused_computation.11 | convolution fusion | flops 1076887552 | bytes 6295552 | tf_op jit(solution)/shard_map/dot_general | solution.py:123
  183.1 1.2 reshape.124
  184.3 5.8 %all-to-all-start.2 = ((bf16[128,4,1024]{2,1,0:T(4,128)(2,1)}), bf16[128,4,1024]{2,1,0:T(4,128)(2,1)}, u32[]{:S(2)}, u32[]{:S(2)}) async-start(bf16[128,4,1024]{2,1,0:T(4,128)(2,1)} %reshape.124), calls=%async_computation.2 | async-start | bytes 2097152 | tf_op jit(solution)/shard_map/all_to_all | solution.py:127
  190.1 18.8 %all-to-all-done.2 = bf16[128,4,1024]{2,1,0:T(4,128)(2,1)} async-done(((bf16[128,4,1024]{2,1,0:T(4,128)(2,1)}), bf16[128,4,1024]{2,1,0:T(4,128)(2,1)}, u32[]{:S(2)}, u32[]{:S(2)}) %all-to-all-start.2) | async-done | bytes 1048608 | tf_op jit(solution)/shard_map/all_to_all | solution.py:127
  208.9 1.3 reshape.125
  210.3 2.0 gather_fusion
  212.2 2.2 %add_convert_fusion = bf16[256,1024]{1,0:T(8,128)(2,1)} fusion(bf16[256,1024]{1,0:T(8,128)(2,1)} %gather_fusion, bf16[256,1024]{1,0:T(8,128)(2,1)} %param.9), kind=kLoop, calls=%fused_computation.16 | loop fusion | flops 1048576 | bytes 1572864 | tf_op jit(solution)/shard_map/convert_element_type | solution.py:129
  (14 shorter events, 0.1 us)
Async XLA Ops:
  0.0 180.4 %copy-start = (bf16[1024,1024]{1,0:T(8,128)(2,1)S(1)}, bf16[1024,1024]{1,0:T(8,128)(2,1)}, u32[]{:S(2)}) copy-start(bf16[1024,1024]{1,0:T(8,128)(2,1)} %param.16) | copy-start | bytes 6291460
  0.0 12.0 %copy-start.3 = (s32[1,128,1,16]{1,3,2,0:T(8,128)S(1)}, s32[1,128,1,16]{1,3,2,0:T(8,128)}, u32[]{:S(2)}) copy-start(s32[1,128,1,16]{1,3,2,0:T(8,128)} %param.14) | copy-start | bytes 24580
  0.0 12.0 %copy-start.2 = (s32[256,1]{0,1:T(1,128)S(1)}, s32[256,1]{0,1:T(1,128)}, u32[]{:S(2)}) copy-start(s32[256,1]{0,1:T(1,128)} %param.10) | copy-start | bytes 3076
  0.0 113.4 %all-to-all-start = ((bf16[1,128,1,16,2048]{4,3,2,0,1:T(8,128)(2,1)}), bf16[1,128,1,16,2048]{4,3,2,0,1:T(8,128)(2,1)}, u32[]{:S(2)}, u32[]{:S(2)}) async-start(bf16[1,128,1,16,2048]{4,3,2,0,1:T(8,128)(2,1)} %bitcast.30), calls=%async_computation | async-start | bytes 16777216 | tf_op jit(solution)/shard_map/all_to_all | solution.py:81
  17.5 107.7 %copy-start.6 = (s32[1,128]{1,0:T(1,128)S(1)}, s32[1,128]{1,0:T(1,128)}, u32[]{:S(2)}) copy-start(s32[1,128]{1,0:T(1,128)} %param.12) | copy-start | bytes 1540
  113.5 31.5 %all-to-all-start.1 = ((bf16[128,4,1152]{2,1,0:T(4,128)(2,1)}), bf16[128,4,1152]{2,1,0:T(4,128)(2,1)S(1)}, u32[]{:S(2)}, u32[]{:S(2)}) async-start(bf16[128,4,1152]{2,1,0:T(4,128)(2,1)} %fusion.2), calls=%async_computation.1 | async-start | bytes 2359296 | tf_op jit(solution)/shard_map/all_to_all | solution.py:97
  149.5 2.9 %copy-start.5 = (f32[8,128]{1,0:T(8,128)S(1)}, f32[8,128]{1,0:T(8,128)}, u32[]{:S(2)}) copy-start(f32[8,128]{1,0:T(8,128)} %param.17) | copy-start | bytes 12292
  149.5 4.0 %copy-start.4 = (f32[512]{0:T(512)S(1)}, f32[512]{0:T(512)}, u32[]{:S(2)}) copy-start(f32[512]{0:T(512)} %rsqrt.20) | copy-start | bytes 6148
  178.3 2.2 %copy-start.1 = (f32[512,1024]{1,0:T(8,128)S(1)}, f32[512,1024]{1,0:T(8,128)}, u32[]{:S(2)}) copy-start(f32[512,1024]{1,0:T(8,128)} %shard_map.91) | copy-start | bytes 6291460
  184.3 24.6 %all-to-all-start.2 = ((bf16[128,4,1024]{2,1,0:T(4,128)(2,1)}), bf16[128,4,1024]{2,1,0:T(4,128)(2,1)}, u32[]{:S(2)}, u32[]{:S(2)}) async-start(bf16[128,4,1024]{2,1,0:T(4,128)(2,1)} %reshape.124), calls=%async_computation.2 | async-start | bytes 2097152 | tf_op jit(solution)/shard_map/all_to_all | solution.py:127

commit v7 on v6

--- a/solution.py
+++ b/solution.py
@@ -78,7 +78,6 @@
     block_ev = kv_store.shape[3]
     capacity = max(2, 2 * row_count // devices)
     event_count = devices * per_owner * block_ev
-    arrived = lax.all_to_all(kv_store, axes, split_axis=1, concat_axis=0, tiled=True)
 
     target = cand_req[:, 0]
     onehot = (target[:, None] == jnp.arange(devices, dtype=jnp.int32)[None, :]).astype(jnp.int32)
@@ -92,9 +91,10 @@
     bucket_send = store_bucket.reshape(devices, capacity, bucket_lanes).astype(cand_x.dtype)
     bucket_send = jnp.pad(bucket_send, ((0, 0), (0, 0), (0, 128 - bucket_lanes)))
     send = jnp.concatenate([slotted, bucket_send], axis=2)
-    arrived, send = lax.optimization_barrier((arrived, send))
+    received = lax.all_to_all(send, axes, split_axis=0, concat_axis=0, tiled=True)
+    received, kv_store = lax.optimization_barrier((received, kv_store))
+    arrived = lax.all_to_all(kv_store, axes, split_axis=1, concat_axis=0, tiled=True)
     events = arrived.reshape(event_count, 2 * features)
-    received = lax.all_to_all(send, axes, split_axis=0, concat_axis=0, tiled=True)
     senders = received.shape[0]
     flat_rows = received[:, :, :features].reshape(senders * capacity, features)
     buckets = received[:, :, features : features + bucket_lanes].astype(jnp.int32).reshape(event_count)

time: 215 us -> 208 us (0.967)
  blocking collectives: 0 us -> 31.7 us
  waiting for transfers between devices: 131 us -> 103 us
  starting transfers between devices: 28.8 us -> 17.4 us
    all_to_all x0 -> x1, blocking collectives: none -> 31.7 us  [shards(): lax.all_to_all(send, axes, split_axis=0, concat_axis=0, tiled=True)]
    all_to_all x1 -> x0, waiting for transfers between devices: 17.9 us -> none  [shards(): lax.all_to_all(send, axes, split_axis=0, concat_axis=0, tiled=True)]
    all_to_all x1 -> x0, starting transfers between devices: 11.1 us -> none  [shards(): lax.all_to_all(send, axes, split_axis=0, concat_axis=0, tiled=True)]
    all_to_all x1, waiting for transfers between devices: 94.3 us -> 84.4 us  [shards(): lax.all_to_all(kv_store, axes, split_axis=1, concat_axis=0, tiled=True)]
    all_to_all x1, starting transfers between devices: 12 us -> 6.08 us  [shards(): lax.all_to_all(kv_store, axes, split_axis=1, concat_axis=0, tiled=True)]
    all_to_all x1, starting transfers between devices: 5.77 us -> 11.4 us  [shards(): lax.all_to_all(update, axes, split_axis=0, concat_axis=0, tiled=True)]
  transfers between devices with their start and end apart: 3 -> 2, of which waited for: 3 -> 2; matrix products, arithmetic and copies ran while one was open for 4% -> 8% of each run, Pallas kernels for 0% -> 0%
where the time goes in v7:
time: 208 us; the launch traced here: 207 us
  waiting for transfers between devices  103 us (50%)
  blocking collectives  31.7 us (15%)
  starting transfers between devices  17.4 us (8%)
  Pallas kernels  16 us (8%)
  local copies, waits for them, and re-layouts  15.5 us (7%)
  other arithmetic  12 us (6%)
  matrix products  10.7 us (5%)
    all_to_all x1, waiting for transfers between devices, shards(): lax.all_to_all(kv_store, axes, split_axis=1, concat_axis=0, tiled=True)  84.4 us
    all_to_all x1, blocking collectives, shards(): lax.all_to_all(send, axes, split_axis=0, concat_axis=0, tiled=True)  31.7 us
    all_to_all x1, waiting for transfers between devices, shards(): lax.all_to_all(update, axes, split_axis=0, concat_axis=0, tiled=True)  18.7 us
    pallas_call x1, Pallas kernels, attend(): pl.pallas_call(kernel, grid=(head_count,), in_specs=[pl.BlockSpec((slot_c...  16 us
    all_to_all x1, starting transfers between devices, shards(): lax.all_to_all(update, axes, split_axis=0, concat_axis=0, tiled=True)  11.4 us
    dot_general x1, matrix products, prepare(): jnp.dot(normed, w_proj, preferred_element_type=jnp.float32)  7.09 us
    all_to_all x1, starting transfers between devices, shards(): lax.all_to_all(kv_store, axes, split_axis=1, concat_axis=0, tiled=True)  6.08 us
  transfers between devices with their start and end apart: 2, of which 2 were waited for; matrix products, arithmetic and copies ran while one was open for 8% of the time, Pallas kernels for 0%

profile of v7, /device:TPU:1, one launch (start us, length us, event | category | flops | bytes accessed | tf_op | source)
XLA Modules:
  0.0 207.2 jit_solution(3183068066490473618)
XLA Ops:
  0.0 0.0 copy-start
  0.0 0.0 copy-start.2
  0.0 0.9 copy.21
  1.0 0.2 fusion.12
  1.3 0.9 fusion.14
  2.1 0.7 compare_select_fusion
  2.8 3.2 %scatter_custom_fusion = bf16[512,1024]{1,0:T(8,128)(2,1)} fusion(s32[256]{0:T(256)S(1)} %bitcast.36, bf16[256,1024]{1,0:T(8,128)(2,1)} %param.9, bf16[]{:T(256)} %constant.10.clone.1), kind=kCustom, calls=%fused_computation.24 | custom fusion | bytes 1049088 | tf_op jit(solution)/shard_map/scatter | solution.py:88
  6.0 1.5 reshape.123
  7.4 0.0 copy-done.2
  7.5 0.2 copy.23
  7.6 0.6 fusion.2
  8.2 31.7 %all_to_all.19 = bf16[128,4,1152]{2,1,0:T(4,128)(2,1)S(1)} all-to-all(bf16[128,4,1152]{2,1,0:T(4,128)(2,1)S(1)} %fusion.2), channel_id=1, replica_groups=mesh['req'=16,'cache'=8] {'req','cache'}, dimensions={0} | all-to-all | bytes 2359296 | tf_op jit(solution)/shard_map/all_to_all | solution.py:94
  39.9 0.0 copy-start.4
  40.0 6.1 %all-to-all-start.1 = ((bf16[1,128,1,16,2048]{4,3,2,0,1:T(8,128)(2,1)}), bf16[1,128,1,16,2048]{4,3,2,0,1:T(8,128)(2,1)}, u32[]{:S(2)}, u32[]{:S(2)}) async-start(bf16[1,128,1,16,2048]{4,3,2,0,1:T(8,128)(2,1)} %bitcast.28), calls=%async_computation.1 | async-start | bytes 16777216 | tf_op jit(solution)/shard_map/all_to_all | solution.py:96
  46.7 0.0 copy-done.4
  46.7 0.1 select_reduce_fusion
  46.8 0.1 fusion.17
  46.9 1.6 reshape.146.live_ref
  48.5 0.5 convert_reduce_fusion
  49.0 0.1 div.19
  49.1 0.8 multiply_reduce_fusion.1
  50.0 0.1 rsqrt.20
  50.1 2.0 slice_convert_fusion
  52.1 0.0 copy-start.3
  52.1 2.9 %reshape.127 = f32[512,1024]{1,0:T(8,128)} reshape(f32[128,4,1024]{2,1,0:T(4,128)} %slice_convert_fusion) | data formatting | bytes 4194304 | tf_op jit(solution)/shard_map/convert_element_type | solution.py:20
  55.0 0.1 slice_convert_fusion.1
  55.1 0.3 reshape.128
  55.4 0.0 copy-done.3
  55.4 1.1 fusion.1.bias_ref
  56.4 7.1 %multiply_convert_fusion.q_ref = bf16[512,2048]{1,0:T(8,128)(2,1)} fusion(bf16[1024,2048]{1,0:T(8,128)(2,1)} %param.15, f32[512,1024]{1,0:T(8,128)} %reshape.127, f32[512]{0:T(512)S(1)} %rsqrt.20, f32[512]{0:T(512)S(1)} %div.19), kind=kOutput, calls=%fused_computation.2 | convolution fusion | flops 2154299392 | bytes 8392704 | tf_op jit(solution)/shard_map/dot_general | solution.py:21
  63.5 84.4 %all-to-all-done.1 = bf16[1,128,1,16,2048]{4,3,2,0,1:T(8,128)(2,1)} async-done(((bf16[1,128,1,16,2048]{4,3,2,0,1:T(8,128)(2,1)}), bf16[1,128,1,16,2048]{4,3,2,0,1:T(8,128)(2,1)}, u32[]{:S(2)}, u32[]{:S(2)}) %all-to-all-start.1) | async-done | bytes 8388640 | tf_op jit(solution)/shard_map/all_to_all | solution.py:96
  147.9 16.0 %shard_map.91 = f32[512,1024]{1,0:T(8,128)} custom-call(bf16[512,2048]{1,0:T(8,128)(2,1)} %multiply_convert_fusion.q_ref, bf16[2048,2048]{1,0:T(8,128)(2,1)} %bitcast.9.k_ref.v_ref, bf16[2048,2048]{1,0:T(8,128)(2,1)} %bitcast.9.k_ref.v_ref, f32[8,2048]{1,0:T(8,128)} %fusion.1.bias_ref, f32[2048,1]{1,0:T(8,128)} %reshape.146.live_ref), custom_call_target="tpu_custom_call" | custom-call | tf_op jit(solution)/shard_map/pallas_call | solution.py:52
  163.9 1.8 reduce_sum.61
  165.6 0.0 copy-start.1
  165.6 2.1 %multiply_reduce_fusion = f32[512]{0:T(512)S(1)} fusion(f32[512,1024]{1,0:T(8,128)} %shard_map.91, f32[512]{0:T(512)S(1)} %broadcast_multiply_fusion.1), kind=kLoop, calls=%fused_computation.8 | loop fusion | flops 1572352 | bytes 2101248 | tf_op jit(solution)/shard_map/reduce_sum | solution.py:15
  167.7 0.0 copy-done
  167.7 0.1 copy-done.1
  167.8 2.6 %convolution_convert_fusion = bf16[512,1024]{1,0:T(8,128)(2,1)S(1)} fusion(bf16[1024,1024]{1,0:T(8,128)(2,1)S(1)} %copy-done, f32[512,1024]{1,0:T(8,128)S(1)} %copy-done.1, bf16[512,2048]{1,0:T(8,128)(2,1)} %multiply_convert_fusion.q_ref, f32[512]{0:T(512)S(1)} %add_rsqrt_fusion.1, f32[512]{0:T(512)S(1)} %broadcast_multiply_fusion.1), kind=kOutput, calls=%fused_computation.11 | convolution fusion | flops 1076887552 | bytes 6295552 | tf_op jit(solution)/shard_map/dot_general | solution.py:123
  170.4 1.2 reshape.125
  171.7 11.4 %all-to-all-start.2 = ((bf16[128,4,1024]{2,1,0:T(4,128)(2,1)}), bf16[128,4,1024]{2,1,0:T(4,128)(2,1)}, u32[]{:S(2)}, u32[]{:S(2)}) async-start(bf16[128,4,1024]{2,1,0:T(4,128)(2,1)} %reshape.125), calls=%async_computation.2 | async-start | bytes 2097152 | tf_op jit(solution)/shard_map/all_to_all | solution.py:127
  183.1 18.7 %all-to-all-done.2 = bf16[128,4,1024]{2,1,0:T(4,128)(2,1)} async-done(((bf16[128,4,1024]{2,1,0:T(4,128)(2,1)}), bf16[128,4,1024]{2,1,0:T(4,128)(2,1)}, u32[]{:S(2)}, u32[]{:S(2)}) %all-to-all-start.2) | async-done | bytes 1048608 | tf_op jit(solution)/shard_map/all_to_all | solution.py:127
  201.7 1.3 reshape.126
  203.1 2.0 gather_fusion
  205.0 2.2 %add_convert_fusion = bf16[256,1024]{1,0:T(8,128)(2,1)} fusion(bf16[256,1024]{1,0:T(8,128)(2,1)} %gather_fusion, bf16[256,1024]{1,0:T(8,128)(2,1)} %param.9), kind=kLoop, calls=%fused_computation.16 | loop fusion | flops 1048576 | bytes 1572864 | tf_op jit(solution)/shard_map/convert_element_type | solution.py:129
  (13 shorter events, 0.1 us)
Async XLA Ops:
  0.0 167.7 %copy-start = (bf16[1024,1024]{1,0:T(8,128)(2,1)S(1)}, bf16[1024,1024]{1,0:T(8,128)(2,1)}, u32[]{:S(2)}) copy-start(bf16[1024,1024]{1,0:T(8,128)(2,1)} %param.16) | copy-start | bytes 6291460
  0.0 7.4 %copy-start.2 = (s32[1,128,1,16]{1,3,2,0:T(8,128)S(1)}, s32[1,128,1,16]{1,3,2,0:T(8,128)}, u32[]{:S(2)}) copy-start(s32[1,128,1,16]{1,3,2,0:T(8,128)} %param.14) | copy-start | bytes 24580
  39.9 6.7 %copy-start.4 = (s32[1,128]{1,0:T(1,128)S(1)}, s32[1,128]{1,0:T(1,128)}, u32[]{:S(2)}) copy-start(s32[1,128]{1,0:T(1,128)} %param.12) | copy-start | bytes 1540
  40.0 107.9 %all-to-all-start.1 = ((bf16[1,128,1,16,2048]{4,3,2,0,1:T(8,128)(2,1)}), bf16[1,128,1,16,2048]{4,3,2,0,1:T(8,128)(2,1)}, u32[]{:S(2)}, u32[]{:S(2)}) async-start(bf16[1,128,1,16,2048]{4,3,2,0,1:T(8,128)(2,1)} %bitcast.28), calls=%async_computation.1 | async-start | bytes 16777216 | tf_op jit(solution)/shard_map/all_to_all | solution.py:96
  52.1 3.3 %copy-start.3 = (f32[8,128]{1,0:T(8,128)S(1)}, f32[8,128]{1,0:T(8,128)}, u32[]{:S(2)}) copy-start(f32[8,128]{1,0:T(8,128)} %param.17) | copy-start | bytes 12292
  165.6 2.2 %copy-start.1 = (f32[512,1024]{1,0:T(8,128)S(1)}, f32[512,1024]{1,0:T(8,128)}, u32[]{:S(2)}) copy-start(f32[512,1024]{1,0:T(8,128)} %shard_map.91) | copy-start | bytes 6291460
  171.7 30.0 %all-to-all-start.2 = ((bf16[128,4,1024]{2,1,0:T(4,128)(2,1)}), bf16[128,4,1024]{2,1,0:T(4,128)(2,1)}, u32[]{:S(2)}, u32[]{:S(2)}) async-start(bf16[128,4,1024]{2,1,0:T(4,128)(2,1)} %reshape.125), calls=%async_computation.2 | async-start | bytes 2097152 | tf_op jit(solution)/shard_map/all_to_all | solution.py:127

commit v8 on v7

--- a/solution.py
+++ b/solution.py
@@ -64,6 +64,32 @@
     )(projected, events, events, half_bias, live)
 
 
+def finish_kernel(a_ref, g_ref, w_ref, o_ref):
+    attended = a_ref[...]
+    average = jnp.mean(attended, axis=-1, keepdims=True)
+    centred = attended - average
+    spread = jnp.mean(centred * centred, axis=-1, keepdims=True)
+    normal = centred * lax.rsqrt(spread + 1e-05)
+    hidden = (normal * g_ref[...].astype(jnp.float32)).astype(jnp.bfloat16)
+    o_ref[...] = jnp.dot(hidden, w_ref[...], preferred_element_type=jnp.float32).astype(o_ref.dtype)
+
+
+def finish(attended, projected, w_out):
+    slot_count, features = attended.shape
+    tile = 256 if slot_count % 256 == 0 else slot_count
+    return pl.pallas_call(
+        finish_kernel,
+        grid=(slot_count // tile,),
+        in_specs=[
+            pl.BlockSpec((tile, features), lambda i: (i, 0)),
+            pl.BlockSpec((tile, features), lambda i: (i, 0)),
+            pl.BlockSpec(w_out.shape, lambda i: (0, 0)),
+        ],
+        out_specs=pl.BlockSpec((tile, w_out.shape[1]), lambda i: (i, 0)),
+        out_shape=jax.ShapeDtypeStruct((slot_count, w_out.shape[1]), jnp.bfloat16),
+    )(attended, projected, w_out)
+
+
 def shards(
     cand_x, cand_req, hist_len, block_place, kv_store, store_bucket, w_proj, w_out, time_bias
 ):
@@ -84,8 +110,12 @@
     earlier = jnp.cumsum(onehot, axis=0) - onehot
     slot_rank = jnp.sum(earlier * onehot, axis=1)
     flat_slot = target * capacity + slot_rank
-    empty = jnp.zeros((devices * capacity, features), cand_x.dtype)
-    slotted = empty.at[flat_slot].set(cand_x).reshape(devices, capacity, features)
+    slot_ids = jnp.arange(devices * capacity, dtype=jnp.int32)
+    slot_table = (flat_slot[:, None] == slot_ids[None, :]).astype(cand_x.dtype)
+    slotted = lax.dot_general(
+        slot_table, cand_x, (((0,), (0,)), ((), ())), preferred_element_type=jnp.float32
+    )
+    slotted = slotted.astype(cand_x.dtype).reshape(devices, capacity, features)
     rows_per = per_owner * block_ev
     bucket_lanes = rows_per // capacity
     bucket_send = store_bucket.reshape(devices, capacity, bucket_lanes).astype(cand_x.dtype)
@@ -116,17 +146,13 @@
 
     projected = prepare(flat_rows, w_proj)
     slot_count = projected.shape[0]
-    gate_u = projected[:, :features]
     attended = attend(projected, events, half_bias, live, head_count, head_dim, half_scale)
-    hidden = (layer_norm(attended) * gate_u.astype(jnp.float32)).astype(jnp.bfloat16)
-    update = (
-        jnp.dot(hidden, w_out, preferred_element_type=jnp.float32)
-        .astype(jnp.bfloat16)
-        .reshape(senders, capacity, features)
+    update = finish(attended, projected, w_out).reshape(senders, capacity, features)
+    returned = lax.all_to_all(update, axes, split_axis=0, concat_axis=0, tiled=True)
+    picked = jnp.dot(
+        slot_table, returned.reshape(devices * capacity, features), preferred_element_type=jnp.float32
     )
-    returned = lax.all_to_all(update, axes, split_axis=0, concat_axis=0, tiled=True)
-    update = returned.reshape(devices * capacity, features)[flat_slot]
-    return (cand_x.astype(jnp.float32) + update.astype(jnp.float32)).astype(jnp.bfloat16)
+    return (cand_x.astype(jnp.float32) + picked).astype(jnp.bfloat16)
 
 
 def solution(mesh):

time: 208 us -> 200 us (0.962)
  blocking collectives: 31.7 us -> 61.7 us
  waiting for transfers between devices: 103 us -> 86.8 us
  starting transfers between devices: 17.4 us -> 6.07 us
  local copies, waits for them, and re-layouts: 15.5 us -> 6.99 us
  other arithmetic: 12 us -> 4.57 us
  Pallas kernels: 16 us -> 21.2 us
    all_to_all x0 -> x1, blocking collectives: none -> 29.9 us  [shards(): lax.all_to_all(update, axes, split_axis=0, concat_axis=0, tiled=True)]
    all_to_all x1 -> x0, waiting for transfers between devices: 18.7 us -> none  [shards(): lax.all_to_all(update, axes, split_axis=0, concat_axis=0, tiled=True)]
    all_to_all x1 -> x0, starting transfers between devices: 11.4 us -> none  [shards(): lax.all_to_all(update, axes, split_axis=0, concat_axis=0, tiled=True)]
    pallas_call x0 -> x1, Pallas kernels: none -> 5.21 us  [finish(): pl.pallas_call(finish_kernel, grid=(slot_count // tile,), in_specs=[pl.Bl...]
    scatter x1 -> x0, local copies, waits for them, and re-layouts: 3.16 us -> none  [shards(): empty.at[flat_slot].set(cand_x).reshape(devices, capacity, features)]
    all_to_all x1, waiting for transfers between devices: 84.4 us -> 86.8 us  [shards(): lax.all_to_all(kv_store, axes, split_axis=1, concat_axis=0, tiled=True)]
    convert_element_type x1 -> x0, other arithmetic: 2.19 us -> none  [shards(): (cand_x.astype(jnp.float32) + update.astype(jnp.float32)).astype(jnp.bflo...]
  transfers between devices with their start and end apart: 2 -> 1, of which waited for: 2 -> 1; matrix products, arithmetic and copies ran while one was open for 8% -> 7% of each run, Pallas kernels for 0% -> 0%
where the time goes in v8:
time: 200 us; the launch traced here: 199 us
  waiting for transfers between devices  86.8 us (43%)
  blocking collectives  61.7 us (31%)
  Pallas kernels  21.2 us (11%)
  matrix products  11 us (6%)
  local copies, waits for them, and re-layouts  6.99 us (3%)
  starting transfers between devices  6.07 us (3%)
  other arithmetic  4.57 us (2%)
    all_to_all x1, waiting for transfers between devices, shards(): lax.all_to_all(kv_store, axes, split_axis=1, concat_axis=0, tiled=True)  86.8 us
    all_to_all x1, blocking collectives, shards(): lax.all_to_all(send, axes, split_axis=0, concat_axis=0, tiled=True)  31.7 us
    all_to_all x1, blocking collectives, shards(): lax.all_to_all(update, axes, split_axis=0, concat_axis=0, tiled=True)  29.9 us
    pallas_call x1, Pallas kernels, attend(): pl.pallas_call(kernel, grid=(head_count,), in_specs=[pl.BlockSpec((slot_c...  16 us
    dot_general x1, matrix products, prepare(): jnp.dot(normed, w_proj, preferred_element_type=jnp.float32)  7.08 us
    all_to_all x1, starting transfers between devices, shards(): lax.all_to_all(kv_store, axes, split_axis=1, concat_axis=0, tiled=True)  6.07 us
    pallas_call x1, Pallas kernels, finish(): pl.pallas_call(finish_kernel, grid=(slot_count // tile,), in_specs=[pl.Bl...  5.21 us
  transfers between devices with their start and end apart: 1, of which 1 were waited for; matrix products, arithmetic and copies ran while one was open for 7% of the time, Pallas kernels for 0%

profile of v8, /device:TPU:1, one launch (start us, length us, event | category | flops | bytes accessed | tf_op | source)
XLA Modules:
  0.0 199.1 jit_solution(14957307631559864671)
XLA Ops:
  0.0 0.0 copy-start
  0.0 0.8 copy.21
  0.8 0.2 fusion.10
  1.1 0.0 copy-start.2
  1.1 0.9 fusion.12
  2.0 0.7 multiply_add_fusion
  2.7 1.6 convolution_convert_fusion
  4.3 0.4 reshape.111
  4.7 0.0 copy-done.2
  4.7 0.2 copy.23
  4.9 0.6 fusion.3
  5.5 31.7 %all_to_all.19 = bf16[128,4,1152]{2,1,0:T(4,128)(2,1)S(1)} all-to-all(bf16[128,4,1152]{2,1,0:T(4,128)(2,1)S(1)} %fusion.3), channel_id=1, replica_groups=mesh['req'=16,'cache'=8] {'req','cache'}, dimensions={0} | all-to-all | bytes 2359296 | tf_op jit(solution)/shard_map/all_to_all | solution.py:124
  37.2 0.0 copy-start.3
  37.2 6.1 %all-to-all-start.1 = ((bf16[1,128,1,16,2048]{4,3,2,0,1:T(8,128)(2,1)}), bf16[1,128,1,16,2048]{4,3,2,0,1:T(8,128)(2,1)}, u32[]{:S(2)}, u32[]{:S(2)}) async-start(bf16[1,128,1,16,2048]{4,3,2,0,1:T(8,128)(2,1)} %bitcast.29), calls=%async_computation.1 | async-start | bytes 16777216 | tf_op jit(solution)/shard_map/all_to_all | solution.py:126
  43.9 0.0 copy-done.3
  44.0 0.1 select_reduce_fusion
  44.1 0.1 fusion.15
  44.2 1.6 reshape.118.live_ref
  45.8 0.5 convert_reduce_fusion
  46.3 0.1 div.13
  46.4 0.8 multiply_reduce_fusion
  47.3 0.1 rsqrt.12
  47.4 0.6 slice_convert_fusion
  48.0 1.7 reshape.115
  49.7 0.1 slice_convert_fusion.1
  49.8 0.3 reshape.116
  50.0 0.0 copy-done
  50.0 1.1 fusion.1.bias_ref
  51.1 7.1 %multiply_convert_fusion.q_ref.g_ref = bf16[512,2048]{1,0:T(8,128)(2,1)} fusion(bf16[1024,2048]{1,0:T(8,128)(2,1)} %param.15, f32[512,1024]{1,0:T(8,128)} %reshape.115, f32[512]{0:T(512)S(1)} %rsqrt.12, f32[512]{0:T(512)S(1)} %div.13), kind=kOutput, calls=%fused_computation | convolution fusion | flops 2154299392 | bytes 8392704 | tf_op jit(solution)/shard_map/dot_general | solution.py:21
  58.2 86.8 %all-to-all-done.1 = bf16[1,128,1,16,2048]{4,3,2,0,1:T(8,128)(2,1)} async-done(((bf16[1,128,1,16,2048]{4,3,2,0,1:T(8,128)(2,1)}), bf16[1,128,1,16,2048]{4,3,2,0,1:T(8,128)(2,1)}, u32[]{:S(2)}, u32[]{:S(2)}) %all-to-all-start.1) | async-done | bytes 8388640 | tf_op jit(solution)/shard_map/all_to_all | solution.py:126
  144.9 16.0 %shard_map.91.a_ref = f32[512,1024]{1,0:T(8,128)} custom-call(bf16[512,2048]{1,0:T(8,128)(2,1)} %multiply_convert_fusion.q_ref.g_ref, bf16[2048,2048]{1,0:T(8,128)(2,1)} %bitcast.9.k_ref.v_ref, bf16[2048,2048]{1,0:T(8,128)(2,1)} %bitcast.9.k_ref.v_ref, f32[8,2048]{1,0:T(8,128)} %fusion.1.bias_ref, f32[2048,1]{1,0:T(8,128)} %reshape.118.live_ref), custom_call_target="tpu_custom_call" | custom-call | tf_op jit(solution)/shard_map/pallas_call | solution.py:52
  160.9 5.2 %shard_map.92 = bf16[512,1024]{1,0:T(8,128)(2,1)} custom-call(f32[512,1024]{1,0:T(8,128)} %shard_map.91.a_ref, bf16[512,2048]{1,0:T(8,128)(2,1)} %multiply_convert_fusion.q_ref.g_ref, bf16[1024,1024]{1,0:T(8,128)(2,1)} %w_ref.1), custom_call_target="tpu_custom_call" | custom-call | tf_op jit(solution)/shard_map/pallas_call | solution.py:80
  166.1 1.5 reshape.113
  167.6 0.0 copy-start.1
  167.6 29.9 %all_to_all.20 = bf16[128,4,1024]{2,1,0:T(4,128)(2,1)S(1)} all-to-all(bf16[128,4,1024]{2,1,0:T(4,128)(2,1)S(1)} %reshape.113), channel_id=1, replica_groups=mesh['req'=16,'cache'=8] {'req','cache'}, dimensions={0} | all-to-all | bytes 2097152 | tf_op jit(solution)/shard_map/all_to_all | solution.py:151
  197.5 0.3 reshape.114
  197.8 0.0 copy-done.1
  197.8 1.3 fusion.2
  (10 shorter events, 0.1 us)
Async XLA Ops:
  0.0 50.0 %copy-start = (f32[8,128]{1,0:T(8,128)S(1)}, f32[8,128]{1,0:T(8,128)}, u32[]{:S(2)}) copy-start(f32[8,128]{1,0:T(8,128)} %param.17) | copy-start | bytes 12292
  1.1 3.6 %copy-start.2 = (s32[1,128,1,16]{1,3,2,0:T(8,128)S(1)}, s32[1,128,1,16]{1,3,2,0:T(8,128)}, u32[]{:S(2)}) copy-start(s32[1,128,1,16]{1,3,2,0:T(8,128)} %param.14) | copy-start | bytes 24580
  37.2 6.7 %copy-start.3 = (s32[1,128]{1,0:T(1,128)S(1)}, s32[1,128]{1,0:T(1,128)}, u32[]{:S(2)}) copy-start(s32[1,128]{1,0:T(1,128)} %param.12) | copy-start | bytes 1540
  37.2 107.7 %all-to-all-start.1 = ((bf16[1,128,1,16,2048]{4,3,2,0,1:T(8,128)(2,1)}), bf16[1,128,1,16,2048]{4,3,2,0,1:T(8,128)(2,1)}, u32[]{:S(2)}, u32[]{:S(2)}) async-start(bf16[1,128,1,16,2048]{4,3,2,0,1:T(8,128)(2,1)} %bitcast.29), calls=%async_computation.1 | async-start | bytes 16777216 | tf_op jit(solution)/shard_map/all_to_all | solution.py:126
  167.6 30.2 %copy-start.1 = (bf16[256,1024]{1,0:T(8,128)(2,1)S(1)}, bf16[256,1024]{1,0:T(8,128)(2,1)}, u32[]{:S(2)}) copy-start(bf16[256,1024]{1,0:T(8,128)(2,1)} %param.9) | copy-start | bytes 1572868

commit v9 on v8

--- a/solution.py
+++ b/solution.py
@@ -23,8 +23,8 @@
     )
 
 
-def attend_kernel(q_ref, k_ref, v_ref, bias_ref, live_ref, o_ref, *, half_scale, chunk):
-    head = pl.program_id(0)
+def attend_kernel(q_ref, k_ref, v_ref, bias_ref, live_ref, o_ref, *, half_scale, chunk, first):
+    head = pl.program_id(0) + first
     query = q_ref[...]
     bias_row = bias_ref[pl.ds(head, 1), :]
     event_count = k_ref.shape[0]
@@ -43,29 +43,29 @@
     o_ref[...] = acc
 
 
-def attend(projected, events, half_bias, live, head_count, head_dim, half_scale):
+def attend(projected, events, half_bias, live, head_count, head_dim, half_scale, first):
     slot_count = projected.shape[0]
     event_count = events.shape[0]
-    features = head_count * head_dim
+    total_heads = half_bias.shape[0]
     chunk = 512 if event_count % 512 == 0 else event_count
-    kernel = functools.partial(attend_kernel, half_scale=half_scale, chunk=chunk)
+    kernel = functools.partial(attend_kernel, half_scale=half_scale, chunk=chunk, first=first)
     return pl.pallas_call(
         kernel,
         grid=(head_count,),
         in_specs=[
-            pl.BlockSpec((slot_count, head_dim), lambda h: (0, head_count + h)),
+            pl.BlockSpec((slot_count, head_dim), lambda h: (0, total_heads + first + h)),
             pl.BlockSpec((event_count, head_dim), lambda h: (0, h)),
             pl.BlockSpec((event_count, head_dim), lambda h: (0, head_count + h)),
             pl.BlockSpec(half_bias.shape, lambda h: (0, 0)),
             pl.BlockSpec(live.shape, lambda h: (0, 0)),
         ],
         out_specs=pl.BlockSpec((slot_count, head_dim), lambda h: (0, h)),
-        out_shape=jax.ShapeDtypeStruct((slot_count, features), jnp.float32),
+        out_shape=jax.ShapeDtypeStruct((slot_count, head_count * head_dim), jnp.float32),
     )(projected, events, events, half_bias, live)
 
 
-def finish_kernel(a_ref, g_ref, w_ref, o_ref):
-    attended = a_ref[...]
+def finish_kernel(a_ref, b_ref, g_ref, w_ref, o_ref):
+    attended = jnp.concatenate([a_ref[...], b_ref[...]], axis=1)
     average = jnp.mean(attended, axis=-1, keepdims=True)
     centred = attended - average
     spread = jnp.mean(centred * centred, axis=-1, keepdims=True)
@@ -74,20 +74,22 @@
     o_ref[...] = jnp.dot(hidden, w_ref[...], preferred_element_type=jnp.float32).astype(o_ref.dtype)
 
 
-def finish(attended, projected, w_out):
-    slot_count, features = attended.shape
+def finish(first_half, second_half, projected, w_out):
+    slot_count, half = first_half.shape
+    features = 2 * half
     tile = 256 if slot_count % 256 == 0 else slot_count
     return pl.pallas_call(
         finish_kernel,
         grid=(slot_count // tile,),
         in_specs=[
-            pl.BlockSpec((tile, features), lambda i: (i, 0)),
+            pl.BlockSpec((tile, half), lambda i: (i, 0)),
+            pl.BlockSpec((tile, half), lambda i: (i, 0)),
             pl.BlockSpec((tile, features), lambda i: (i, 0)),
             pl.BlockSpec(w_out.shape, lambda i: (0, 0)),
         ],
         out_specs=pl.BlockSpec((tile, w_out.shape[1]), lambda i: (i, 0)),
         out_shape=jax.ShapeDtypeStruct((slot_count, w_out.shape[1]), jnp.bfloat16),
-    )(attended, projected, w_out)
+    )(first_half, second_half, projected, w_out)
 
 
 def shards(
@@ -121,10 +123,21 @@
     bucket_send = store_bucket.reshape(devices, capacity, bucket_lanes).astype(cand_x.dtype)
     bucket_send = jnp.pad(bucket_send, ((0, 0), (0, 0), (0, 128 - bucket_lanes)))
     send = jnp.concatenate([slotted, bucket_send], axis=2)
+    half_heads = head_count // 2
+    split = half_heads * head_dim
+    kv_first = jnp.concatenate(
+        [kv_store[..., :split], kv_store[..., features : features + split]], axis=-1
+    )
+    kv_second = jnp.concatenate(
+        [kv_store[..., split:features], kv_store[..., features + split :]], axis=-1
+    )
+    arrived_first = lax.all_to_all(kv_first, axes, split_axis=1, concat_axis=0, tiled=True)
+    arrived_first, send = lax.optimization_barrier((arrived_first, send))
     received = lax.all_to_all(send, axes, split_axis=0, concat_axis=0, tiled=True)
-    received, kv_store = lax.optimization_barrier((received, kv_store))
-    arrived = lax.all_to_all(kv_store, axes, split_axis=1, concat_axis=0, tiled=True)
-    events = arrived.reshape(event_count, 2 * features)
+    received, kv_second = lax.optimization_barrier((received, kv_second))
+    arrived_second = lax.all_to_all(kv_second, axes, split_axis=1, concat_axis=0, tiled=True)
+    events_first = arrived_first.reshape(event_count, features)
+    events_second = arrived_second.reshape(event_count, features)
     senders = received.shape[0]
     flat_rows = received[:, :, :features].reshape(senders * capacity, features)
     buckets = received[:, :, features : features + bucket_lanes].astype(jnp.int32).reshape(event_count)
@@ -146,8 +159,14 @@
 
     projected = prepare(flat_rows, w_proj)
     slot_count = projected.shape[0]
-    attended = attend(projected, events, half_bias, live, head_count, head_dim, half_scale)
-    update = finish(attended, projected, w_out).reshape(senders, capacity, features)
+    attended_first = attend(
+        projected, events_first, half_bias, live, half_heads, head_dim, half_scale, 0
+    )
+    attended_second = attend(
+        projected, events_second, half_bias, live, half_heads, head_dim, half_scale, half_heads
+    )
+    update = finish(attended_first, attended_second, projected, w_out)
+    update = update.reshape(senders, capacity, features)
     returned = lax.all_to_all(update, axes, split_axis=0, concat_axis=0, tiled=True)
     picked = jnp.dot(
         slot_table, returned.reshape(devices * capacity, features), preferred_element_type=jnp.float32

time: 200 us -> 199 us (level)
  blocking collectives: 61.7 us -> 25.6 us
  starting transfers between devices: 6.07 us -> 22.7 us
  other arithmetic: 4.57 us -> 11.1 us
  local copies, waits for them, and re-layouts: 6.99 us -> 12.2 us
  waiting for transfers between devices: 86.8 us -> 91.9 us
  Pallas kernels: 21.2 us -> 23.8 us
    all_to_all x1 -> x0, blocking collectives: 31.7 us -> none  [shards(): lax.all_to_all(send, axes, split_axis=0, concat_axis=0, tiled=True)]
    all_to_all x1 -> x3, starting transfers between devices: 6.07 us -> 22.7 us  [the longest x1 11.9 us: shards(): lax.all_to_all(kv_first, axes, split_axis=1, concat_axis=0, tiled=True)]
    concatenate x0 -> x2, other arithmetic: none -> 6.84 us  [the longest x1 4.31 us: shards(): jnp.concatenate([kv_store[..., split:features], kv_store[..., features +...]
    all_to_all x1 -> x3, waiting for transfers between devices: 86.8 us -> 91.9 us  [the longest x1 46.8 us: shards(): lax.all_to_all(kv_first, axes, split_axis=1, concat_axis=0, tiled=True)]
    slice x0 -> x1, local copies, waits for them, and re-layouts: none -> 4.89 us  [shards(): kv_store[..., split:features]]
    all_to_all x1, blocking collectives: 29.9 us -> 25.6 us  [shards(): lax.all_to_all(update, axes, split_axis=0, concat_axis=0, tiled=True)]
    pallas_call x1 -> x2, Pallas kernels: 16 us -> 18.5 us  [attend(): pl.pallas_call(kernel, grid=(head_count,), in_specs=[pl.BlockSpec((slot_c...]
  transfers between devices with their start and end apart: 1 -> 3, of which waited for: 1 -> 3; matrix products, arithmetic and copies ran while one was open for 7% -> 12% of each run, Pallas kernels for 0% -> 5%
where the time goes in v9:
time: 199 us; the launch traced here: 198 us
  waiting for transfers between devices  91.9 us (46%)
  blocking collectives  25.6 us (13%)
  Pallas kernels  23.8 us (12%)
  starting transfers between devices  22.7 us (11%)
  local copies, waits for them, and re-layouts  12.2 us (6%)
  other arithmetic  11.1 us (6%)
  matrix products  10.3 us (5%)
    all_to_all x1, waiting for transfers between devices, shards(): lax.all_to_all(kv_first, axes, split_axis=1, concat_axis=0, tiled=True)  46.8 us
    all_to_all x1, waiting for transfers between devices, shards(): lax.all_to_all(kv_second, axes, split_axis=1, concat_axis=0, tiled=True)  28.9 us
    all_to_all x1, blocking collectives, shards(): lax.all_to_all(update, axes, split_axis=0, concat_axis=0, tiled=True)  25.6 us
    pallas_call x2, Pallas kernels, attend(): pl.pallas_call(kernel, grid=(head_count,), in_specs=[pl.BlockSpec((slot_c...  18.5 us
    all_to_all x1, waiting for transfers between devices, shards(): lax.all_to_all(send, axes, split_axis=0, concat_axis=0, tiled=True)  16.2 us
    all_to_all x1, starting transfers between devices, shards(): lax.all_to_all(kv_first, axes, split_axis=1, concat_axis=0, tiled=True)  11.9 us
    dot_general x1, matrix products, prepare(): jnp.dot(normed, w_proj, preferred_element_type=jnp.float32)  6.44 us
    all_to_all x1, starting transfers between devices, shards(): lax.all_to_all(kv_second, axes, split_axis=1, concat_axis=0, tiled=True)  5.84 us
  transfers between devices with their start and end apart: 3, of which 3 were waited for; matrix products, arithmetic and copies ran while one was open for 12% of the time, Pallas kernels for 5%

profile of v9, /device:TPU:1, one launch (start us, length us, event | category | flops | bytes accessed | tf_op | source)
XLA Modules:
  0.0 198.4 jit_solution(4046691623182492284)
XLA Ops:
  0.0 0.0 copy-start
  0.0 4.9 %fusion.16 = (bf16[1,128,1,16,512]{4,3,2,0,1:T(8,128)(2,1)S(1)}, bf16[1,128,1,16,512]{4,3,2,0,1:T(8,128)(2,1)}, bf16[1,128,1,16,512]{4,3,2,0,1:T(8,128)(2,1)S(1)}, bf16[1,128,1,16,512]{4,3,2,0,1:T(8,128)(2,1)S(1)}) fusion(bf16[1,128,1,16,2048]{4,3,2,0,1:T(8,128)(2,1)} %bitcast.34), kind=kLoop, calls=%fused_computation.42 | loop fusion | bytes 16777216 | tf_op jit(solution)/shard_map/slice | solution.py:132
  4.9 2.5 %pad_maximum_fusion = bf16[1,128,1,16,1024]{4,3,2,0,1:T(8,128)(2,1)} fusion(bf16[1,128,1,16,512]{4,3,2,0,1:T(8,128)(2,1)S(1)} %get-tuple-element.15, bf16[1,128,1,16,512]{4,3,2,0,1:T(8,128)(2,1)S(1)} %get-tuple-element.16), kind=kLoop, calls=%fused_computation | loop fusion | flops 8388608 | bytes 8388608 | tf_op jit(solution)/shard_map/concatenate | solution.py:128
  7.4 0.0 copy-start.5
  7.4 0.0 copy-start.4
  7.4 0.0 copy-start.2
  7.4 11.9 %all-to-all-start = ((bf16[1,128,1,16,1024]{4,3,2,0,1:T(8,128)(2,1)}), bf16[1,128,1,16,1024]{4,3,2,0,1:T(8,128)(2,1)}, u32[]{:S(2)}, u32[]{:S(2)}) async-start(bf16[1,128,1,16,1024]{4,3,2,0,1:T(8,128)(2,1)} %pad_maximum_fusion), calls=%async_computation | async-start | bytes 8388608 | tf_op jit(solution)/shard_map/all_to_all | solution.py:134
  19.4 0.0 copy-done.5
  19.4 0.2 copy.30
  19.6 0.0 copy-done.4
  19.6 0.1 copy.26
  19.7 0.2 fusion.10
  20.0 0.2 fusion.12
  20.2 0.0 copy-done.2
  20.2 1.5 convolution_convert_fusion
  21.8 1.5 reshape.117
  23.2 1.6 fusion.3
  24.8 46.8 %all-to-all-done = bf16[1,128,1,16,1024]{4,3,2,0,1:T(8,128)(2,1)} async-done(((bf16[1,128,1,16,1024]{4,3,2,0,1:T(8,128)(2,1)}), bf16[1,128,1,16,1024]{4,3,2,0,1:T(8,128)(2,1)}, u32[]{:S(2)}, u32[]{:S(2)}) %all-to-all-start) | async-done | bytes 4194336 | tf_op jit(solution)/shard_map/all_to_all | solution.py:134
  71.6 4.9 %all-to-all-start.1 = ((bf16[128,4,1152]{2,1,0:T(4,128)(2,1)}), bf16[128,4,1152]{2,1,0:T(4,128)(2,1)S(1)}, u32[]{:S(2)}, u32[]{:S(2)}) async-start(bf16[128,4,1152]{2,1,0:T(4,128)(2,1)} %fusion.3), calls=%async_computation.1 | async-start | bytes 2359296 | tf_op jit(solution)/shard_map/all_to_all | solution.py:136
  76.5 4.3 %pad_maximum_fusion.1 = bf16[1,128,1,16,1024]{4,3,2,0,1:T(8,128)(2,1)} fusion(bf16[1,128,1,16,512]{4,3,2,0,1:T(8,128)(2,1)} %get-tuple-element.14, bf16[1,128,1,16,512]{4,3,2,0,1:T(8,128)(2,1)S(1)} %get-tuple-element.13), kind=kLoop, calls=%fused_computation.1 | loop fusion | flops 8388608 | bytes 8388608 | tf_op jit(solution)/shard_map/concatenate | solution.py:131
  80.8 16.2 %all-to-all-done.1 = bf16[128,4,1152]{2,1,0:T(4,128)(2,1)S(1)} async-done(((bf16[128,4,1152]{2,1,0:T(4,128)(2,1)}), bf16[128,4,1152]{2,1,0:T(4,128)(2,1)S(1)}, u32[]{:S(2)}, u32[]{:S(2)}) %all-to-all-start.1) | async-done | bytes 1179680 | tf_op jit(solution)/shard_map/all_to_all | solution.py:136
  97.0 5.8 %all-to-all-start.2 = ((bf16[1,128,1,16,1024]{4,3,2,0,1:T(8,128)(2,1)}), bf16[1,128,1,16,1024]{4,3,2,0,1:T(8,128)(2,1)}, u32[]{:S(2)}, u32[]{:S(2)}) async-start(bf16[1,128,1,16,1024]{4,3,2,0,1:T(8,128)(2,1)} %pad_maximum_fusion.1), calls=%async_computation.2 | async-start | bytes 8388608 | tf_op jit(solution)/shard_map/all_to_all | solution.py:138
  103.5 0.0 copy-done.6
  103.5 0.1 select_reduce_fusion
  103.6 0.1 fusion.15
  103.7 1.6 reshape.125.live_ref
  105.3 0.6 slice_convert_fusion
  105.9 1.7 reshape.122
  107.7 0.5 convert_reduce_fusion
  108.1 0.1 div.13
  108.3 0.8 multiply_reduce_fusion
  109.1 0.1 rsqrt.12
  109.2 0.1 slice_convert_fusion.1
  109.3 0.3 reshape.123
  109.5 0.0 copy-done
  109.5 1.1 fusion.1.bias_ref
  110.6 0.0 copy-done.1
  110.6 6.4 %multiply_convert_fusion.q_ref.g_ref = bf16[512,2048]{1,0:T(8,128)(2,1)} fusion(bf16[1024,2048]{1,0:T(8,128)(2,1)} %param.15, f32[512,1024]{1,0:T(8,128)S(1)} %copy-done.1, f32[512]{0:T(512)S(1)} %rsqrt.12, f32[512]{0:T(512)S(1)} %div.13), kind=kOutput, calls=%fused_computation.2 | convolution fusion | flops 2154299392 | bytes 8392704 | tf_op jit(solution)/shard_map/dot_general | solution.py:21
  117.1 9.3 %shard_map.91.a_ref = f32[512,512]{1,0:T(8,128)} custom-call(bf16[512,2048]{1,0:T(8,128)(2,1)} %multiply_convert_fusion.q_ref.g_ref, bf16[2048,1024]{1,0:T(8,128)(2,1)} %bitcast.13.k_ref.v_ref, bf16[2048,1024]{1,0:T(8,128)(2,1)} %bitcast.13.k_ref.v_ref, f32[8,2048]{1,0:T(8,128)} %fusion.1.bias_ref, f32[2048,1]{1,0:T(8,128)} %reshape.125.live_ref), custom_call_target="tpu_custom_call" | custom-call | tf_op jit(solution)/shard_map/pallas_call | solution.py:52
  126.3 28.9 %all-to-all-done.2 = bf16[1,128,1,16,1024]{4,3,2,0,1:T(8,128)(2,1)} async-done(((bf16[1,128,1,16,1024]{4,3,2,0,1:T(8,128)(2,1)}), bf16[1,128,1,16,1024]{4,3,2,0,1:T(8,128)(2,1)}, u32[]{:S(2)}, u32[]{:S(2)}) %all-to-all-start.2) | async-done | bytes 4194336 | tf_op jit(solution)/shard_map/all_to_all | solution.py:138
  155.2 9.3 %shard_map.92.b_ref = f32[512,512]{1,0:T(8,128)} custom-call(bf16[512,2048]{1,0:T(8,128)(2,1)} %multiply_convert_fusion.q_ref.g_ref, bf16[2048,1024]{1,0:T(8,128)(2,1)} %bitcast.17.k_ref.v_ref, bf16[2048,1024]{1,0:T(8,128)(2,1)} %bitcast.17.k_ref.v_ref, f32[8,2048]{1,0:T(8,128)} %fusion.1.bias_ref, f32[2048,1]{1,0:T(8,128)} %reshape.125.live_ref), custom_call_target="tpu_custom_call" | custom-call | tf_op jit(solution)/shard_map/pallas_call | solution.py:52
  164.5 5.2 %shard_map.93 = bf16[512,1024]{1,0:T(8,128)(2,1)} custom-call(f32[512,512]{1,0:T(8,128)} %shard_map.91.a_ref, f32[512,512]{1,0:T(8,128)} %shard_map.92.b_ref, bf16[512,2048]{1,0:T(8,128)(2,1)} %multiply_convert_fusion.q_ref.g_ref, bf16[1024,1024]{1,0:T(8,128)(2,1)} %w_ref.1), custom_call_target="tpu_custom_call" | custom-call | tf_op jit(solution)/shard_map/pallas_call | solution.py:81
  169.7 1.5 reshape.120
  171.2 0.0 copy-start.3
  171.2 25.6 %all_to_all.31 = bf16[128,4,1024]{2,1,0:T(4,128)(2,1)S(1)} all-to-all(bf16[128,4,1024]{2,1,0:T(4,128)(2,1)S(1)} %reshape.120), channel_id=1, replica_groups=mesh['req'=16,'cache'=8] {'req','cache'}, dimensions={0} | all-to-all | bytes 2097152 | tf_op jit(solution)/shard_map/all_to_all | solution.py:170
  196.8 0.3 reshape.121
  197.1 0.0 copy-done.3
  197.1 1.3 fusion.2
  (13 shorter events, 0.1 us)
Async XLA Ops:
  0.0 109.5 %copy-start = (f32[8,128]{1,0:T(8,128)S(1)}, f32[8,128]{1,0:T(8,128)}, u32[]{:S(2)}) copy-start(f32[8,128]{1,0:T(8,128)} %param.17) | copy-start | bytes 12292
  7.4 12.0 %copy-start.5 = (s32[1,128,1,16]{1,3,2,0:T(8,128)S(1)}, s32[1,128,1,16]{1,3,2,0:T(8,128)}, u32[]{:S(2)}) copy-start(s32[1,128,1,16]{1,3,2,0:T(8,128)} %param.14) | copy-start | bytes 24580
  7.4 12.2 %copy-start.4 = (s32[256,1]{0,1:T(1,128)S(1)}, s32[256,1]{0,1:T(1,128)}, u32[]{:S(2)}) copy-start(s32[256,1]{0,1:T(1,128)} %param.10) | copy-start | bytes 3076
  7.4 12.8 %copy-start.2 = (bf16[256,1024]{1,0:T(8,128)(2,1)S(1)}, bf16[256,1024]{1,0:T(8,128)(2,1)}, u32[]{:S(2)}) copy-start(bf16[256,1024]{1,0:T(8,128)(2,1)} %param.9) | copy-start | bytes 1572868
  7.4 64.2 %all-to-all-start = ((bf16[1,128,1,16,1024]{4,3,2,0,1:T(8,128)(2,1)}), bf16[1,128,1,16,1024]{4,3,2,0,1:T(8,128)(2,1)}, u32[]{:S(2)}, u32[]{:S(2)}) async-start(bf16[1,128,1,16,1024]{4,3,2,0,1:T(8,128)(2,1)} %pad_maximum_fusion), calls=%async_computation | async-start | bytes 8388608 | tf_op jit(solution)/shard_map/all_to_all | solution.py:134
  71.6 25.4 %all-to-all-start.1 = ((bf16[128,4,1152]{2,1,0:T(4,128)(2,1)}), bf16[128,4,1152]{2,1,0:T(4,128)(2,1)S(1)}, u32[]{:S(2)}, u32[]{:S(2)}) async-start(bf16[128,4,1152]{2,1,0:T(4,128)(2,1)} %fusion.3), calls=%async_computation.1 | async-start | bytes 2359296 | tf_op jit(solution)/shard_map/all_to_all | solution.py:136
  80.8 22.7 %copy-start.6 = (s32[1,128]{1,0:T(1,128)S(1)}, s32[1,128]{1,0:T(1,128)}, u32[]{:S(2)}) copy-start(s32[1,128]{1,0:T(1,128)} %param.12) | copy-start | bytes 1540
  97.0 58.2 %all-to-all-start.2 = ((bf16[1,128,1,16,1024]{4,3,2,0,1:T(8,128)(2,1)}), bf16[1,128,1,16,1024]{4,3,2,0,1:T(8,128)(2,1)}, u32[]{:S(2)}, u32[]{:S(2)}) async-start(bf16[1,128,1,16,1024]{4,3,2,0,1:T(8,128)(2,1)} %pad_maximum_fusion.1), calls=%async_computation.2 | async-start | bytes 8388608 | tf_op jit(solution)/shard_map/all_to_all | solution.py:138
  107.7 3.0 %copy-start.1 = (f32[512,1024]{1,0:T(8,128)S(1)}, f32[512,1024]{1,0:T(8,128)}, u32[]{:S(2)}) copy-start(f32[512,1024]{1,0:T(8,128)} %reshape.122) | copy-start | bytes 6291460
  171.2 25.9 %copy-start.3 = (bf16[256,1024]{1,0:T(8,128)(2,1)S(1)}, bf16[256,1024]{1,0:T(8,128)(2,1)}, u32[]{:S(2)}) copy-start(bf16[256,1024]{1,0:T(8,128)(2,1)} %param.9) | copy-start | bytes 1572868

commit v10 on v9

--- a/solution.py
+++ b/solution.py
@@ -119,28 +119,31 @@
     )
     slotted = slotted.astype(cand_x.dtype).reshape(devices, capacity, features)
     rows_per = per_owner * block_ev
-    bucket_lanes = rows_per // capacity
-    bucket_send = store_bucket.reshape(devices, capacity, bucket_lanes).astype(cand_x.dtype)
-    bucket_send = jnp.pad(bucket_send, ((0, 0), (0, 0), (0, 128 - bucket_lanes)))
-    send = jnp.concatenate([slotted, bucket_send], axis=2)
     half_heads = head_count // 2
     split = half_heads * head_dim
     kv_first = jnp.concatenate(
         [kv_store[..., :split], kv_store[..., features : features + split]], axis=-1
-    )
+    ).reshape(devices, rows_per, 2 * split)
     kv_second = jnp.concatenate(
         [kv_store[..., split:features], kv_store[..., features + split :]], axis=-1
     )
-    arrived_first = lax.all_to_all(kv_first, axes, split_axis=1, concat_axis=0, tiled=True)
-    arrived_first, send = lax.optimization_barrier((arrived_first, send))
+    query_width = capacity * features // rows_per
+    bucket_send = store_bucket.reshape(devices, rows_per, 1).astype(cand_x.dtype)
+    bucket_send = jnp.pad(bucket_send, ((0, 0), (0, 0), (0, 127)))
+    send = jnp.concatenate(
+        [kv_first, slotted.reshape(devices, rows_per, query_width), bucket_send], axis=2
+    )
     received = lax.all_to_all(send, axes, split_axis=0, concat_axis=0, tiled=True)
     received, kv_second = lax.optimization_barrier((received, kv_second))
     arrived_second = lax.all_to_all(kv_second, axes, split_axis=1, concat_axis=0, tiled=True)
-    events_first = arrived_first.reshape(event_count, features)
+    senders = received.shape[0]
+    width = received.shape[2]
+    events_first = received.reshape(event_count, width)
     events_second = arrived_second.reshape(event_count, features)
-    senders = received.shape[0]
-    flat_rows = received[:, :, :features].reshape(senders * capacity, features)
-    buckets = received[:, :, features : features + bucket_lanes].astype(jnp.int32).reshape(event_count)
+    flat_rows = received[:, :, 2 * split : 2 * split + query_width].reshape(
+        senders * capacity, features
+    )
+    buckets = received[:, :, 2 * split + query_width].astype(jnp.int32).reshape(event_count)
 
     places = block_place[0]
     block_count = places.shape[0]

time: 199 us -> 201 us (1.010)
  other arithmetic: 11.1 us -> 18.4 us
  waiting for transfers between devices: 91.9 us -> 86.8 us
  local copies, waits for them, and re-layouts: 12.2 us -> 15.1 us
    all_to_all x1, waiting for transfers between devices: 16.2 us -> 65.2 us  [shards(): lax.all_to_all(send, axes, split_axis=0, concat_axis=0, tiled=True)]
    all_to_all x1 -> x0, waiting for transfers between devices: 46.8 us -> none  [shards(): lax.all_to_all(kv_first, axes, split_axis=1, concat_axis=0, tiled=True)]
    all_to_all x1 -> x0, starting transfers between devices: 11.9 us -> none  [shards(): lax.all_to_all(kv_first, axes, split_axis=1, concat_axis=0, tiled=True)]
    all_to_all x1, waiting for transfers between devices: 28.9 us -> 21.5 us  [shards(): lax.all_to_all(kv_second, axes, split_axis=1, concat_axis=0, tiled=True)]
    all_to_all x1, starting transfers between devices: 4.9 us -> 11.9 us  [shards(): lax.all_to_all(send, axes, split_axis=0, concat_axis=0, tiled=True)]
    slice x0 -> x1, local copies, waits for them, and re-layouts: none -> 4.04 us  [shards(): kv_store[..., :split]]
    all_to_all x1, starting transfers between devices: 5.84 us -> 9.26 us  [shards(): lax.all_to_all(kv_second, axes, split_axis=1, concat_axis=0, tiled=True)]
    convert_element_type x1 -> x2, other arithmetic: 0.01 us -> 3.28 us  [the longest x1 3.28 us: shards(): received[:, :, 2 * split + query_width].astype(jnp.int32)]
  transfers between devices with their start and end apart: 3 -> 2, of which waited for: 3 -> 2; matrix products, arithmetic and copies ran while one was open for 12% -> 13% of each run, Pallas kernels for 5% -> 5%
where the time goes in v10:
time: 201 us
  waiting for transfers between devices  86.8 us (43%)
  Pallas kernels  23.8 us (12%)
  blocking collectives  23.7 us (12%)
  starting transfers between devices  21.1 us (10%)
  other arithmetic  18.4 us (9%)
  local copies, waits for them, and re-layouts  15.1 us (8%)
  matrix products  10.9 us (5%)
    all_to_all x1, waiting for transfers between devices, shards(): lax.all_to_all(send, axes, split_axis=0, concat_axis=0, tiled=True)  65.2 us
    all_to_all x1, blocking collectives, shards(): lax.all_to_all(update, axes, split_axis=0, concat_axis=0, tiled=True)  23.7 us
    all_to_all x1, waiting for transfers between devices, shards(): lax.all_to_all(kv_second, axes, split_axis=1, concat_axis=0, tiled=True)  21.5 us
    pallas_call x2, Pallas kernels, attend(): pl.pallas_call(kernel, grid=(head_count,), in_specs=[pl.BlockSpec((slot_c...  18.6 us
    all_to_all x1, starting transfers between devices, shards(): lax.all_to_all(send, axes, split_axis=0, concat_axis=0, tiled=True)  11.9 us
    all_to_all x1, starting transfers between devices, shards(): lax.all_to_all(kv_second, axes, split_axis=1, concat_axis=0, tiled=True)  9.26 us
    dot_general x1, matrix products, prepare(): jnp.dot(normed, w_proj, preferred_element_type=jnp.float32)  7 us
    pallas_call x1, Pallas kernels, finish(): pl.pallas_call(finish_kernel, grid=(slot_count // tile,), in_specs=[pl.Bl...  5.25 us
  transfers between devices with their start and end apart: 2, of which 2 were waited for; matrix products, arithmetic and copies ran while one was open for 13% of the time, Pallas kernels for 5%

profile of v10, /device:TPU:1, one launch (start us, length us, event | category | flops | bytes accessed | tf_op | source)
XLA Modules:
  0.0 200.8 jit_solution(2192928538299974251)
XLA Ops:
  0.0 0.0 copy-start
  0.0 0.8 copy.28
  0.8 0.2 fusion.10
  1.1 0.9 fusion.12
  2.0 0.7 multiply_add_fusion
  2.7 1.6 convolution_convert_fusion
  4.3 0.7 reshape_reshape.3
  4.9 0.0 copy-start.3
  4.9 4.0 %fusion.17 = (bf16[1,128,1,16,512]{4,3,2,1,0:T(8,128)(2,1)S(1)}, bf16[1,128,1,16,512]{4,3,2,1,0:T(8,128)(2,1)}) fusion(bf16[1,128,1,16,2048]{4,3,2,1,0:T(8,128)(2,1)} %param.13), kind=kLoop, calls=%fused_computation.44 | loop fusion | bytes 8388608 | tf_op jit(solution)/shard_map/slice | solution.py:125
  9.0 0.0 copy-done.3
  9.0 1.2 copy.37
  10.2 2.4 %maximum_bitcast_fusion = bf16[128,16,1024]{2,1,0:T(8,128)(2,1)S(1)} fusion(bf16[1,128,1,16,512]{4,3,2,1,0:T(8,128)(2,1)} %get-tuple-element.12, bf16[1,128,1,16,512]{4,3,2,1,0:T(8,128)(2,1)S(1)} %get-tuple-element.11), kind=kLoop, calls=%fused_computation.3 | loop fusion | flops 8388608 | bytes 8388608 | tf_op jit(solution)/shard_map/reshape | solution.py:126
  12.6 0.0 copy-done.1
  12.6 2.9 %fusion.1 = bf16[128,16,1408]{2,1,0:T(8,128)(2,1)} fusion(bf16[128,16,1]{2,1,0:T(8,128)(2,1)S(1)} %copy-done.1, bf16[128,16,256]{2,1,0:T(8,128)(2,1)S(1)} %reshape_reshape.3, bf16[128,16,1024]{2,1,0:T(8,128)(2,1)S(1)} %maximum_bitcast_fusion), kind=kLoop, calls=%fused_computation.2 | loop fusion | flops 23068672 | bytes 11014144 | tf_op jit(solution)/shard_map/concatenate | solution.py:133
  15.6 11.9 %all-to-all-start = ((bf16[128,16,1408]{2,1,0:T(8,128)(2,1)}), bf16[128,16,1408]{2,1,0:T(8,128)(2,1)}, u32[]{:S(2)}, u32[]{:S(2)}) async-start(bf16[128,16,1408]{2,1,0:T(8,128)(2,1)} %fusion.1), calls=%async_computation | async-start | bytes 11534336 | tf_op jit(solution)/shard_map/all_to_all | solution.py:136
  27.5 2.7 %fusion.16 = (bf16[1,128,1,16,512]{4,3,2,0,1:T(8,128)(2,1)S(1)}, bf16[1,128,1,16,512]{4,3,2,0,1:T(8,128)(2,1)S(1)}) fusion(bf16[1,128,1,16,2048]{4,3,2,0,1:T(8,128)(2,1)} %bitcast.35), kind=kLoop, calls=%fused_computation.43 | loop fusion | bytes 8388608 | tf_op jit(solution)/shard_map/slice | solution.py:128
  30.1 2.6 %pad_maximum_fusion = bf16[1,128,1,16,1024]{4,3,2,0,1:T(8,128)(2,1)} fusion(bf16[1,128,1,16,512]{4,3,2,0,1:T(8,128)(2,1)S(1)} %get-tuple-element.10, bf16[1,128,1,16,512]{4,3,2,0,1:T(8,128)(2,1)S(1)} %get-tuple-element.9), kind=kLoop, calls=%fused_computation.4 | loop fusion | flops 8388608 | bytes 8388608 | tf_op jit(solution)/shard_map/concatenate | solution.py:127
  32.7 65.2 %all-to-all-done = bf16[128,16,1408]{2,1,0:T(8,128)(2,1)} async-done(((bf16[128,16,1408]{2,1,0:T(8,128)(2,1)}), bf16[128,16,1408]{2,1,0:T(8,128)(2,1)}, u32[]{:S(2)}, u32[]{:S(2)}) %all-to-all-start) | async-done | bytes 5767200 | tf_op jit(solution)/shard_map/all_to_all | solution.py:136
  98.0 9.3 %all-to-all-start.1 = ((bf16[1,128,1,16,1024]{4,3,2,0,1:T(8,128)(2,1)}), bf16[1,128,1,16,1024]{4,3,2,0,1:T(8,128)(2,1)}, u32[]{:S(2)}, u32[]{:S(2)}) async-start(bf16[1,128,1,16,1024]{4,3,2,0,1:T(8,128)(2,1)} %pad_maximum_fusion), calls=%async_computation.1 | async-start | bytes 8388608 | tf_op jit(solution)/shard_map/all_to_all | solution.py:138
  107.9 0.0 copy-done.4
  107.9 0.1 select_reduce_fusion
  108.0 0.1 fusion.15
  108.1 1.6 reshape.128.live_ref
  109.7 1.6 convert_reduce_fusion.1
  111.2 0.1 reduce_sum.55
  111.4 0.1 reduce_sum.56
  111.5 0.1 div.13
  111.6 0.1 copy.33
  111.7 0.1 copy.34
  111.8 1.9 multiply_reduce_fusion
  113.7 0.1 reduce_sum.58
  113.8 0.1 reduce_sum.59
  114.0 1.5 slice_convert_fusion
  115.5 1.7 reshape.125
  117.1 3.3 %convert_reduce_fusion = s32[128,16]{1,0:T(8,128)S(1)} fusion(bf16[128,16,1408]{2,1,0:T(8,128)(2,1)} %all-to-all-done), kind=kLoop, calls=%fused_computation.14 | loop fusion | flops 2048 | bytes 12288 | tf_op jit(solution)/shard_map/convert_element_type | solution.py:146
  120.4 0.1 reshape.126
  120.5 0.0 copy-done
  120.5 1.1 fusion.2.bias_ref
  121.6 7.0 %multiply_convert_fusion.q_ref.g_ref = bf16[512,2048]{1,0:T(8,128)(2,1)} fusion(bf16[1024,2048]{1,0:T(8,128)(2,1)} %param.15, f32[512,1024]{1,0:T(8,128)} %reshape.125, f32[512]{0:T(512)S(1)} %add_rsqrt_fusion, f32[512]{0:T(512)S(1)} %broadcast_multiply_fusion), kind=kOutput, calls=%fused_computation.5 | convolution fusion | flops 2154299392 | bytes 8392704 | tf_op jit(solution)/shard_map/dot_general | solution.py:21
  128.6 9.3 %shard_map.91.a_ref = f32[512,512]{1,0:T(8,128)} custom-call(bf16[512,2048]{1,0:T(8,128)(2,1)} %multiply_convert_fusion.q_ref.g_ref, bf16[2048,1408]{1,0:T(8,128)(2,1)} %bitcast.12.k_ref.v_ref, bf16[2048,1408]{1,0:T(8,128)(2,1)} %bitcast.12.k_ref.v_ref, f32[8,2048]{1,0:T(8,128)} %fusion.2.bias_ref, f32[2048,1]{1,0:T(8,128)} %reshape.128.live_ref), custom_call_target="tpu_custom_call" | custom-call | tf_op jit(solution)/shard_map/pallas_call | solution.py:52
  137.9 21.5 %all-to-all-done.1 = bf16[1,128,1,16,1024]{4,3,2,0,1:T(8,128)(2,1)} async-done(((bf16[1,128,1,16,1024]{4,3,2,0,1:T(8,128)(2,1)}), bf16[1,128,1,16,1024]{4,3,2,0,1:T(8,128)(2,1)}, u32[]{:S(2)}, u32[]{:S(2)}) %all-to-all-start.1) | async-done | bytes 4194336 | tf_op jit(solution)/shard_map/all_to_all | solution.py:138
  159.4 9.3 %shard_map.92.b_ref = f32[512,512]{1,0:T(8,128)} custom-call(bf16[512,2048]{1,0:T(8,128)(2,1)} %multiply_convert_fusion.q_ref.g_ref, bf16[2048,1024]{1,0:T(8,128)(2,1)} %bitcast.16.k_ref.v_ref, bf16[2048,1024]{1,0:T(8,128)(2,1)} %bitcast.16.k_ref.v_ref, f32[8,2048]{1,0:T(8,128)} %fusion.2.bias_ref, f32[2048,1]{1,0:T(8,128)} %reshape.128.live_ref), custom_call_target="tpu_custom_call" | custom-call | tf_op jit(solution)/shard_map/pallas_call | solution.py:52
  168.7 5.3 %shard_map.93 = bf16[512,1024]{1,0:T(8,128)(2,1)} custom-call(f32[512,512]{1,0:T(8,128)} %shard_map.91.a_ref, f32[512,512]{1,0:T(8,128)} %shard_map.92.b_ref, bf16[512,2048]{1,0:T(8,128)(2,1)} %multiply_convert_fusion.q_ref.g_ref, bf16[1024,1024]{1,0:T(8,128)(2,1)} %w_ref.1), custom_call_target="tpu_custom_call" | custom-call | tf_op jit(solution)/shard_map/pallas_call | solution.py:81
  174.0 1.5 reshape.123
  175.5 23.7 %all_to_all.19 = bf16[128,4,1024]{2,1,0:T(4,128)(2,1)S(1)} all-to-all(bf16[128,4,1024]{2,1,0:T(4,128)(2,1)S(1)} %reshape.123), channel_id=1, replica_groups=mesh['req'=16,'cache'=8] {'req','cache'}, dimensions={0} | all-to-all | bytes 2097152 | tf_op jit(solution)/shard_map/all_to_all | solution.py:173
  199.2 0.3 reshape.124
  199.5 0.0 copy-done.2
  199.5 1.3 fusion.3
  (14 shorter events, 0.1 us)
Async XLA Ops:
  0.0 120.5 %copy-start = (f32[8,128]{1,0:T(8,128)S(1)}, f32[8,128]{1,0:T(8,128)}, u32[]{:S(2)}) copy-start(f32[8,128]{1,0:T(8,128)} %param.17) | copy-start | bytes 12292
  4.9 4.0 %copy-start.3 = (s32[1,128,1,16]{1,3,2,0:T(8,128)S(1)}, s32[1,128,1,16]{1,3,2,0:T(8,128)}, u32[]{:S(2)}) copy-start(s32[1,128,1,16]{1,3,2,0:T(8,128)} %param.14) | copy-start | bytes 24580
  10.2 2.4 %copy-start.1 = (bf16[128,16,1]{2,1,0:T(8,128)(2,1)S(1)}, bf16[128,16,1]{2,1,0:T(8,128)(2,1)}, u32[]{:S(2)}) copy-start(bf16[128,16,1]{2,1,0:T(8,128)(2,1)} %copy.37) | copy-start | bytes 12292
  15.6 82.4 %all-to-all-start = ((bf16[128,16,1408]{2,1,0:T(8,128)(2,1)}), bf16[128,16,1408]{2,1,0:T(8,128)(2,1)}, u32[]{:S(2)}, u32[]{:S(2)}) async-start(bf16[128,16,1408]{2,1,0:T(8,128)(2,1)} %fusion.1), calls=%async_computation | async-start | bytes 11534336 | tf_op jit(solution)/shard_map/all_to_all | solution.py:136
  32.7 75.1 %copy-start.4 = (s32[1,128]{1,0:T(1,128)S(1)}, s32[1,128]{1,0:T(1,128)}, u32[]{:S(2)}) copy-start(s32[1,128]{1,0:T(1,128)} %param.12) | copy-start | bytes 1540
  98.0 61.5 %all-to-all-start.1 = ((bf16[1,128,1,16,1024]{4,3,2,0,1:T(8,128)(2,1)}), bf16[1,128,1,16,1024]{4,3,2,0,1:T(8,128)(2,1)}, u32[]{:S(2)}, u32[]{:S(2)}) async-start(bf16[1,128,1,16,1024]{4,3,2,0,1:T(8,128)(2,1)} %pad_maximum_fusion), calls=%async_computation.1 | async-start | bytes 8388608 | tf_op jit(solution)/shard_map/all_to_all | solution.py:138
  174.0 25.5 %copy-start.2 = (bf16[256,1024]{1,0:T(8,128)(2,1)S(1)}, bf16[256,1024]{1,0:T(8,128)(2,1)}, u32[]{:S(2)}) copy-start(bf16[256,1024]{1,0:T(8,128)(2,1)} %param.9) | copy-start | bytes 1572868

commit v11 on v9

--- a/solution.py
+++ b/solution.py
@@ -131,10 +131,10 @@
     kv_second = jnp.concatenate(
         [kv_store[..., split:features], kv_store[..., features + split :]], axis=-1
     )
+    received = lax.all_to_all(send, axes, split_axis=0, concat_axis=0, tiled=True)
+    received, kv_first = lax.optimization_barrier((received, kv_first))
     arrived_first = lax.all_to_all(kv_first, axes, split_axis=1, concat_axis=0, tiled=True)
-    arrived_first, send = lax.optimization_barrier((arrived_first, send))
-    received = lax.all_to_all(send, axes, split_axis=0, concat_axis=0, tiled=True)
-    received, kv_second = lax.optimization_barrier((received, kv_second))
+    arrived_first, kv_second = lax.optimization_barrier((arrived_first, kv_second))
     arrived_second = lax.all_to_all(kv_second, axes, split_axis=1, concat_axis=0, tiled=True)
     events_first = arrived_first.reshape(event_count, features)
     events_second = arrived_second.reshape(event_count, features)

time: 199 us -> 199 us (level)
  waiting for transfers between devices: 91.9 us -> 89.2 us
  other arithmetic: 11.1 us -> 13.1 us
    all_to_all x1, starting transfers between devices: 4.9 us -> 11.5 us  [shards(): lax.all_to_all(send, axes, split_axis=0, concat_axis=0, tiled=True)]
    all_to_all x1, starting transfers between devices: 11.9 us -> 5.83 us  [shards(): lax.all_to_all(kv_first, axes, split_axis=1, concat_axis=0, tiled=True)]
    all_to_all x1, waiting for transfers between devices: 16.2 us -> 13 us  [shards(): lax.all_to_all(send, axes, split_axis=0, concat_axis=0, tiled=True)]
  transfers between devices with their start and end apart: 3 -> 3, of which waited for: 3 -> 3; matrix products, arithmetic and copies ran while one was open for 12% -> 13% of each run, Pallas kernels for 5% -> 5%
where the time goes in v11:
time: 199 us; the launch traced here: 198 us
  waiting for transfers between devices  89.2 us (45%)
  starting transfers between devices  24.6 us (12%)
  Pallas kernels  23.8 us (12%)
  blocking collectives  23.7 us (12%)
  other arithmetic  13.1 us (7%)
  local copies, waits for them, and re-layouts  11.8 us (6%)
  matrix products  11 us (6%)
    all_to_all x1, waiting for transfers between devices, shards(): lax.all_to_all(kv_first, axes, split_axis=1, concat_axis=0, tiled=True)  48.1 us
    all_to_all x1, waiting for transfers between devices, shards(): lax.all_to_all(kv_second, axes, split_axis=1, concat_axis=0, tiled=True)  28.1 us
    all_to_all x1, blocking collectives, shards(): lax.all_to_all(update, axes, split_axis=0, concat_axis=0, tiled=True)  23.7 us
    pallas_call x2, Pallas kernels, attend(): pl.pallas_call(kernel, grid=(head_count,), in_specs=[pl.BlockSpec((slot_c...  18.5 us
    all_to_all x1, waiting for transfers between devices, shards(): lax.all_to_all(send, axes, split_axis=0, concat_axis=0, tiled=True)  13 us
    all_to_all x1, starting transfers between devices, shards(): lax.all_to_all(send, axes, split_axis=0, concat_axis=0, tiled=True)  11.5 us
    all_to_all x1, starting transfers between devices, shards(): lax.all_to_all(kv_second, axes, split_axis=1, concat_axis=0, tiled=True)  7.25 us
    dot_general x1, matrix products, prepare(): jnp.dot(normed, w_proj, preferred_element_type=jnp.float32)  7.05 us
  transfers between devices with their start and end apart: 3, of which 3 were waited for; matrix products, arithmetic and copies ran while one was open for 13% of the time, Pallas kernels for 5%

profile of v11, /device:TPU:1, one launch (start us, length us, event | category | flops | bytes accessed | tf_op | source)
XLA Modules:
  0.0 198.0 jit_solution(12017233007545429566)
XLA Ops:
  0.0 0.0 copy-start
  0.0 0.7 convert_element_type.53
  0.7 0.8 copy.26
  1.5 0.2 fusion.10
  1.8 0.9 fusion.12
  2.7 0.7 multiply_add_fusion
  3.4 0.2 copy.28
  3.5 1.6 convolution_convert_fusion
  5.1 0.4 reshape.117
  5.6 1.6 fusion.3
  7.2 11.5 %all-to-all-start = ((bf16[128,4,1152]{2,1,0:T(4,128)(2,1)}), bf16[128,4,1152]{2,1,0:T(4,128)(2,1)S(1)}, u32[]{:S(2)}, u32[]{:S(2)}) async-start(bf16[128,4,1152]{2,1,0:T(4,128)(2,1)} %fusion.3), calls=%async_computation | async-start | bytes 2359296 | tf_op jit(solution)/shard_map/all_to_all | solution.py:134
  18.7 4.9 %fusion.16 = (bf16[1,128,1,16,512]{4,3,2,0,1:T(8,128)(2,1)S(1)}, bf16[1,128,1,16,512]{4,3,2,0,1:T(8,128)(2,1)}, bf16[1,128,1,16,512]{4,3,2,0,1:T(8,128)(2,1)S(1)}, bf16[1,128,1,16,512]{4,3,2,0,1:T(8,128)(2,1)S(1)}) fusion(bf16[1,128,1,16,2048]{4,3,2,0,1:T(8,128)(2,1)} %bitcast.34), kind=kLoop, calls=%fused_computation.42 | loop fusion | bytes 16777216 | tf_op jit(solution)/shard_map/slice | solution.py:132
  23.5 2.5 %pad_maximum_fusion = bf16[1,128,1,16,1024]{4,3,2,0,1:T(8,128)(2,1)} fusion(bf16[1,128,1,16,512]{4,3,2,0,1:T(8,128)(2,1)S(1)} %get-tuple-element.15, bf16[1,128,1,16,512]{4,3,2,0,1:T(8,128)(2,1)S(1)} %get-tuple-element.16), kind=kLoop, calls=%fused_computation | loop fusion | flops 8388608 | bytes 8388608 | tf_op jit(solution)/shard_map/concatenate | solution.py:128
  26.1 13.0 %all-to-all-done = bf16[128,4,1152]{2,1,0:T(4,128)(2,1)S(1)} async-done(((bf16[128,4,1152]{2,1,0:T(4,128)(2,1)}), bf16[128,4,1152]{2,1,0:T(4,128)(2,1)S(1)}, u32[]{:S(2)}, u32[]{:S(2)}) %all-to-all-start) | async-done | bytes 1179680 | tf_op jit(solution)/shard_map/all_to_all | solution.py:134
  39.1 5.8 %all-to-all-start.1 = ((bf16[1,128,1,16,1024]{4,3,2,0,1:T(8,128)(2,1)}), bf16[1,128,1,16,1024]{4,3,2,0,1:T(8,128)(2,1)}, u32[]{:S(2)}, u32[]{:S(2)}) async-start(bf16[1,128,1,16,1024]{4,3,2,0,1:T(8,128)(2,1)} %pad_maximum_fusion), calls=%async_computation.1 | async-start | bytes 8388608 | tf_op jit(solution)/shard_map/all_to_all | solution.py:136
  44.9 4.3 %pad_maximum_fusion.1 = bf16[1,128,1,16,1024]{4,3,2,0,1:T(8,128)(2,1)} fusion(bf16[1,128,1,16,512]{4,3,2,0,1:T(8,128)(2,1)} %get-tuple-element.14, bf16[1,128,1,16,512]{4,3,2,0,1:T(8,128)(2,1)S(1)} %get-tuple-element.13), kind=kLoop, calls=%fused_computation.1 | loop fusion | flops 8388608 | bytes 8388608 | tf_op jit(solution)/shard_map/concatenate | solution.py:131
  49.2 48.1 %all-to-all-done.1 = bf16[1,128,1,16,1024]{4,3,2,0,1:T(8,128)(2,1)} async-done(((bf16[1,128,1,16,1024]{4,3,2,0,1:T(8,128)(2,1)}), bf16[1,128,1,16,1024]{4,3,2,0,1:T(8,128)(2,1)}, u32[]{:S(2)}, u32[]{:S(2)}) %all-to-all-start.1) | async-done | bytes 4194336 | tf_op jit(solution)/shard_map/all_to_all | solution.py:136
  97.3 0.0 copy-start.2
  97.3 7.3 %all-to-all-start.2 = ((bf16[1,128,1,16,1024]{4,3,2,0,1:T(8,128)(2,1)}), bf16[1,128,1,16,1024]{4,3,2,0,1:T(8,128)(2,1)}, u32[]{:S(2)}, u32[]{:S(2)}) async-start(bf16[1,128,1,16,1024]{4,3,2,0,1:T(8,128)(2,1)} %pad_maximum_fusion.1), calls=%async_computation.2 | async-start | bytes 8388608 | tf_op jit(solution)/shard_map/all_to_all | solution.py:138
  105.2 0.0 copy-done.2
  105.2 0.1 select_reduce_fusion
  105.3 0.1 fusion.15
  105.4 1.6 reshape.125.live_ref
  107.0 0.5 convert_reduce_fusion
  107.5 0.1 div.13
  107.6 0.8 multiply_reduce_fusion
  108.5 0.1 rsqrt.12
  108.6 0.1 slice_convert_fusion.1
  108.6 0.3 reshape.123
  108.9 0.6 slice_convert_fusion
  109.5 1.8 reshape.122
  111.2 0.0 copy-done
  111.2 1.1 fusion.1.bias_ref
  112.3 7.1 %multiply_convert_fusion.q_ref.g_ref = bf16[512,2048]{1,0:T(8,128)(2,1)} fusion(bf16[1024,2048]{1,0:T(8,128)(2,1)} %param.15, f32[512,1024]{1,0:T(8,128)} %reshape.122, f32[512]{0:T(512)S(1)} %rsqrt.12, f32[512]{0:T(512)S(1)} %div.13), kind=kOutput, calls=%fused_computation.2 | convolution fusion | flops 2154299392 | bytes 8392704 | tf_op jit(solution)/shard_map/dot_general | solution.py:21
  119.4 9.3 %shard_map.91.a_ref = f32[512,512]{1,0:T(8,128)} custom-call(bf16[512,2048]{1,0:T(8,128)(2,1)} %multiply_convert_fusion.q_ref.g_ref, bf16[2048,1024]{1,0:T(8,128)(2,1)} %bitcast.13.k_ref.v_ref, bf16[2048,1024]{1,0:T(8,128)(2,1)} %bitcast.13.k_ref.v_ref, f32[8,2048]{1,0:T(8,128)} %fusion.1.bias_ref, f32[2048,1]{1,0:T(8,128)} %reshape.125.live_ref), custom_call_target="tpu_custom_call" | custom-call | tf_op jit(solution)/shard_map/pallas_call | solution.py:52
  128.6 28.1 %all-to-all-done.2 = bf16[1,128,1,16,1024]{4,3,2,0,1:T(8,128)(2,1)} async-done(((bf16[1,128,1,16,1024]{4,3,2,0,1:T(8,128)(2,1)}), bf16[1,128,1,16,1024]{4,3,2,0,1:T(8,128)(2,1)}, u32[]{:S(2)}, u32[]{:S(2)}) %all-to-all-start.2) | async-done | bytes 4194336 | tf_op jit(solution)/shard_map/all_to_all | solution.py:138
  156.8 9.3 %shard_map.92.b_ref = f32[512,512]{1,0:T(8,128)} custom-call(bf16[512,2048]{1,0:T(8,128)(2,1)} %multiply_convert_fusion.q_ref.g_ref, bf16[2048,1024]{1,0:T(8,128)(2,1)} %bitcast.17.k_ref.v_ref, bf16[2048,1024]{1,0:T(8,128)(2,1)} %bitcast.17.k_ref.v_ref, f32[8,2048]{1,0:T(8,128)} %fusion.1.bias_ref, f32[2048,1]{1,0:T(8,128)} %reshape.125.live_ref), custom_call_target="tpu_custom_call" | custom-call | tf_op jit(solution)/shard_map/pallas_call | solution.py:52
  166.0 5.2 %shard_map.93 = bf16[512,1024]{1,0:T(8,128)(2,1)} custom-call(f32[512,512]{1,0:T(8,128)} %shard_map.91.a_ref, f32[512,512]{1,0:T(8,128)} %shard_map.92.b_ref, bf16[512,2048]{1,0:T(8,128)(2,1)} %multiply_convert_fusion.q_ref.g_ref, bf16[1024,1024]{1,0:T(8,128)(2,1)} %w_ref.1), custom_call_target="tpu_custom_call" | custom-call | tf_op jit(solution)/shard_map/pallas_call | solution.py:81
  171.3 1.5 reshape.120
  172.7 0.0 copy-start.1
  172.7 23.7 %all_to_all.31 = bf16[128,4,1024]{2,1,0:T(4,128)(2,1)S(1)} all-to-all(bf16[128,4,1024]{2,1,0:T(4,128)(2,1)S(1)} %reshape.120), channel_id=1, replica_groups=mesh['req'=16,'cache'=8] {'req','cache'}, dimensions={0} | all-to-all | bytes 2097152 | tf_op jit(solution)/shard_map/all_to_all | solution.py:170
  196.5 0.3 reshape.121
  196.8 0.0 copy-done.1
  196.8 1.3 fusion.2
  (9 shorter events, 0.1 us)
Async XLA Ops:
  0.0 111.2 %copy-start = (f32[8,128]{1,0:T(8,128)S(1)}, f32[8,128]{1,0:T(8,128)}, u32[]{:S(2)}) copy-start(f32[8,128]{1,0:T(8,128)} %param.17) | copy-start | bytes 12292
  7.2 31.9 %all-to-all-start = ((bf16[128,4,1152]{2,1,0:T(4,128)(2,1)}), bf16[128,4,1152]{2,1,0:T(4,128)(2,1)S(1)}, u32[]{:S(2)}, u32[]{:S(2)}) async-start(bf16[128,4,1152]{2,1,0:T(4,128)(2,1)} %fusion.3), calls=%async_computation | async-start | bytes 2359296 | tf_op jit(solution)/shard_map/all_to_all | solution.py:134
  39.1 58.2 %all-to-all-start.1 = ((bf16[1,128,1,16,1024]{4,3,2,0,1:T(8,128)(2,1)}), bf16[1,128,1,16,1024]{4,3,2,0,1:T(8,128)(2,1)}, u32[]{:S(2)}, u32[]{:S(2)}) async-start(bf16[1,128,1,16,1024]{4,3,2,0,1:T(8,128)(2,1)} %pad_maximum_fusion), calls=%async_computation.1 | async-start | bytes 8388608 | tf_op jit(solution)/shard_map/all_to_all | solution.py:136
  97.3 7.9 %copy-start.2 = (s32[1,128]{1,0:T(1,128)S(1)}, s32[1,128]{1,0:T(1,128)}, u32[]{:S(2)}) copy-start(s32[1,128]{1,0:T(1,128)} %param.12) | copy-start | bytes 1540
  97.3 59.5 %all-to-all-start.2 = ((bf16[1,128,1,16,1024]{4,3,2,0,1:T(8,128)(2,1)}), bf16[1,128,1,16,1024]{4,3,2,0,1:T(8,128)(2,1)}, u32[]{:S(2)}, u32[]{:S(2)}) async-start(bf16[1,128,1,16,1024]{4,3,2,0,1:T(8,128)(2,1)} %pad_maximum_fusion.1), calls=%async_computation.2 | async-start | bytes 8388608 | tf_op jit(solution)/shard_map/all_to_all | solution.py:138
  172.7 24.0 %copy-start.1 = (bf16[256,1024]{1,0:T(8,128)(2,1)S(1)}, bf16[256,1024]{1,0:T(8,128)(2,1)}, u32[]{:S(2)}) copy-start(bf16[256,1024]{1,0:T(8,128)(2,1)} %param.9) | copy-start | bytes 1572868

commit v12 on v11

--- a/solution.py
+++ b/solution.py
@@ -75,15 +75,16 @@
 
 
 def finish(first_half, second_half, projected, w_out):
-    slot_count, half = first_half.shape
-    features = 2 * half
+    slot_count, first_width = first_half.shape
+    second_width = second_half.shape[1]
+    features = first_width + second_width
     tile = 256 if slot_count % 256 == 0 else slot_count
     return pl.pallas_call(
         finish_kernel,
         grid=(slot_count // tile,),
         in_specs=[
-            pl.BlockSpec((tile, half), lambda i: (i, 0)),
-            pl.BlockSpec((tile, half), lambda i: (i, 0)),
+            pl.BlockSpec((tile, first_width), lambda i: (i, 0)),
+            pl.BlockSpec((tile, second_width), lambda i: (i, 0)),
             pl.BlockSpec((tile, features), lambda i: (i, 0)),
             pl.BlockSpec(w_out.shape, lambda i: (0, 0)),
         ],
@@ -123,8 +124,8 @@
     bucket_send = store_bucket.reshape(devices, capacity, bucket_lanes).astype(cand_x.dtype)
     bucket_send = jnp.pad(bucket_send, ((0, 0), (0, 0), (0, 128 - bucket_lanes)))
     send = jnp.concatenate([slotted, bucket_send], axis=2)
-    half_heads = head_count // 2
-    split = half_heads * head_dim
+    first_heads = head_count * 3 // 4
+    split = first_heads * head_dim
     kv_first = jnp.concatenate(
         [kv_store[..., :split], kv_store[..., features : features + split]], axis=-1
     )
@@ -136,8 +137,8 @@
     arrived_first = lax.all_to_all(kv_first, axes, split_axis=1, concat_axis=0, tiled=True)
     arrived_first, kv_second = lax.optimization_barrier((arrived_first, kv_second))
     arrived_second = lax.all_to_all(kv_second, axes, split_axis=1, concat_axis=0, tiled=True)
-    events_first = arrived_first.reshape(event_count, features)
-    events_second = arrived_second.reshape(event_count, features)
+    events_first = arrived_first.reshape(event_count, 2 * split)
+    events_second = arrived_second.reshape(event_count, 2 * (features - split))
     senders = received.shape[0]
     flat_rows = received[:, :, :features].reshape(senders * capacity, features)
     buckets = received[:, :, features : features + bucket_lanes].astype(jnp.int32).reshape(event_count)
@@ -160,10 +161,11 @@
     projected = prepare(flat_rows, w_proj)
     slot_count = projected.shape[0]
     attended_first = attend(
-        projected, events_first, half_bias, live, half_heads, head_dim, half_scale, 0
+        projected, events_first, half_bias, live, first_heads, head_dim, half_scale, 0
     )
+    second_heads = head_count - first_heads
     attended_second = attend(
-        projected, events_second, half_bias, live, half_heads, head_dim, half_scale, half_heads
+        projected, events_second, half_bias, live, second_heads, head_dim, half_scale, first_heads
     )
     update = finish(attended_first, attended_second, projected, w_out)
     update = update.reshape(senders, capacity, features)

time: 199 us -> 200 us (level)
  local copies, waits for them, and re-layouts: 11.8 us -> 14.5 us
  waiting for transfers between devices: 89.2 us -> 87 us
    all_to_all x1, waiting for transfers between devices: 28.1 us -> 2.99 us  [shards(): lax.all_to_all(kv_second, axes, split_axis=1, concat_axis=0, tiled=True)]
    all_to_all x1, waiting for transfers between devices: 48.1 us -> 70.4 us  [shards(): lax.all_to_all(kv_first, axes, split_axis=1, concat_axis=0, tiled=True)]
    slice x0 -> x1, local copies, waits for them, and re-layouts: none -> 3.27 us  [shards(): kv_store[..., :split]]
    slice x1, local copies, waits for them, and re-layouts: 4.89 us -> 1.69 us  [shards(): kv_store[..., split:features]]
    concatenate x1, other arithmetic: 4.31 us -> 1.65 us  [shards(): jnp.concatenate([kv_store[..., split:features], kv_store[..., features +...]
  transfers between devices with their start and end apart: 3 -> 3, of which waited for: 3 -> 3; matrix products, arithmetic and copies ran while one was open for 13% -> 13% of each run, Pallas kernels for 5% -> 6%
where the time goes in v12:
time: 200 us; the launch traced here: 199 us
  waiting for transfers between devices  87 us (44%)
  blocking collectives  25.6 us (13%)
  starting transfers between devices  24.5 us (12%)
  Pallas kernels  23.5 us (12%)
  local copies, waits for them, and re-layouts  14.5 us (7%)
  other arithmetic  12.1 us (6%)
  matrix products  11 us (6%)
    all_to_all x1, waiting for transfers between devices, shards(): lax.all_to_all(kv_first, axes, split_axis=1, concat_axis=0, tiled=True)  70.4 us
    all_to_all x1, blocking collectives, shards(): lax.all_to_all(update, axes, split_axis=0, concat_axis=0, tiled=True)  25.6 us
    pallas_call x2, Pallas kernels, attend(): pl.pallas_call(kernel, grid=(head_count,), in_specs=[pl.BlockSpec((slot_c...  18.5 us
    all_to_all x1, waiting for transfers between devices, shards(): lax.all_to_all(send, axes, split_axis=0, concat_axis=0, tiled=True)  13.6 us
    all_to_all x1, starting transfers between devices, shards(): lax.all_to_all(send, axes, split_axis=0, concat_axis=0, tiled=True)  11.5 us
    all_to_all x1, starting transfers between devices, shards(): lax.all_to_all(kv_second, axes, split_axis=1, concat_axis=0, tiled=True)  7.14 us
    dot_general x1, matrix products, prepare(): jnp.dot(normed, w_proj, preferred_element_type=jnp.float32)  7.04 us
    all_to_all x1, starting transfers between devices, shards(): lax.all_to_all(kv_first, axes, split_axis=1, concat_axis=0, tiled=True)  5.84 us
  transfers between devices with their start and end apart: 3, of which 3 were waited for; matrix products, arithmetic and copies ran while one was open for 13% of the time, Pallas kernels for 6%

profile of v12, /device:TPU:1, one launch (start us, length us, event | category | flops | bytes accessed | tf_op | source)
XLA Modules:
  0.0 199.0 jit_solution(10633901591887235103)
XLA Ops:
  0.0 0.0 copy-start
  0.0 0.0 copy-start.3
  0.0 0.8 copy.26
  0.8 0.2 fusion.10
  1.1 0.9 fusion.12
  2.0 0.7 multiply_add_fusion
  2.7 1.6 convolution_convert_fusion
  4.3 0.4 reshape.117
  4.7 0.0 copy-done.3
  4.7 0.2 copy.28
  4.9 1.6 fusion.3
  6.5 11.5 %all-to-all-start = ((bf16[128,4,1152]{2,1,0:T(4,128)(2,1)}), bf16[128,4,1152]{2,1,0:T(4,128)(2,1)S(1)}, u32[]{:S(2)}, u32[]{:S(2)}) async-start(bf16[128,4,1152]{2,1,0:T(4,128)(2,1)} %fusion.3), calls=%async_computation | async-start | bytes 2359296 | tf_op jit(solution)/shard_map/all_to_all | solution.py:135
  18.0 3.3 %fusion.17 = (bf16[1,128,1,16,768]{4,3,2,0,1:T(8,128)(2,1)S(1)}, bf16[1,128,1,16,768]{4,3,2,0,1:T(8,128)(2,1)S(1)}) fusion(bf16[1,128,1,16,2048]{4,3,2,0,1:T(8,128)(2,1)} %bitcast.36), kind=kLoop, calls=%fused_computation.43 | loop fusion | bytes 12582912 | tf_op jit(solution)/shard_map/slice | solution.py:130
  21.3 3.5 %pad_maximum_fusion = bf16[1,128,1,16,1536]{4,3,2,0,1:T(8,128)(2,1)} fusion(bf16[1,128,1,16,768]{4,3,2,0,1:T(8,128)(2,1)S(1)} %get-tuple-element.16, bf16[1,128,1,16,768]{4,3,2,0,1:T(8,128)(2,1)S(1)} %get-tuple-element.15), kind=kLoop, calls=%fused_computation | loop fusion | flops 12582912 | bytes 12582912 | tf_op jit(solution)/shard_map/concatenate | solution.py:129
  24.8 0.0 copy-start.4
  24.8 13.6 %all-to-all-done = bf16[128,4,1152]{2,1,0:T(4,128)(2,1)S(1)} async-done(((bf16[128,4,1152]{2,1,0:T(4,128)(2,1)}), bf16[128,4,1152]{2,1,0:T(4,128)(2,1)S(1)}, u32[]{:S(2)}, u32[]{:S(2)}) %all-to-all-start) | async-done | bytes 1179680 | tf_op jit(solution)/shard_map/all_to_all | solution.py:135
  38.4 5.8 %all-to-all-start.1 = ((bf16[1,128,1,16,1536]{4,3,2,0,1:T(8,128)(2,1)}), bf16[1,128,1,16,1536]{4,3,2,0,1:T(8,128)(2,1)}, u32[]{:S(2)}, u32[]{:S(2)}) async-start(bf16[1,128,1,16,1536]{4,3,2,0,1:T(8,128)(2,1)} %pad_maximum_fusion), calls=%async_computation.1 | async-start | bytes 12582912 | tf_op jit(solution)/shard_map/all_to_all | solution.py:137
  44.9 0.0 copy-done.4
  44.9 0.1 select_reduce_fusion
  45.0 0.1 fusion.15
  45.1 1.6 reshape.125.live_ref
  46.7 1.7 fusion.16
  48.4 1.7 pad_maximum_fusion.1
  50.0 0.5 convert_reduce_fusion
  50.5 70.4 %all-to-all-done.1 = bf16[1,128,1,16,1536]{4,3,2,0,1:T(8,128)(2,1)} async-done(((bf16[1,128,1,16,1536]{4,3,2,0,1:T(8,128)(2,1)}), bf16[1,128,1,16,1536]{4,3,2,0,1:T(8,128)(2,1)}, u32[]{:S(2)}, u32[]{:S(2)}) %all-to-all-start.1) | async-done | bytes 6291488 | tf_op jit(solution)/shard_map/all_to_all | solution.py:137
  120.9 7.1 %all-to-all-start.2 = ((bf16[1,128,1,16,512]{4,3,2,0,1:T(8,128)(2,1)}), bf16[1,128,1,16,512]{4,3,2,0,1:T(8,128)(2,1)S(1)}, u32[]{:S(2)}, u32[]{:S(2)}) async-start(bf16[1,128,1,16,512]{4,3,2,0,1:T(8,128)(2,1)} %pad_maximum_fusion.1), calls=%async_computation.2 | async-start | bytes 4194304 | tf_op jit(solution)/shard_map/all_to_all | solution.py:139
  128.1 0.8 multiply_reduce_fusion
  128.9 0.1 div.13
  129.1 0.1 rsqrt.12
  129.2 2.0 slice_convert_fusion
  131.1 3.0 %reshape.122 = f32[512,1024]{1,0:T(8,128)} reshape(f32[128,4,1024]{2,1,0:T(4,128)} %slice_convert_fusion) | data formatting | bytes 4194304 | tf_op jit(solution)/shard_map/convert_element_type | solution.py:20
  134.1 0.1 slice_convert_fusion.1
  134.2 0.3 reshape.123
  134.4 0.0 copy-done
  134.4 1.1 fusion.1.bias_ref
  135.5 7.0 %multiply_convert_fusion.q_ref.g_ref = bf16[512,2048]{1,0:T(8,128)(2,1)} fusion(bf16[1024,2048]{1,0:T(8,128)(2,1)} %param.15, f32[512,1024]{1,0:T(8,128)} %reshape.122, f32[512]{0:T(512)S(1)} %rsqrt.12, f32[512]{0:T(512)S(1)} %div.13), kind=kOutput, calls=%fused_computation.1 | convolution fusion | flops 2154299392 | bytes 8392704 | tf_op jit(solution)/shard_map/dot_general | solution.py:21
  142.5 12.7 %shard_map.91.a_ref = f32[512,768]{1,0:T(8,128)} custom-call(bf16[512,2048]{1,0:T(8,128)(2,1)} %multiply_convert_fusion.q_ref.g_ref, bf16[2048,1536]{1,0:T(8,128)(2,1)} %bitcast.13.k_ref.v_ref, bf16[2048,1536]{1,0:T(8,128)(2,1)} %bitcast.13.k_ref.v_ref, f32[8,2048]{1,0:T(8,128)} %fusion.1.bias_ref, f32[2048,1]{1,0:T(8,128)} %reshape.125.live_ref), custom_call_target="tpu_custom_call" | custom-call | tf_op jit(solution)/shard_map/pallas_call | solution.py:52
  155.2 3.0 %all-to-all-done.2 = bf16[1,128,1,16,512]{4,3,2,0,1:T(8,128)(2,1)S(1)} async-done(((bf16[1,128,1,16,512]{4,3,2,0,1:T(8,128)(2,1)}), bf16[1,128,1,16,512]{4,3,2,0,1:T(8,128)(2,1)S(1)}, u32[]{:S(2)}, u32[]{:S(2)}) %all-to-all-start.2) | async-done | bytes 2097184 | tf_op jit(solution)/shard_map/all_to_all | solution.py:139
  158.2 0.0 copy-start.1
  158.2 1.3 copy-done.1
  159.5 5.9 %shard_map.92.b_ref = f32[512,256]{1,0:T(8,128)} custom-call(bf16[512,2048]{1,0:T(8,128)(2,1)} %multiply_convert_fusion.q_ref.g_ref, bf16[2048,512]{1,0:T(8,128)(2,1)} %bitcast.34, bf16[2048,512]{1,0:T(8,128)(2,1)} %bitcast.35, f32[8,2048]{1,0:T(8,128)} %fusion.1.bias_ref, f32[2048,1]{1,0:T(8,128)} %reshape.125.live_ref), custom_call_target="tpu_custom_call" | custom-call | tf_op jit(solution)/shard_map/pallas_call | solution.py:52
  165.4 5.0 %shard_map.93 = bf16[512,1024]{1,0:T(8,128)(2,1)} custom-call(f32[512,768]{1,0:T(8,128)} %shard_map.91.a_ref, f32[512,256]{1,0:T(8,128)} %shard_map.92.b_ref, bf16[512,2048]{1,0:T(8,128)(2,1)} %multiply_convert_fusion.q_ref.g_ref, bf16[1024,1024]{1,0:T(8,128)(2,1)} %w_ref.1), custom_call_target="tpu_custom_call" | custom-call | tf_op jit(solution)/shard_map/pallas_call | solution.py:82
  170.4 1.5 reshape.120
  171.9 0.0 copy-start.2
  171.9 25.6 %all_to_all.31 = bf16[128,4,1024]{2,1,0:T(4,128)(2,1)S(1)} all-to-all(bf16[128,4,1024]{2,1,0:T(4,128)(2,1)S(1)} %reshape.120), channel_id=1, replica_groups=mesh['req'=16,'cache'=8] {'req','cache'}, dimensions={0} | all-to-all | bytes 2097152 | tf_op jit(solution)/shard_map/all_to_all | solution.py:172
  197.4 0.3 reshape.121
  197.7 0.0 copy-done.2
  197.7 1.3 fusion.2
  (10 shorter events, 0.1 us)
Async XLA Ops:
  0.0 134.4 %copy-start = (f32[8,128]{1,0:T(8,128)S(1)}, f32[8,128]{1,0:T(8,128)}, u32[]{:S(2)}) copy-start(f32[8,128]{1,0:T(8,128)} %param.17) | copy-start | bytes 12292
  0.0 4.7 %copy-start.3 = (s32[1,128,1,16]{1,3,2,0:T(8,128)S(1)}, s32[1,128,1,16]{1,3,2,0:T(8,128)}, u32[]{:S(2)}) copy-start(s32[1,128,1,16]{1,3,2,0:T(8,128)} %param.14) | copy-start | bytes 24580
  6.5 31.9 %all-to-all-start = ((bf16[128,4,1152]{2,1,0:T(4,128)(2,1)}), bf16[128,4,1152]{2,1,0:T(4,128)(2,1)S(1)}, u32[]{:S(2)}, u32[]{:S(2)}) async-start(bf16[128,4,1152]{2,1,0:T(4,128)(2,1)} %fusion.3), calls=%async_computation | async-start | bytes 2359296 | tf_op jit(solution)/shard_map/all_to_all | solution.py:135
  24.8 20.1 %copy-start.4 = (s32[1,128]{1,0:T(1,128)S(1)}, s32[1,128]{1,0:T(1,128)}, u32[]{:S(2)}) copy-start(s32[1,128]{1,0:T(1,128)} %param.12) | copy-start | bytes 1540
  38.4 82.5 %all-to-all-start.1 = ((bf16[1,128,1,16,1536]{4,3,2,0,1:T(8,128)(2,1)}), bf16[1,128,1,16,1536]{4,3,2,0,1:T(8,128)(2,1)}, u32[]{:S(2)}, u32[]{:S(2)}) async-start(bf16[1,128,1,16,1536]{4,3,2,0,1:T(8,128)(2,1)} %pad_maximum_fusion), calls=%async_computation.1 | async-start | bytes 12582912 | tf_op jit(solution)/shard_map/all_to_all | solution.py:137
  120.9 37.2 %all-to-all-start.2 = ((bf16[1,128,1,16,512]{4,3,2,0,1:T(8,128)(2,1)}), bf16[1,128,1,16,512]{4,3,2,0,1:T(8,128)(2,1)S(1)}, u32[]{:S(2)}, u32[]{:S(2)}) async-start(bf16[1,128,1,16,512]{4,3,2,0,1:T(8,128)(2,1)} %pad_maximum_fusion.1), calls=%async_computation.2 | async-start | bytes 4194304 | tf_op jit(solution)/shard_map/all_to_all | solution.py:139
  158.2 1.4 copy-start.1
  171.9 25.9 %copy-start.2 = (bf16[256,1024]{1,0:T(8,128)(2,1)S(1)}, bf16[256,1024]{1,0:T(8,128)(2,1)}, u32[]{:S(2)}) copy-start(bf16[256,1024]{1,0:T(8,128)(2,1)} %param.9) | copy-start | bytes 1572868

commit v13 on v12

--- a/solution.py
+++ b/solution.py
@@ -135,10 +135,6 @@
     received = lax.all_to_all(send, axes, split_axis=0, concat_axis=0, tiled=True)
     received, kv_first = lax.optimization_barrier((received, kv_first))
     arrived_first = lax.all_to_all(kv_first, axes, split_axis=1, concat_axis=0, tiled=True)
-    arrived_first, kv_second = lax.optimization_barrier((arrived_first, kv_second))
-    arrived_second = lax.all_to_all(kv_second, axes, split_axis=1, concat_axis=0, tiled=True)
-    events_first = arrived_first.reshape(event_count, 2 * split)
-    events_second = arrived_second.reshape(event_count, 2 * (features - split))
     senders = received.shape[0]
     flat_rows = received[:, :, :features].reshape(senders * capacity, features)
     buckets = received[:, :, features : features + bucket_lanes].astype(jnp.int32).reshape(event_count)
@@ -159,6 +155,12 @@
     half_scale = 0.5 / math.sqrt(head_dim)
 
     projected = prepare(flat_rows, w_proj)
+    arrived_first, kv_second, projected, half_bias, live = lax.optimization_barrier(
+        (arrived_first, kv_second, projected, half_bias, live)
+    )
+    arrived_second = lax.all_to_all(kv_second, axes, split_axis=1, concat_axis=0, tiled=True)
+    events_first = arrived_first.reshape(event_count, 2 * split)
+    events_second = arrived_second.reshape(event_count, 2 * (features - split))
     slot_count = projected.shape[0]
     attended_first = attend(
         projected, events_first, half_bias, live, first_heads, head_dim, half_scale, 0

time: 200 us -> 198 us (0.990)
  blocking collectives: 25.6 us -> 23.5 us
  waiting for transfers between devices: 87 us -> 89.1 us
    all_to_all x1, waiting for transfers between devices: 2.99 us -> 16 us  [shards(): lax.all_to_all(kv_second, axes, split_axis=1, concat_axis=0, tiled=True)]
    all_to_all x1, waiting for transfers between devices: 70.4 us -> 59.5 us  [shards(): lax.all_to_all(kv_first, axes, split_axis=1, concat_axis=0, tiled=True)]
    all_to_all x1, blocking collectives: 25.6 us -> 23.5 us  [shards(): lax.all_to_all(update, axes, split_axis=0, concat_axis=0, tiled=True)]
where the time goes in v13:
time: 198 us
  waiting for transfers between devices  89.1 us (45%)
  starting transfers between devices  24.5 us (12%)
  Pallas kernels  23.5 us (12%)
  blocking collectives  23.5 us (12%)
  local copies, waits for them, and re-layouts  14.4 us (7%)
  other arithmetic  11.4 us (6%)
  matrix products  10.4 us (5%)
    all_to_all x1, waiting for transfers between devices, shards(): lax.all_to_all(kv_first, axes, split_axis=1, concat_axis=0, tiled=True)  59.5 us
    all_to_all x1, blocking collectives, shards(): lax.all_to_all(update, axes, split_axis=0, concat_axis=0, tiled=True)  23.5 us
    pallas_call x2, Pallas kernels, attend(): pl.pallas_call(kernel, grid=(head_count,), in_specs=[pl.BlockSpec((slot_c...  18.5 us
    all_to_all x1, waiting for transfers between devices, shards(): lax.all_to_all(kv_second, axes, split_axis=1, concat_axis=0, tiled=True)  16 us
    all_to_all x1, waiting for transfers between devices, shards(): lax.all_to_all(send, axes, split_axis=0, concat_axis=0, tiled=True)  13.6 us
    all_to_all x1, starting transfers between devices, shards(): lax.all_to_all(send, axes, split_axis=0, concat_axis=0, tiled=True)  11.5 us
    all_to_all x1, starting transfers between devices, shards(): lax.all_to_all(kv_second, axes, split_axis=1, concat_axis=0, tiled=True)  7.14 us
    dot_general x1, matrix products, prepare(): jnp.dot(normed, w_proj, preferred_element_type=jnp.float32)  6.45 us
  transfers between devices with their start and end apart: 3, of which 3 were waited for; matrix products, arithmetic and copies ran while one was open for 13% of the time, Pallas kernels for 6%

profile of v13, /device:TPU:1, one launch (start us, length us, event | category | flops | bytes accessed | tf_op | source)
XLA Modules:
  0.0 197.6 jit_solution(18317964523370243030)
XLA Ops:
  0.0 0.0 copy-start
  0.0 0.7 convert_element_type.62
  0.7 0.2 copy.28
  0.9 0.8 copy.26
  1.7 0.2 fusion.10
  2.0 0.9 fusion.12
  2.9 0.7 multiply_add_fusion
  3.6 1.6 convolution_convert_fusion
  5.2 0.4 reshape.117
  5.6 1.6 fusion.3
  7.2 11.5 %all-to-all-start = ((bf16[128,4,1152]{2,1,0:T(4,128)(2,1)}), bf16[128,4,1152]{2,1,0:T(4,128)(2,1)S(1)}, u32[]{:S(2)}, u32[]{:S(2)}) async-start(bf16[128,4,1152]{2,1,0:T(4,128)(2,1)} %fusion.3), calls=%async_computation | async-start | bytes 2359296 | tf_op jit(solution)/shard_map/all_to_all | solution.py:135
  18.7 3.3 %fusion.17 = (bf16[1,128,1,16,768]{4,3,2,0,1:T(8,128)(2,1)S(1)}, bf16[1,128,1,16,768]{4,3,2,0,1:T(8,128)(2,1)S(1)}) fusion(bf16[1,128,1,16,2048]{4,3,2,0,1:T(8,128)(2,1)} %bitcast.36), kind=kLoop, calls=%fused_computation.43 | loop fusion | bytes 12582912 | tf_op jit(solution)/shard_map/slice | solution.py:130
  21.9 3.5 %pad_maximum_fusion = bf16[1,128,1,16,1536]{4,3,2,0,1:T(8,128)(2,1)} fusion(bf16[1,128,1,16,768]{4,3,2,0,1:T(8,128)(2,1)S(1)} %get-tuple-element.22, bf16[1,128,1,16,768]{4,3,2,0,1:T(8,128)(2,1)S(1)} %get-tuple-element.21), kind=kLoop, calls=%fused_computation | loop fusion | flops 12582912 | bytes 12582912 | tf_op jit(solution)/shard_map/concatenate | solution.py:129
  25.5 0.0 copy-start.4
  25.5 13.6 %all-to-all-done = bf16[128,4,1152]{2,1,0:T(4,128)(2,1)S(1)} async-done(((bf16[128,4,1152]{2,1,0:T(4,128)(2,1)}), bf16[128,4,1152]{2,1,0:T(4,128)(2,1)S(1)}, u32[]{:S(2)}, u32[]{:S(2)}) %all-to-all-start) | async-done | bytes 1179680 | tf_op jit(solution)/shard_map/all_to_all | solution.py:135
  39.1 5.8 %all-to-all-start.1 = ((bf16[1,128,1,16,1536]{4,3,2,0,1:T(8,128)(2,1)}), bf16[1,128,1,16,1536]{4,3,2,0,1:T(8,128)(2,1)}, u32[]{:S(2)}, u32[]{:S(2)}) async-start(bf16[1,128,1,16,1536]{4,3,2,0,1:T(8,128)(2,1)} %pad_maximum_fusion), calls=%async_computation.1 | async-start | bytes 12582912 | tf_op jit(solution)/shard_map/all_to_all | solution.py:137
  45.6 0.0 copy-done.4
  45.6 0.1 select_reduce_fusion
  45.7 0.1 fusion.15
  45.8 0.1 reshape.124
  45.9 1.7 fusion.16
  47.6 1.6 pad_maximum_fusion.1
  49.2 0.6 slice_convert_fusion
  49.8 1.7 reshape.122
  51.6 0.5 convert_reduce_fusion
  52.1 0.7 div.13
  52.7 0.8 multiply_reduce_fusion
  53.6 0.7 rsqrt.12
  54.3 0.1 slice_convert_fusion.1
  54.3 0.3 reshape.123
  54.6 0.0 copy-done
  54.6 1.1 fusion.1.bias_ref
  55.7 0.0 copy-done.2
  55.7 6.5 %multiply_convert_fusion.q_ref.g_ref = bf16[512,2048]{1,0:T(8,128)(2,1)} fusion(bf16[1024,2048]{1,0:T(8,128)(2,1)} %param.15, f32[512,1024]{1,0:T(8,128)S(1)} %copy-done.2, f32[512]{0:T(512)} %rsqrt.12, f32[512]{0:T(512)} %div.13), kind=kOutput, calls=%fused_computation.1 | convolution fusion | flops 2154299392 | bytes 8392704 | tf_op jit(solution)/shard_map/dot_general | solution.py:21
  62.1 59.5 %all-to-all-done.1 = bf16[1,128,1,16,1536]{4,3,2,0,1:T(8,128)(2,1)} async-done(((bf16[1,128,1,16,1536]{4,3,2,0,1:T(8,128)(2,1)}), bf16[1,128,1,16,1536]{4,3,2,0,1:T(8,128)(2,1)}, u32[]{:S(2)}, u32[]{:S(2)}) %all-to-all-start.1) | async-done | bytes 6291488 | tf_op jit(solution)/shard_map/all_to_all | solution.py:137
  121.6 7.1 %all-to-all-start.2 = ((bf16[1,128,1,16,512]{4,3,2,0,1:T(8,128)(2,1)}), bf16[1,128,1,16,512]{4,3,2,0,1:T(8,128)(2,1)S(1)}, u32[]{:S(2)}, u32[]{:S(2)}) async-start(bf16[1,128,1,16,512]{4,3,2,0,1:T(8,128)(2,1)} %pad_maximum_fusion.1), calls=%async_computation.2 | async-start | bytes 4194304 | tf_op jit(solution)/shard_map/all_to_all | solution.py:161
  128.8 1.4 copy.33.live_ref
  130.2 12.7 %shard_map.91.a_ref = f32[512,768]{1,0:T(8,128)} custom-call(bf16[512,2048]{1,0:T(8,128)(2,1)} %multiply_convert_fusion.q_ref.g_ref, bf16[2048,1536]{1,0:T(8,128)(2,1)} %bitcast.16.k_ref.v_ref, bf16[2048,1536]{1,0:T(8,128)(2,1)} %bitcast.16.k_ref.v_ref, f32[8,2048]{1,0:T(8,128)} %fusion.1.bias_ref, f32[2048,1]{1,0:T(8,128)} %copy.33.live_ref), custom_call_target="tpu_custom_call" | custom-call | tf_op jit(solution)/shard_map/pallas_call | solution.py:52
  142.9 16.0 %all-to-all-done.2 = bf16[1,128,1,16,512]{4,3,2,0,1:T(8,128)(2,1)S(1)} async-done(((bf16[1,128,1,16,512]{4,3,2,0,1:T(8,128)(2,1)}), bf16[1,128,1,16,512]{4,3,2,0,1:T(8,128)(2,1)S(1)}, u32[]{:S(2)}, u32[]{:S(2)}) %all-to-all-start.2) | async-done | bytes 2097184 | tf_op jit(solution)/shard_map/all_to_all | solution.py:161
  158.8 1.3 copy-done.1
  160.2 5.9 %shard_map.92.b_ref = f32[512,256]{1,0:T(8,128)} custom-call(bf16[512,2048]{1,0:T(8,128)(2,1)} %multiply_convert_fusion.q_ref.g_ref, bf16[2048,512]{1,0:T(8,128)(2,1)} %bitcast.34, bf16[2048,512]{1,0:T(8,128)(2,1)} %bitcast.35, f32[8,2048]{1,0:T(8,128)} %fusion.1.bias_ref, f32[2048,1]{1,0:T(8,128)} %copy.33.live_ref), custom_call_target="tpu_custom_call" | custom-call | tf_op jit(solution)/shard_map/pallas_call | solution.py:52
  166.1 5.0 %shard_map.93 = bf16[512,1024]{1,0:T(8,128)(2,1)} custom-call(f32[512,768]{1,0:T(8,128)} %shard_map.91.a_ref, f32[512,256]{1,0:T(8,128)} %shard_map.92.b_ref, bf16[512,2048]{1,0:T(8,128)(2,1)} %multiply_convert_fusion.q_ref.g_ref, bf16[1024,1024]{1,0:T(8,128)(2,1)} %w_ref.1), custom_call_target="tpu_custom_call" | custom-call | tf_op jit(solution)/shard_map/pallas_call | solution.py:82
  171.1 1.5 reshape.120
  172.5 0.0 copy-start.3
  172.5 23.5 %all_to_all.31 = bf16[128,4,1024]{2,1,0:T(4,128)(2,1)S(1)} all-to-all(bf16[128,4,1024]{2,1,0:T(4,128)(2,1)S(1)} %reshape.120), channel_id=1, replica_groups=mesh['req'=16,'cache'=8] {'req','cache'}, dimensions={0} | all-to-all | bytes 2097152 | tf_op jit(solution)/shard_map/all_to_all | solution.py:174
  196.0 0.3 reshape.121
  196.3 0.0 copy-done.3
  196.3 1.3 fusion.2
  (11 shorter events, 0.1 us)
Async XLA Ops:
  0.0 54.6 %copy-start = (f32[8,128]{1,0:T(8,128)S(1)}, f32[8,128]{1,0:T(8,128)}, u32[]{:S(2)}) copy-start(f32[8,128]{1,0:T(8,128)} %param.17) | copy-start | bytes 12292
  7.2 31.9 %all-to-all-start = ((bf16[128,4,1152]{2,1,0:T(4,128)(2,1)}), bf16[128,4,1152]{2,1,0:T(4,128)(2,1)S(1)}, u32[]{:S(2)}, u32[]{:S(2)}) async-start(bf16[128,4,1152]{2,1,0:T(4,128)(2,1)} %fusion.3), calls=%async_computation | async-start | bytes 2359296 | tf_op jit(solution)/shard_map/all_to_all | solution.py:135
  25.5 20.1 %copy-start.4 = (s32[1,128]{1,0:T(1,128)S(1)}, s32[1,128]{1,0:T(1,128)}, u32[]{:S(2)}) copy-start(s32[1,128]{1,0:T(1,128)} %param.12) | copy-start | bytes 1540
  39.1 82.5 %all-to-all-start.1 = ((bf16[1,128,1,16,1536]{4,3,2,0,1:T(8,128)(2,1)}), bf16[1,128,1,16,1536]{4,3,2,0,1:T(8,128)(2,1)}, u32[]{:S(2)}, u32[]{:S(2)}) async-start(bf16[1,128,1,16,1536]{4,3,2,0,1:T(8,128)(2,1)} %pad_maximum_fusion), calls=%async_computation.1 | async-start | bytes 12582912 | tf_op jit(solution)/shard_map/all_to_all | solution.py:137
  51.6 4.1 %copy-start.2 = (f32[512,1024]{1,0:T(8,128)S(1)}, f32[512,1024]{1,0:T(8,128)}, u32[]{:S(2)}) copy-start(f32[512,1024]{1,0:T(8,128)} %reshape.122) | copy-start | bytes 6291460
  121.6 37.2 %all-to-all-start.2 = ((bf16[1,128,1,16,512]{4,3,2,0,1:T(8,128)(2,1)}), bf16[1,128,1,16,512]{4,3,2,0,1:T(8,128)(2,1)S(1)}, u32[]{:S(2)}, u32[]{:S(2)}) async-start(bf16[1,128,1,16,512]{4,3,2,0,1:T(8,128)(2,1)} %pad_maximum_fusion.1), calls=%async_computation.2 | async-start | bytes 4194304 | tf_op jit(solution)/shard_map/all_to_all | solution.py:161
  158.8 1.4 copy-start.1
  172.5 23.8 %copy-start.3 = (bf16[256,1024]{1,0:T(8,128)(2,1)S(1)}, bf16[256,1024]{1,0:T(8,128)(2,1)}, u32[]{:S(2)}) copy-start(bf16[256,1024]{1,0:T(8,128)(2,1)} %param.9) | copy-start | bytes 1572868

commit v14 on v13

--- a/solution.py
+++ b/solution.py
@@ -124,7 +124,7 @@
     bucket_send = store_bucket.reshape(devices, capacity, bucket_lanes).astype(cand_x.dtype)
     bucket_send = jnp.pad(bucket_send, ((0, 0), (0, 0), (0, 128 - bucket_lanes)))
     send = jnp.concatenate([slotted, bucket_send], axis=2)
-    first_heads = head_count * 3 // 4
+    first_heads = head_count - 1
     split = first_heads * head_dim
     kv_first = jnp.concatenate(
         [kv_store[..., :split], kv_store[..., features : features + split]], axis=-1

time: 198 us -> 204 us (1.030)
  waiting for transfers between devices: 89.1 us -> 83.2 us
  starting transfers between devices: 24.5 us -> 29.3 us
  local copies, waits for them, and re-layouts: 14.4 us -> 17.2 us
  other arithmetic: 11.4 us -> 14.1 us
    all_to_all x1, waiting for transfers between devices: 59.5 us -> 73 us  [shards(): lax.all_to_all(kv_first, axes, split_axis=1, concat_axis=0, tiled=True)]
    all_to_all x1, waiting for transfers between devices: 16 us -> 3.32 us  [shards(): lax.all_to_all(kv_second, axes, split_axis=1, concat_axis=0, tiled=True)]
    all_to_all x1, waiting for transfers between devices: 13.6 us -> 6.96 us  [shards(): lax.all_to_all(send, axes, split_axis=0, concat_axis=0, tiled=True)]
    all_to_all x1, starting transfers between devices: 7.14 us -> 12 us  [shards(): lax.all_to_all(kv_second, axes, split_axis=1, concat_axis=0, tiled=True)]
    slice x1, local copies, waits for them, and re-layouts: 3.27 us -> 6.78 us  [shards(): kv_store[..., :split]]
    concatenate x1, other arithmetic: 3.53 us -> 6.69 us  [shards(): jnp.concatenate([kv_store[..., :split], kv_store[..., features:features +...]
  transfers between devices with their start and end apart: 3 -> 3, of which waited for: 3 -> 3; matrix products, arithmetic and copies ran while one was open for 13% -> 15% of each run, Pallas kernels for 6% -> 7%
where the time goes in v14:
time: 204 us
  waiting for transfers between devices  83.2 us (41%)
  starting transfers between devices  29.3 us (14%)
  blocking collectives  25.3 us (12%)
  Pallas kernels  23.3 us (11%)
  local copies, waits for them, and re-layouts  17.2 us (8%)
  other arithmetic  14.1 us (7%)
  matrix products  10.4 us (5%)
    all_to_all x1, waiting for transfers between devices, shards(): lax.all_to_all(kv_first, axes, split_axis=1, concat_axis=0, tiled=True)  73 us
    all_to_all x1, blocking collectives, shards(): lax.all_to_all(update, axes, split_axis=0, concat_axis=0, tiled=True)  25.3 us
    pallas_call x2, Pallas kernels, attend(): pl.pallas_call(kernel, grid=(head_count,), in_specs=[pl.BlockSpec((slot_c...  18.3 us
    all_to_all x1, starting transfers between devices, shards(): lax.all_to_all(kv_second, axes, split_axis=1, concat_axis=0, tiled=True)  12 us
    all_to_all x1, starting transfers between devices, shards(): lax.all_to_all(send, axes, split_axis=0, concat_axis=0, tiled=True)  11.5 us
    all_to_all x1, waiting for transfers between devices, shards(): lax.all_to_all(send, axes, split_axis=0, concat_axis=0, tiled=True)  6.96 us
    slice x1, local copies, waits for them, and re-layouts, shards(): kv_store[..., :split]  6.78 us
    concatenate x1, other arithmetic, shards(): jnp.concatenate([kv_store[..., :split], kv_store[..., features:features +...  6.69 us
  transfers between devices with their start and end apart: 3, of which 3 were waited for; matrix products, arithmetic and copies ran while one was open for 15% of the time, Pallas kernels for 7%

profile of v14, /device:TPU:1, one launch (start us, length us, event | category | flops | bytes accessed | tf_op | source)
XLA Modules:
  0.0 203.6 jit_solution(13895144327987586731)
XLA Ops:
  0.0 0.0 copy-start
  0.0 0.7 convert_element_type.62
  0.7 0.2 copy.28
  0.9 0.8 copy.26
  1.7 0.2 fusion.10
  2.0 0.9 fusion.12
  2.9 0.7 multiply_add_fusion
  3.6 1.6 convolution_convert_fusion
  5.2 0.4 reshape.117
  5.6 1.6 fusion.3
  7.2 11.5 %all-to-all-start = ((bf16[128,4,1152]{2,1,0:T(4,128)(2,1)}), bf16[128,4,1152]{2,1,0:T(4,128)(2,1)S(1)}, u32[]{:S(2)}, u32[]{:S(2)}) async-start(bf16[128,4,1152]{2,1,0:T(4,128)(2,1)} %fusion.3), calls=%async_computation | async-start | bytes 2359296 | tf_op jit(solution)/shard_map/all_to_all | solution.py:135
  18.7 6.8 %fusion.17 = (bf16[1,128,1,16,896]{4,3,2,0,1:T(8,128)(2,1)}, bf16[1,128,1,16,896]{4,3,2,0,1:T(8,128)(2,1)}) fusion(bf16[1,128,1,16,2048]{4,3,2,0,1:T(8,128)(2,1)} %bitcast.36), kind=kLoop, calls=%fused_computation.43 | loop fusion | bytes 14680064 | tf_op jit(solution)/shard_map/slice | solution.py:130
  25.5 6.7 %pad_maximum_fusion = bf16[1,128,1,16,1792]{4,3,2,0,1:T(8,128)(2,1)} fusion(bf16[1,128,1,16,896]{4,3,2,0,1:T(8,128)(2,1)} %get-tuple-element.22, bf16[1,128,1,16,896]{4,3,2,0,1:T(8,128)(2,1)} %get-tuple-element.21), kind=kLoop, calls=%fused_computation | loop fusion | flops 14680064 | bytes 14680064 | tf_op jit(solution)/shard_map/concatenate | solution.py:129
  32.2 0.0 copy-start.4
  32.2 7.0 %all-to-all-done = bf16[128,4,1152]{2,1,0:T(4,128)(2,1)S(1)} async-done(((bf16[128,4,1152]{2,1,0:T(4,128)(2,1)}), bf16[128,4,1152]{2,1,0:T(4,128)(2,1)S(1)}, u32[]{:S(2)}, u32[]{:S(2)}) %all-to-all-start) | async-done | bytes 1179680 | tf_op jit(solution)/shard_map/all_to_all | solution.py:135
  39.1 5.9 %all-to-all-start.1 = ((bf16[1,128,1,16,1792]{4,3,2,0,1:T(8,128)(2,1)}), bf16[1,128,1,16,1792]{4,3,2,0,1:T(8,128)(2,1)}, u32[]{:S(2)}, u32[]{:S(2)}) async-start(bf16[1,128,1,16,1792]{4,3,2,0,1:T(8,128)(2,1)} %pad_maximum_fusion), calls=%async_computation.1 | async-start | bytes 14680064 | tf_op jit(solution)/shard_map/all_to_all | solution.py:137
  45.6 0.0 copy-done.4
  45.6 0.1 select_reduce_fusion
  45.7 0.1 fusion.15
  45.8 0.1 reshape.124
  45.9 1.4 fusion.16
  47.3 1.1 pad_maximum_fusion.1
  48.4 0.6 slice_convert_fusion
  49.1 1.8 reshape.122
  50.8 0.5 convert_reduce_fusion
  51.3 0.7 div.13
  52.0 0.8 multiply_reduce_fusion
  52.9 0.7 rsqrt.12
  53.5 0.1 slice_convert_fusion.1
  53.6 0.3 reshape.123
  53.9 0.0 copy-done
  53.9 1.1 fusion.1.bias_ref
  54.9 0.0 copy-done.2
  54.9 6.4 %multiply_convert_fusion.q_ref.g_ref = bf16[512,2048]{1,0:T(8,128)(2,1)} fusion(bf16[1024,2048]{1,0:T(8,128)(2,1)} %param.15, f32[512,1024]{1,0:T(8,128)S(1)} %copy-done.2, f32[512]{0:T(512)} %rsqrt.12, f32[512]{0:T(512)} %div.13), kind=kOutput, calls=%fused_computation.1 | convolution fusion | flops 2154299392 | bytes 8392704 | tf_op jit(solution)/shard_map/dot_general | solution.py:21
  61.3 73.0 %all-to-all-done.1 = bf16[1,128,1,16,1792]{4,3,2,0,1:T(8,128)(2,1)} async-done(((bf16[1,128,1,16,1792]{4,3,2,0,1:T(8,128)(2,1)}), bf16[1,128,1,16,1792]{4,3,2,0,1:T(8,128)(2,1)}, u32[]{:S(2)}, u32[]{:S(2)}) %all-to-all-start.1) | async-done | bytes 7340064 | tf_op jit(solution)/shard_map/all_to_all | solution.py:137
  134.3 12.0 %all-to-all-start.2 = ((bf16[1,128,1,16,256]{4,3,2,0,1:T(8,128)(2,1)}), bf16[1,128,1,16,256]{4,3,2,0,1:T(8,128)(2,1)S(1)}, u32[]{:S(2)}, u32[]{:S(2)}) async-start(bf16[1,128,1,16,256]{4,3,2,0,1:T(8,128)(2,1)} %pad_maximum_fusion.1), calls=%async_computation.2 | async-start | bytes 2097152 | tf_op jit(solution)/shard_map/all_to_all | solution.py:161
  146.3 1.4 copy.33.live_ref
  147.7 14.3 %shard_map.91.a_ref = f32[512,896]{1,0:T(8,128)} custom-call(bf16[512,2048]{1,0:T(8,128)(2,1)} %multiply_convert_fusion.q_ref.g_ref, bf16[2048,1792]{1,0:T(8,128)(2,1)} %bitcast.16.k_ref.v_ref, bf16[2048,1792]{1,0:T(8,128)(2,1)} %bitcast.16.k_ref.v_ref, f32[8,2048]{1,0:T(8,128)} %fusion.1.bias_ref, f32[2048,1]{1,0:T(8,128)} %copy.33.live_ref), custom_call_target="tpu_custom_call" | custom-call | tf_op jit(solution)/shard_map/pallas_call | solution.py:52
  162.0 3.3 %all-to-all-done.2 = bf16[1,128,1,16,256]{4,3,2,0,1:T(8,128)(2,1)S(1)} async-done(((bf16[1,128,1,16,256]{4,3,2,0,1:T(8,128)(2,1)}), bf16[1,128,1,16,256]{4,3,2,0,1:T(8,128)(2,1)S(1)}, u32[]{:S(2)}, u32[]{:S(2)}) %all-to-all-start.2) | async-done | bytes 1048608 | tf_op jit(solution)/shard_map/all_to_all | solution.py:161
  165.3 1.0 copy-done.1
  166.3 4.0 %shard_map.92.b_ref = f32[512,128]{1,0:T(8,128)} custom-call(bf16[512,2048]{1,0:T(8,128)(2,1)} %multiply_convert_fusion.q_ref.g_ref, bf16[2048,256]{1,0:T(8,128)(2,1)} %bitcast.34, bf16[2048,256]{1,0:T(8,128)(2,1)} %bitcast.35, f32[8,2048]{1,0:T(8,128)} %fusion.1.bias_ref, f32[2048,1]{1,0:T(8,128)} %copy.33.live_ref), custom_call_target="tpu_custom_call" | custom-call | tf_op jit(solution)/shard_map/pallas_call | solution.py:52
  170.3 5.0 %shard_map.93 = bf16[512,1024]{1,0:T(8,128)(2,1)} custom-call(f32[512,896]{1,0:T(8,128)} %shard_map.91.a_ref, f32[512,128]{1,0:T(8,128)} %shard_map.92.b_ref, bf16[512,2048]{1,0:T(8,128)(2,1)} %multiply_convert_fusion.q_ref.g_ref, bf16[1024,1024]{1,0:T(8,128)(2,1)} %w_ref.1), custom_call_target="tpu_custom_call" | custom-call | tf_op jit(solution)/shard_map/pallas_call | solution.py:82
  175.2 1.5 reshape.120
  176.7 0.0 copy-start.3
  176.7 25.3 %all_to_all.31 = bf16[128,4,1024]{2,1,0:T(4,128)(2,1)S(1)} all-to-all(bf16[128,4,1024]{2,1,0:T(4,128)(2,1)S(1)} %reshape.120), channel_id=1, replica_groups=mesh['req'=16,'cache'=8] {'req','cache'}, dimensions={0} | all-to-all | bytes 2097152 | tf_op jit(solution)/shard_map/all_to_all | solution.py:174
  202.0 0.3 reshape.121
  202.3 0.0 copy-done.3
  202.3 1.3 fusion.2
  (11 shorter events, 0.1 us)
Async XLA Ops:
  0.0 53.9 %copy-start = (f32[8,128]{1,0:T(8,128)S(1)}, f32[8,128]{1,0:T(8,128)}, u32[]{:S(2)}) copy-start(f32[8,128]{1,0:T(8,128)} %param.17) | copy-start | bytes 12292
  7.2 31.9 %all-to-all-start = ((bf16[128,4,1152]{2,1,0:T(4,128)(2,1)}), bf16[128,4,1152]{2,1,0:T(4,128)(2,1)S(1)}, u32[]{:S(2)}, u32[]{:S(2)}) async-start(bf16[128,4,1152]{2,1,0:T(4,128)(2,1)} %fusion.3), calls=%async_computation | async-start | bytes 2359296 | tf_op jit(solution)/shard_map/all_to_all | solution.py:135
  32.2 13.5 %copy-start.4 = (s32[1,128]{1,0:T(1,128)S(1)}, s32[1,128]{1,0:T(1,128)}, u32[]{:S(2)}) copy-start(s32[1,128]{1,0:T(1,128)} %param.12) | copy-start | bytes 1540
  39.1 95.2 %all-to-all-start.1 = ((bf16[1,128,1,16,1792]{4,3,2,0,1:T(8,128)(2,1)}), bf16[1,128,1,16,1792]{4,3,2,0,1:T(8,128)(2,1)}, u32[]{:S(2)}, u32[]{:S(2)}) async-start(bf16[1,128,1,16,1792]{4,3,2,0,1:T(8,128)(2,1)} %pad_maximum_fusion), calls=%async_computation.1 | async-start | bytes 14680064 | tf_op jit(solution)/shard_map/all_to_all | solution.py:137
  50.8 4.1 %copy-start.2 = (f32[512,1024]{1,0:T(8,128)S(1)}, f32[512,1024]{1,0:T(8,128)}, u32[]{:S(2)}) copy-start(f32[512,1024]{1,0:T(8,128)} %reshape.122) | copy-start | bytes 6291460
  134.3 31.0 %all-to-all-start.2 = ((bf16[1,128,1,16,256]{4,3,2,0,1:T(8,128)(2,1)}), bf16[1,128,1,16,256]{4,3,2,0,1:T(8,128)(2,1)S(1)}, u32[]{:S(2)}, u32[]{:S(2)}) async-start(bf16[1,128,1,16,256]{4,3,2,0,1:T(8,128)(2,1)} %pad_maximum_fusion.1), calls=%async_computation.2 | async-start | bytes 2097152 | tf_op jit(solution)/shard_map/all_to_all | solution.py:161
  165.3 1.0 copy-start.1
  176.7 25.6 %copy-start.3 = (bf16[256,1024]{1,0:T(8,128)(2,1)S(1)}, bf16[256,1024]{1,0:T(8,128)(2,1)}, u32[]{:S(2)}) copy-start(bf16[256,1024]{1,0:T(8,128)(2,1)} %param.9) | copy-start | bytes 1572868

commit v15 on v14

--- a/solution.py
+++ b/solution.py
@@ -124,7 +124,7 @@
     bucket_send = store_bucket.reshape(devices, capacity, bucket_lanes).astype(cand_x.dtype)
     bucket_send = jnp.pad(bucket_send, ((0, 0), (0, 0), (0, 128 - bucket_lanes)))
     send = jnp.concatenate([slotted, bucket_send], axis=2)
-    first_heads = head_count - 1
+    first_heads = head_count * 5 // 8
     split = first_heads * head_dim
     kv_first = jnp.concatenate(
         [kv_store[..., :split], kv_store[..., features : features + split]], axis=-1

time: 204 us -> 200 us (0.980)
  waiting for transfers between devices: 83.2 us -> 89.4 us
  starting transfers between devices: 29.3 us -> 25.4 us
  other arithmetic: 14.1 us -> 11.1 us
  local copies, waits for them, and re-layouts: 17.2 us -> 14.8 us
    all_to_all x1, waiting for transfers between devices: 73 us -> 46 us  [shards(): lax.all_to_all(kv_first, axes, split_axis=1, concat_axis=0, tiled=True)]
    all_to_all x1, waiting for transfers between devices: 3.32 us -> 28.8 us  [shards(): lax.all_to_all(kv_second, axes, split_axis=1, concat_axis=0, tiled=True)]
    all_to_all x1, waiting for transfers between devices: 6.96 us -> 14.6 us  [shards(): lax.all_to_all(send, axes, split_axis=0, concat_axis=0, tiled=True)]
    all_to_all x1, starting transfers between devices: 12 us -> 8.1 us  [shards(): lax.all_to_all(kv_second, axes, split_axis=1, concat_axis=0, tiled=True)]
    concatenate x1, other arithmetic: 6.69 us -> 2.8 us  [shards(): jnp.concatenate([kv_store[..., :split], kv_store[..., features:features +...]
    slice x1, local copies, waits for them, and re-layouts: 6.78 us -> 3 us  [shards(): kv_store[..., :split]]
  transfers between devices with their start and end apart: 3 -> 3, of which waited for: 3 -> 3; matrix products, arithmetic and copies ran while one was open for 15% -> 12% of each run, Pallas kernels for 7% -> 6%
where the time goes in v15:
time: 200 us; the launch traced here: 199 us
  waiting for transfers between devices  89.4 us (45%)
  starting transfers between devices  25.4 us (13%)
  blocking collectives  23.7 us (12%)
  Pallas kernels  23.6 us (12%)
  local copies, waits for them, and re-layouts  14.8 us (7%)
  other arithmetic  11.1 us (6%)
  matrix products  10.3 us (5%)
    all_to_all x1, waiting for transfers between devices, shards(): lax.all_to_all(kv_first, axes, split_axis=1, concat_axis=0, tiled=True)  46 us
    all_to_all x1, waiting for transfers between devices, shards(): lax.all_to_all(kv_second, axes, split_axis=1, concat_axis=0, tiled=True)  28.8 us
    all_to_all x1, blocking collectives, shards(): lax.all_to_all(update, axes, split_axis=0, concat_axis=0, tiled=True)  23.7 us
    pallas_call x2, Pallas kernels, attend(): pl.pallas_call(kernel, grid=(head_count,), in_specs=[pl.BlockSpec((slot_c...  18.6 us
    all_to_all x1, waiting for transfers between devices, shards(): lax.all_to_all(send, axes, split_axis=0, concat_axis=0, tiled=True)  14.6 us
    all_to_all x1, starting transfers between devices, shards(): lax.all_to_all(send, axes, split_axis=0, concat_axis=0, tiled=True)  11.5 us
    all_to_all x1, starting transfers between devices, shards(): lax.all_to_all(kv_second, axes, split_axis=1, concat_axis=0, tiled=True)  8.1 us
    dot_general x1, matrix products, prepare(): jnp.dot(normed, w_proj, preferred_element_type=jnp.float32)  6.37 us
  transfers between devices with their start and end apart: 3, of which 3 were waited for; matrix products, arithmetic and copies ran while one was open for 12% of the time, Pallas kernels for 6%

profile of v15, /device:TPU:1, one launch (start us, length us, event | category | flops | bytes accessed | tf_op | source)
XLA Modules:
  0.0 199.1 jit_solution(11774728878400629611)
XLA Ops:
  0.0 0.0 copy-start
  0.0 0.7 convert_element_type.62
  0.7 0.2 copy.28
  0.9 0.8 copy.26
  1.7 0.2 fusion.10
  2.0 0.9 fusion.12
  2.9 0.7 multiply_add_fusion
  3.6 1.6 convolution_convert_fusion
  5.2 0.4 reshape.117
  5.6 1.6 fusion.3
  7.2 11.5 %all-to-all-start = ((bf16[128,4,1152]{2,1,0:T(4,128)(2,1)}), bf16[128,4,1152]{2,1,0:T(4,128)(2,1)S(1)}, u32[]{:S(2)}, u32[]{:S(2)}) async-start(bf16[128,4,1152]{2,1,0:T(4,128)(2,1)} %fusion.3), calls=%async_computation | async-start | bytes 2359296 | tf_op jit(solution)/shard_map/all_to_all | solution.py:135
  18.7 3.0 %fusion.17 = (bf16[1,128,1,16,640]{4,3,2,0,1:T(8,128)(2,1)S(1)}, bf16[1,128,1,16,640]{4,3,2,0,1:T(8,128)(2,1)S(1)}) fusion(bf16[1,128,1,16,2048]{4,3,2,0,1:T(8,128)(2,1)} %bitcast.36), kind=kLoop, calls=%fused_computation.43 | loop fusion | bytes 10485760 | tf_op jit(solution)/shard_map/slice | solution.py:130
  21.7 2.8 %pad_maximum_fusion = bf16[1,128,1,16,1280]{4,3,2,0,1:T(8,128)(2,1)} fusion(bf16[1,128,1,16,640]{4,3,2,0,1:T(8,128)(2,1)S(1)} %get-tuple-element.22, bf16[1,128,1,16,640]{4,3,2,0,1:T(8,128)(2,1)S(1)} %get-tuple-element.21), kind=kLoop, calls=%fused_computation | loop fusion | flops 10485760 | bytes 10485760 | tf_op jit(solution)/shard_map/concatenate | solution.py:129
  24.5 0.0 copy-start.4
  24.5 14.6 %all-to-all-done = bf16[128,4,1152]{2,1,0:T(4,128)(2,1)S(1)} async-done(((bf16[128,4,1152]{2,1,0:T(4,128)(2,1)}), bf16[128,4,1152]{2,1,0:T(4,128)(2,1)S(1)}, u32[]{:S(2)}, u32[]{:S(2)}) %all-to-all-start) | async-done | bytes 1179680 | tf_op jit(solution)/shard_map/all_to_all | solution.py:135
  39.1 5.8 %all-to-all-start.1 = ((bf16[1,128,1,16,1280]{4,3,2,0,1:T(8,128)(2,1)}), bf16[1,128,1,16,1280]{4,3,2,0,1:T(8,128)(2,1)}, u32[]{:S(2)}, u32[]{:S(2)}) async-start(bf16[1,128,1,16,1280]{4,3,2,0,1:T(8,128)(2,1)} %pad_maximum_fusion), calls=%async_computation.1 | async-start | bytes 10485760 | tf_op jit(solution)/shard_map/all_to_all | solution.py:137
  45.6 0.0 copy-done.4
  45.6 0.1 select_reduce_fusion
  45.7 0.1 fusion.15
  45.8 0.1 reshape.124
  45.9 2.2 %fusion.16 = (bf16[1,128,1,16,384]{4,3,2,0,1:T(8,128)(2,1)S(1)}, bf16[1,128,1,16,384]{4,3,2,0,1:T(8,128)(2,1)S(1)}) fusion(bf16[1,128,1,16,2048]{4,3,2,0,1:T(8,128)(2,1)} %bitcast.37), kind=kLoop, calls=%fused_computation.42 | loop fusion | bytes 6291456 | tf_op jit(solution)/shard_map/slice | solution.py:133
  48.1 2.0 %pad_maximum_fusion.1 = bf16[1,128,1,16,768]{4,3,2,0,1:T(8,128)(2,1)} fusion(bf16[1,128,1,16,384]{4,3,2,0,1:T(8,128)(2,1)S(1)} %get-tuple-element.20, bf16[1,128,1,16,384]{4,3,2,0,1:T(8,128)(2,1)S(1)} %get-tuple-element.19), kind=kLoop, calls=%fused_computation.2 | loop fusion | flops 6291456 | bytes 6291456 | tf_op jit(solution)/shard_map/concatenate | solution.py:132
  50.1 0.6 slice_convert_fusion
  50.7 1.7 reshape.122
  52.5 0.5 convert_reduce_fusion
  52.9 0.7 div.13
  53.6 0.8 multiply_reduce_fusion
  54.5 0.6 rsqrt.12
  55.1 0.1 slice_convert_fusion.1
  55.2 0.3 reshape.123
  55.5 0.0 copy-done
  55.5 1.1 fusion.1.bias_ref
  56.5 0.0 copy-done.2
  56.5 6.4 %multiply_convert_fusion.q_ref.g_ref = bf16[512,2048]{1,0:T(8,128)(2,1)} fusion(bf16[1024,2048]{1,0:T(8,128)(2,1)} %param.15, f32[512,1024]{1,0:T(8,128)S(1)} %copy-done.2, f32[512]{0:T(512)} %rsqrt.12, f32[512]{0:T(512)} %div.13), kind=kOutput, calls=%fused_computation.1 | convolution fusion | flops 2154299392 | bytes 8392704 | tf_op jit(solution)/shard_map/dot_general | solution.py:21
  62.9 46.0 %all-to-all-done.1 = bf16[1,128,1,16,1280]{4,3,2,0,1:T(8,128)(2,1)} async-done(((bf16[1,128,1,16,1280]{4,3,2,0,1:T(8,128)(2,1)}), bf16[1,128,1,16,1280]{4,3,2,0,1:T(8,128)(2,1)}, u32[]{:S(2)}, u32[]{:S(2)}) %all-to-all-start.1) | async-done | bytes 5242912 | tf_op jit(solution)/shard_map/all_to_all | solution.py:137
  108.9 8.1 %all-to-all-start.2 = ((bf16[1,128,1,16,768]{4,3,2,0,1:T(8,128)(2,1)}), bf16[1,128,1,16,768]{4,3,2,0,1:T(8,128)(2,1)S(1)}, u32[]{:S(2)}, u32[]{:S(2)}) async-start(bf16[1,128,1,16,768]{4,3,2,0,1:T(8,128)(2,1)} %pad_maximum_fusion.1), calls=%async_computation.2 | async-start | bytes 6291456 | tf_op jit(solution)/shard_map/all_to_all | solution.py:161
  117.0 1.4 copy.33.live_ref
  118.3 11.0 %shard_map.91.a_ref = f32[512,640]{1,0:T(8,128)} custom-call(bf16[512,2048]{1,0:T(8,128)(2,1)} %multiply_convert_fusion.q_ref.g_ref, bf16[2048,1280]{1,0:T(8,128)(2,1)} %bitcast.16.k_ref.v_ref, bf16[2048,1280]{1,0:T(8,128)(2,1)} %bitcast.16.k_ref.v_ref, f32[8,2048]{1,0:T(8,128)} %fusion.1.bias_ref, f32[2048,1]{1,0:T(8,128)} %copy.33.live_ref), custom_call_target="tpu_custom_call" | custom-call | tf_op jit(solution)/shard_map/pallas_call | solution.py:52
  129.3 28.8 %all-to-all-done.2 = bf16[1,128,1,16,768]{4,3,2,0,1:T(8,128)(2,1)S(1)} async-done(((bf16[1,128,1,16,768]{4,3,2,0,1:T(8,128)(2,1)}), bf16[1,128,1,16,768]{4,3,2,0,1:T(8,128)(2,1)S(1)}, u32[]{:S(2)}, u32[]{:S(2)}) %all-to-all-start.2) | async-done | bytes 3145760 | tf_op jit(solution)/shard_map/all_to_all | solution.py:161
  158.1 1.7 copy-done.1
  159.8 7.6 %shard_map.92.b_ref = f32[512,384]{1,0:T(8,128)} custom-call(bf16[512,2048]{1,0:T(8,128)(2,1)} %multiply_convert_fusion.q_ref.g_ref, bf16[2048,768]{1,0:T(8,128)(2,1)} %bitcast.34, bf16[2048,768]{1,0:T(8,128)(2,1)} %bitcast.35, f32[8,2048]{1,0:T(8,128)} %fusion.1.bias_ref, f32[2048,1]{1,0:T(8,128)} %copy.33.live_ref), custom_call_target="tpu_custom_call" | custom-call | tf_op jit(solution)/shard_map/pallas_call | solution.py:52
  167.4 5.1 %shard_map.93 = bf16[512,1024]{1,0:T(8,128)(2,1)} custom-call(f32[512,640]{1,0:T(8,128)} %shard_map.91.a_ref, f32[512,384]{1,0:T(8,128)} %shard_map.92.b_ref, bf16[512,2048]{1,0:T(8,128)(2,1)} %multiply_convert_fusion.q_ref.g_ref, bf16[1024,1024]{1,0:T(8,128)(2,1)} %w_ref.1), custom_call_target="tpu_custom_call" | custom-call | tf_op jit(solution)/shard_map/pallas_call | solution.py:82
  172.4 1.5 reshape.120
  173.9 0.0 copy-start.3
  173.9 23.7 %all_to_all.31 = bf16[128,4,1024]{2,1,0:T(4,128)(2,1)S(1)} all-to-all(bf16[128,4,1024]{2,1,0:T(4,128)(2,1)S(1)} %reshape.120), channel_id=1, replica_groups=mesh['req'=16,'cache'=8] {'req','cache'}, dimensions={0} | all-to-all | bytes 2097152 | tf_op jit(solution)/shard_map/all_to_all | solution.py:174
  197.6 0.3 reshape.121
  197.8 0.0 copy-done.3
  197.8 1.3 fusion.2
  (11 shorter events, 0.1 us)
Async XLA Ops:
  0.0 55.5 %copy-start = (f32[8,128]{1,0:T(8,128)S(1)}, f32[8,128]{1,0:T(8,128)}, u32[]{:S(2)}) copy-start(f32[8,128]{1,0:T(8,128)} %param.17) | copy-start | bytes 12292
  7.2 31.9 %all-to-all-start = ((bf16[128,4,1152]{2,1,0:T(4,128)(2,1)}), bf16[128,4,1152]{2,1,0:T(4,128)(2,1)S(1)}, u32[]{:S(2)}, u32[]{:S(2)}) async-start(bf16[128,4,1152]{2,1,0:T(4,128)(2,1)} %fusion.3), calls=%async_computation | async-start | bytes 2359296 | tf_op jit(solution)/shard_map/all_to_all | solution.py:135
  24.5 21.1 %copy-start.4 = (s32[1,128]{1,0:T(1,128)S(1)}, s32[1,128]{1,0:T(1,128)}, u32[]{:S(2)}) copy-start(s32[1,128]{1,0:T(1,128)} %param.12) | copy-start | bytes 1540
  39.1 69.8 %all-to-all-start.1 = ((bf16[1,128,1,16,1280]{4,3,2,0,1:T(8,128)(2,1)}), bf16[1,128,1,16,1280]{4,3,2,0,1:T(8,128)(2,1)}, u32[]{:S(2)}, u32[]{:S(2)}) async-start(bf16[1,128,1,16,1280]{4,3,2,0,1:T(8,128)(2,1)} %pad_maximum_fusion), calls=%async_computation.1 | async-start | bytes 10485760 | tf_op jit(solution)/shard_map/all_to_all | solution.py:137
  52.5 4.1 %copy-start.2 = (f32[512,1024]{1,0:T(8,128)S(1)}, f32[512,1024]{1,0:T(8,128)}, u32[]{:S(2)}) copy-start(f32[512,1024]{1,0:T(8,128)} %reshape.122) | copy-start | bytes 6291460
  108.9 49.3 %all-to-all-start.2 = ((bf16[1,128,1,16,768]{4,3,2,0,1:T(8,128)(2,1)}), bf16[1,128,1,16,768]{4,3,2,0,1:T(8,128)(2,1)S(1)}, u32[]{:S(2)}, u32[]{:S(2)}) async-start(bf16[1,128,1,16,768]{4,3,2,0,1:T(8,128)(2,1)} %pad_maximum_fusion.1), calls=%async_computation.2 | async-start | bytes 6291456 | tf_op jit(solution)/shard_map/all_to_all | solution.py:161
  158.1 1.7 copy-start.1
  173.9 23.9 %copy-start.3 = (bf16[256,1024]{1,0:T(8,128)(2,1)S(1)}, bf16[256,1024]{1,0:T(8,128)(2,1)}, u32[]{:S(2)}) copy-start(bf16[256,1024]{1,0:T(8,128)(2,1)} %param.9) | copy-start | bytes 1572868

commit v16 on v13

--- a/solution.py
+++ b/solution.py
@@ -78,7 +78,7 @@
     slot_count, first_width = first_half.shape
     second_width = second_half.shape[1]
     features = first_width + second_width
-    tile = 256 if slot_count % 256 == 0 else slot_count
+    tile = 128 if slot_count % 128 == 0 else slot_count
     return pl.pallas_call(
         finish_kernel,
         grid=(slot_count // tile,),

time: 198 us -> 199 us (level)
  transfers between devices with their start and end apart: 3 -> 3, of which waited for: 3 -> 3; matrix products, arithmetic and copies ran while one was open for 13% -> 12% of each run, Pallas kernels for 6% -> 6%
where the time goes in v16:
time: 199 us; the launch traced here: 198 us
  waiting for transfers between devices  89.1 us (45%)
  starting transfers between devices  24.5 us (12%)
  Pallas kernels  24.3 us (12%)
  blocking collectives  23.5 us (12%)
  local copies, waits for them, and re-layouts  14.4 us (7%)
  other arithmetic  11.4 us (6%)
  matrix products  10.4 us (5%)
    all_to_all x1, waiting for transfers between devices, shards(): lax.all_to_all(kv_first, axes, split_axis=1, concat_axis=0, tiled=True)  59.5 us
    all_to_all x1, blocking collectives, shards(): lax.all_to_all(update, axes, split_axis=0, concat_axis=0, tiled=True)  23.5 us
    pallas_call x2, Pallas kernels, attend(): pl.pallas_call(kernel, grid=(head_count,), in_specs=[pl.BlockSpec((slot_c...  18.5 us
    all_to_all x1, waiting for transfers between devices, shards(): lax.all_to_all(kv_second, axes, split_axis=1, concat_axis=0, tiled=True)  16 us
    all_to_all x1, waiting for transfers between devices, shards(): lax.all_to_all(send, axes, split_axis=0, concat_axis=0, tiled=True)  13.6 us
    all_to_all x1, starting transfers between devices, shards(): lax.all_to_all(send, axes, split_axis=0, concat_axis=0, tiled=True)  11.5 us
    all_to_all x1, starting transfers between devices, shards(): lax.all_to_all(kv_second, axes, split_axis=1, concat_axis=0, tiled=True)  7.14 us
    dot_general x1, matrix products, prepare(): jnp.dot(normed, w_proj, preferred_element_type=jnp.float32)  6.45 us
  transfers between devices with their start and end apart: 3, of which 3 were waited for; matrix products, arithmetic and copies ran while one was open for 12% of the time, Pallas kernels for 6%

profile of v16, /device:TPU:1, one launch (start us, length us, event | category | flops | bytes accessed | tf_op | source)
XLA Modules:
  0.0 198.4 jit_solution(8025405014093557543)
XLA Ops:
  0.0 0.0 copy-start
  0.0 0.7 convert_element_type.62
  0.7 0.2 copy.28
  0.9 0.8 copy.26
  1.7 0.2 fusion.10
  2.0 0.9 fusion.12
  2.9 0.7 multiply_add_fusion
  3.6 1.6 convolution_convert_fusion
  5.2 0.4 reshape.117
  5.6 1.6 fusion.3
  7.2 11.5 %all-to-all-start = ((bf16[128,4,1152]{2,1,0:T(4,128)(2,1)}), bf16[128,4,1152]{2,1,0:T(4,128)(2,1)S(1)}, u32[]{:S(2)}, u32[]{:S(2)}) async-start(bf16[128,4,1152]{2,1,0:T(4,128)(2,1)} %fusion.3), calls=%async_computation | async-start | bytes 2359296 | tf_op jit(solution)/shard_map/all_to_all | solution.py:135
  18.7 3.3 %fusion.17 = (bf16[1,128,1,16,768]{4,3,2,0,1:T(8,128)(2,1)S(1)}, bf16[1,128,1,16,768]{4,3,2,0,1:T(8,128)(2,1)S(1)}) fusion(bf16[1,128,1,16,2048]{4,3,2,0,1:T(8,128)(2,1)} %bitcast.36), kind=kLoop, calls=%fused_computation.43 | loop fusion | bytes 12582912 | tf_op jit(solution)/shard_map/slice | solution.py:130
  21.9 3.5 %pad_maximum_fusion = bf16[1,128,1,16,1536]{4,3,2,0,1:T(8,128)(2,1)} fusion(bf16[1,128,1,16,768]{4,3,2,0,1:T(8,128)(2,1)S(1)} %get-tuple-element.22, bf16[1,128,1,16,768]{4,3,2,0,1:T(8,128)(2,1)S(1)} %get-tuple-element.21), kind=kLoop, calls=%fused_computation | loop fusion | flops 12582912 | bytes 12582912 | tf_op jit(solution)/shard_map/concatenate | solution.py:129
  25.5 0.0 copy-start.4
  25.5 13.6 %all-to-all-done = bf16[128,4,1152]{2,1,0:T(4,128)(2,1)S(1)} async-done(((bf16[128,4,1152]{2,1,0:T(4,128)(2,1)}), bf16[128,4,1152]{2,1,0:T(4,128)(2,1)S(1)}, u32[]{:S(2)}, u32[]{:S(2)}) %all-to-all-start) | async-done | bytes 1179680 | tf_op jit(solution)/shard_map/all_to_all | solution.py:135
  39.1 5.8 %all-to-all-start.1 = ((bf16[1,128,1,16,1536]{4,3,2,0,1:T(8,128)(2,1)}), bf16[1,128,1,16,1536]{4,3,2,0,1:T(8,128)(2,1)}, u32[]{:S(2)}, u32[]{:S(2)}) async-start(bf16[1,128,1,16,1536]{4,3,2,0,1:T(8,128)(2,1)} %pad_maximum_fusion), calls=%async_computation.1 | async-start | bytes 12582912 | tf_op jit(solution)/shard_map/all_to_all | solution.py:137
  45.6 0.0 copy-done.4
  45.6 0.1 select_reduce_fusion
  45.7 0.1 fusion.15
  45.8 0.1 reshape.124
  45.9 1.7 fusion.16
  47.6 1.6 pad_maximum_fusion.1
  49.2 0.6 slice_convert_fusion
  49.8 1.7 reshape.122
  51.6 0.5 convert_reduce_fusion
  52.1 0.7 div.13
  52.7 0.8 multiply_reduce_fusion
  53.6 0.7 rsqrt.12
  54.3 0.1 slice_convert_fusion.1
  54.3 0.3 reshape.123
  54.6 0.0 copy-done
  54.6 1.1 fusion.1.bias_ref
  55.7 0.0 copy-done.2
  55.7 6.5 %multiply_convert_fusion.q_ref.g_ref = bf16[512,2048]{1,0:T(8,128)(2,1)} fusion(bf16[1024,2048]{1,0:T(8,128)(2,1)} %param.15, f32[512,1024]{1,0:T(8,128)S(1)} %copy-done.2, f32[512]{0:T(512)} %rsqrt.12, f32[512]{0:T(512)} %div.13), kind=kOutput, calls=%fused_computation.1 | convolution fusion | flops 2154299392 | bytes 8392704 | tf_op jit(solution)/shard_map/dot_general | solution.py:21
  62.1 59.5 %all-to-all-done.1 = bf16[1,128,1,16,1536]{4,3,2,0,1:T(8,128)(2,1)} async-done(((bf16[1,128,1,16,1536]{4,3,2,0,1:T(8,128)(2,1)}), bf16[1,128,1,16,1536]{4,3,2,0,1:T(8,128)(2,1)}, u32[]{:S(2)}, u32[]{:S(2)}) %all-to-all-start.1) | async-done | bytes 6291488 | tf_op jit(solution)/shard_map/all_to_all | solution.py:137
  121.6 7.1 %all-to-all-start.2 = ((bf16[1,128,1,16,512]{4,3,2,0,1:T(8,128)(2,1)}), bf16[1,128,1,16,512]{4,3,2,0,1:T(8,128)(2,1)S(1)}, u32[]{:S(2)}, u32[]{:S(2)}) async-start(bf16[1,128,1,16,512]{4,3,2,0,1:T(8,128)(2,1)} %pad_maximum_fusion.1), calls=%async_computation.2 | async-start | bytes 4194304 | tf_op jit(solution)/shard_map/all_to_all | solution.py:161
  128.8 1.4 copy.33.live_ref
  130.2 12.7 %shard_map.91.a_ref = f32[512,768]{1,0:T(8,128)} custom-call(bf16[512,2048]{1,0:T(8,128)(2,1)} %multiply_convert_fusion.q_ref.g_ref, bf16[2048,1536]{1,0:T(8,128)(2,1)} %bitcast.16.k_ref.v_ref, bf16[2048,1536]{1,0:T(8,128)(2,1)} %bitcast.16.k_ref.v_ref, f32[8,2048]{1,0:T(8,128)} %fusion.1.bias_ref, f32[2048,1]{1,0:T(8,128)} %copy.33.live_ref), custom_call_target="tpu_custom_call" | custom-call | tf_op jit(solution)/shard_map/pallas_call | solution.py:52
  142.9 16.0 %all-to-all-done.2 = bf16[1,128,1,16,512]{4,3,2,0,1:T(8,128)(2,1)S(1)} async-done(((bf16[1,128,1,16,512]{4,3,2,0,1:T(8,128)(2,1)}), bf16[1,128,1,16,512]{4,3,2,0,1:T(8,128)(2,1)S(1)}, u32[]{:S(2)}, u32[]{:S(2)}) %all-to-all-start.2) | async-done | bytes 2097184 | tf_op jit(solution)/shard_map/all_to_all | solution.py:161
  158.8 1.3 copy-done.1
  160.2 5.9 %shard_map.92.b_ref = f32[512,256]{1,0:T(8,128)} custom-call(bf16[512,2048]{1,0:T(8,128)(2,1)} %multiply_convert_fusion.q_ref.g_ref, bf16[2048,512]{1,0:T(8,128)(2,1)} %bitcast.34, bf16[2048,512]{1,0:T(8,128)(2,1)} %bitcast.35, f32[8,2048]{1,0:T(8,128)} %fusion.1.bias_ref, f32[2048,1]{1,0:T(8,128)} %copy.33.live_ref), custom_call_target="tpu_custom_call" | custom-call | tf_op jit(solution)/shard_map/pallas_call | solution.py:52
  166.1 5.8 %shard_map.93 = bf16[512,1024]{1,0:T(8,128)(2,1)} custom-call(f32[512,768]{1,0:T(8,128)} %shard_map.91.a_ref, f32[512,256]{1,0:T(8,128)} %shard_map.92.b_ref, bf16[512,2048]{1,0:T(8,128)(2,1)} %multiply_convert_fusion.q_ref.g_ref, bf16[1024,1024]{1,0:T(8,128)(2,1)} %w_ref.1), custom_call_target="tpu_custom_call" | custom-call | tf_op jit(solution)/shard_map/pallas_call | solution.py:82
  171.8 1.5 reshape.120
  173.3 0.0 copy-start.3
  173.3 23.5 %all_to_all.31 = bf16[128,4,1024]{2,1,0:T(4,128)(2,1)S(1)} all-to-all(bf16[128,4,1024]{2,1,0:T(4,128)(2,1)S(1)} %reshape.120), channel_id=1, replica_groups=mesh['req'=16,'cache'=8] {'req','cache'}, dimensions={0} | all-to-all | bytes 2097152 | tf_op jit(solution)/shard_map/all_to_all | solution.py:174
  196.8 0.3 reshape.121
  197.1 0.0 copy-done.3
  197.1 1.3 fusion.2
  (11 shorter events, 0.1 us)
Async XLA Ops:
  0.0 54.6 %copy-start = (f32[8,128]{1,0:T(8,128)S(1)}, f32[8,128]{1,0:T(8,128)}, u32[]{:S(2)}) copy-start(f32[8,128]{1,0:T(8,128)} %param.17) | copy-start | bytes 12292
  7.2 31.9 %all-to-all-start = ((bf16[128,4,1152]{2,1,0:T(4,128)(2,1)}), bf16[128,4,1152]{2,1,0:T(4,128)(2,1)S(1)}, u32[]{:S(2)}, u32[]{:S(2)}) async-start(bf16[128,4,1152]{2,1,0:T(4,128)(2,1)} %fusion.3), calls=%async_computation | async-start | bytes 2359296 | tf_op jit(solution)/shard_map/all_to_all | solution.py:135
  25.5 20.1 %copy-start.4 = (s32[1,128]{1,0:T(1,128)S(1)}, s32[1,128]{1,0:T(1,128)}, u32[]{:S(2)}) copy-start(s32[1,128]{1,0:T(1,128)} %param.12) | copy-start | bytes 1540
  39.1 82.5 %all-to-all-start.1 = ((bf16[1,128,1,16,1536]{4,3,2,0,1:T(8,128)(2,1)}), bf16[1,128,1,16,1536]{4,3,2,0,1:T(8,128)(2,1)}, u32[]{:S(2)}, u32[]{:S(2)}) async-start(bf16[1,128,1,16,1536]{4,3,2,0,1:T(8,128)(2,1)} %pad_maximum_fusion), calls=%async_computation.1 | async-start | bytes 12582912 | tf_op jit(solution)/shard_map/all_to_all | solution.py:137
  51.6 4.1 %copy-start.2 = (f32[512,1024]{1,0:T(8,128)S(1)}, f32[512,1024]{1,0:T(8,128)}, u32[]{:S(2)}) copy-start(f32[512,1024]{1,0:T(8,128)} %reshape.122) | copy-start | bytes 6291460
  121.6 37.2 %all-to-all-start.2 = ((bf16[1,128,1,16,512]{4,3,2,0,1:T(8,128)(2,1)}), bf16[1,128,1,16,512]{4,3,2,0,1:T(8,128)(2,1)S(1)}, u32[]{:S(2)}, u32[]{:S(2)}) async-start(bf16[1,128,1,16,512]{4,3,2,0,1:T(8,128)(2,1)} %pad_maximum_fusion.1), calls=%async_computation.2 | async-start | bytes 4194304 | tf_op jit(solution)/shard_map/all_to_all | solution.py:161
  158.8 1.4 copy-start.1
  173.3 23.7 %copy-start.3 = (bf16[256,1024]{1,0:T(8,128)(2,1)S(1)}, bf16[256,1024]{1,0:T(8,128)(2,1)}, u32[]{:S(2)}) copy-start(bf16[256,1024]{1,0:T(8,128)(2,1)} %param.9) | copy-start | bytes 1572868

commit v17 on v13

--- a/solution.py
+++ b/solution.py
@@ -47,7 +47,7 @@
     slot_count = projected.shape[0]
     event_count = events.shape[0]
     total_heads = half_bias.shape[0]
-    chunk = 512 if event_count % 512 == 0 else event_count
+    chunk = 1024 if event_count % 1024 == 0 else event_count
     kernel = functools.partial(attend_kernel, half_scale=half_scale, chunk=chunk, first=first)
     return pl.pallas_call(
         kernel,

time: 198 us -> 199 us (level)
  Pallas kernels: 23.5 us -> 25.9 us
    pallas_call x2, Pallas kernels: 18.5 us -> 20.9 us  [attend(): pl.pallas_call(kernel, grid=(head_count,), in_specs=[pl.BlockSpec((slot_c...]
  transfers between devices with their start and end apart: 3 -> 3, of which waited for: 3 -> 3; matrix products, arithmetic and copies ran while one was open for 13% -> 12% of each run, Pallas kernels for 6% -> 7%
where the time goes in v17:
time: 199 us; the launch traced here: 198 us
  waiting for transfers between devices  87.3 us (44%)
  Pallas kernels  25.9 us (13%)
  starting transfers between devices  24.5 us (12%)
  blocking collectives  23.5 us (12%)
  local copies, waits for them, and re-layouts  14.4 us (7%)
  other arithmetic  11.4 us (6%)
  matrix products  10.4 us (5%)
    all_to_all x1, waiting for transfers between devices, shards(): lax.all_to_all(kv_first, axes, split_axis=1, concat_axis=0, tiled=True)  59.5 us
    all_to_all x1, blocking collectives, shards(): lax.all_to_all(update, axes, split_axis=0, concat_axis=0, tiled=True)  23.5 us
    pallas_call x2, Pallas kernels, attend(): pl.pallas_call(kernel, grid=(head_count,), in_specs=[pl.BlockSpec((slot_c...  20.9 us
    all_to_all x1, waiting for transfers between devices, shards(): lax.all_to_all(kv_second, axes, split_axis=1, concat_axis=0, tiled=True)  14.2 us
    all_to_all x1, waiting for transfers between devices, shards(): lax.all_to_all(send, axes, split_axis=0, concat_axis=0, tiled=True)  13.6 us
    all_to_all x1, starting transfers between devices, shards(): lax.all_to_all(send, axes, split_axis=0, concat_axis=0, tiled=True)  11.5 us
    all_to_all x1, starting transfers between devices, shards(): lax.all_to_all(kv_second, axes, split_axis=1, concat_axis=0, tiled=True)  7.14 us
    dot_general x1, matrix products, prepare(): jnp.dot(normed, w_proj, preferred_element_type=jnp.float32)  6.45 us
  transfers between devices with their start and end apart: 3, of which 3 were waited for; matrix products, arithmetic and copies ran while one was open for 12% of the time, Pallas kernels for 7%

profile of v17, /device:TPU:1, one launch (start us, length us, event | category | flops | bytes accessed | tf_op | source)
XLA Modules:
  0.0 198.2 jit_solution(9576822847864950453)
XLA Ops:
  0.0 0.0 copy-start
  0.0 0.7 convert_element_type.62
  0.7 0.2 copy.28
  0.9 0.8 copy.26
  1.7 0.2 fusion.10
  2.0 0.9 fusion.12
  2.9 0.7 multiply_add_fusion
  3.6 1.6 convolution_convert_fusion
  5.2 0.4 reshape.117
  5.6 1.6 fusion.3
  7.2 11.5 %all-to-all-start = ((bf16[128,4,1152]{2,1,0:T(4,128)(2,1)}), bf16[128,4,1152]{2,1,0:T(4,128)(2,1)S(1)}, u32[]{:S(2)}, u32[]{:S(2)}) async-start(bf16[128,4,1152]{2,1,0:T(4,128)(2,1)} %fusion.3), calls=%async_computation | async-start | bytes 2359296 | tf_op jit(solution)/shard_map/all_to_all | solution.py:135
  18.7 3.3 %fusion.17 = (bf16[1,128,1,16,768]{4,3,2,0,1:T(8,128)(2,1)S(1)}, bf16[1,128,1,16,768]{4,3,2,0,1:T(8,128)(2,1)S(1)}) fusion(bf16[1,128,1,16,2048]{4,3,2,0,1:T(8,128)(2,1)} %bitcast.36), kind=kLoop, calls=%fused_computation.43 | loop fusion | bytes 12582912 | tf_op jit(solution)/shard_map/slice | solution.py:130
  21.9 3.5 %pad_maximum_fusion = bf16[1,128,1,16,1536]{4,3,2,0,1:T(8,128)(2,1)} fusion(bf16[1,128,1,16,768]{4,3,2,0,1:T(8,128)(2,1)S(1)} %get-tuple-element.22, bf16[1,128,1,16,768]{4,3,2,0,1:T(8,128)(2,1)S(1)} %get-tuple-element.21), kind=kLoop, calls=%fused_computation | loop fusion | flops 12582912 | bytes 12582912 | tf_op jit(solution)/shard_map/concatenate | solution.py:129
  25.5 0.0 copy-start.4
  25.5 13.6 %all-to-all-done = bf16[128,4,1152]{2,1,0:T(4,128)(2,1)S(1)} async-done(((bf16[128,4,1152]{2,1,0:T(4,128)(2,1)}), bf16[128,4,1152]{2,1,0:T(4,128)(2,1)S(1)}, u32[]{:S(2)}, u32[]{:S(2)}) %all-to-all-start) | async-done | bytes 1179680 | tf_op jit(solution)/shard_map/all_to_all | solution.py:135
  39.1 5.8 %all-to-all-start.1 = ((bf16[1,128,1,16,1536]{4,3,2,0,1:T(8,128)(2,1)}), bf16[1,128,1,16,1536]{4,3,2,0,1:T(8,128)(2,1)}, u32[]{:S(2)}, u32[]{:S(2)}) async-start(bf16[1,128,1,16,1536]{4,3,2,0,1:T(8,128)(2,1)} %pad_maximum_fusion), calls=%async_computation.1 | async-start | bytes 12582912 | tf_op jit(solution)/shard_map/all_to_all | solution.py:137
  45.6 0.0 copy-done.4
  45.6 0.1 select_reduce_fusion
  45.7 0.1 fusion.15
  45.8 0.1 reshape.124
  45.9 1.7 fusion.16
  47.6 1.6 pad_maximum_fusion.1
  49.2 0.6 slice_convert_fusion
  49.8 1.7 reshape.122
  51.6 0.5 convert_reduce_fusion
  52.1 0.7 div.13
  52.7 0.8 multiply_reduce_fusion
  53.6 0.7 rsqrt.12
  54.3 0.1 slice_convert_fusion.1
  54.3 0.3 reshape.123
  54.6 0.0 copy-done
  54.6 1.1 fusion.1.bias_ref
  55.7 0.0 copy-done.2
  55.7 6.5 %multiply_convert_fusion.q_ref.g_ref = bf16[512,2048]{1,0:T(8,128)(2,1)} fusion(bf16[1024,2048]{1,0:T(8,128)(2,1)} %param.15, f32[512,1024]{1,0:T(8,128)S(1)} %copy-done.2, f32[512]{0:T(512)} %rsqrt.12, f32[512]{0:T(512)} %div.13), kind=kOutput, calls=%fused_computation.1 | convolution fusion | flops 2154299392 | bytes 8392704 | tf_op jit(solution)/shard_map/dot_general | solution.py:21
  62.1 59.5 %all-to-all-done.1 = bf16[1,128,1,16,1536]{4,3,2,0,1:T(8,128)(2,1)} async-done(((bf16[1,128,1,16,1536]{4,3,2,0,1:T(8,128)(2,1)}), bf16[1,128,1,16,1536]{4,3,2,0,1:T(8,128)(2,1)}, u32[]{:S(2)}, u32[]{:S(2)}) %all-to-all-start.1) | async-done | bytes 6291488 | tf_op jit(solution)/shard_map/all_to_all | solution.py:137
  121.6 7.1 %all-to-all-start.2 = ((bf16[1,128,1,16,512]{4,3,2,0,1:T(8,128)(2,1)}), bf16[1,128,1,16,512]{4,3,2,0,1:T(8,128)(2,1)S(1)}, u32[]{:S(2)}, u32[]{:S(2)}) async-start(bf16[1,128,1,16,512]{4,3,2,0,1:T(8,128)(2,1)} %pad_maximum_fusion.1), calls=%async_computation.2 | async-start | bytes 4194304 | tf_op jit(solution)/shard_map/all_to_all | solution.py:161
  128.8 1.4 copy.33.live_ref
  130.2 14.4 %shard_map.91.a_ref = f32[512,768]{1,0:T(8,128)} custom-call(bf16[512,2048]{1,0:T(8,128)(2,1)} %multiply_convert_fusion.q_ref.g_ref, bf16[2048,1536]{1,0:T(8,128)(2,1)} %bitcast.16.k_ref.v_ref, bf16[2048,1536]{1,0:T(8,128)(2,1)} %bitcast.16.k_ref.v_ref, f32[8,2048]{1,0:T(8,128)} %fusion.1.bias_ref, f32[2048,1]{1,0:T(8,128)} %copy.33.live_ref), custom_call_target="tpu_custom_call" | custom-call | tf_op jit(solution)/shard_map/pallas_call | solution.py:52
  144.6 14.2 %all-to-all-done.2 = bf16[1,128,1,16,512]{4,3,2,0,1:T(8,128)(2,1)S(1)} async-done(((bf16[1,128,1,16,512]{4,3,2,0,1:T(8,128)(2,1)}), bf16[1,128,1,16,512]{4,3,2,0,1:T(8,128)(2,1)S(1)}, u32[]{:S(2)}, u32[]{:S(2)}) %all-to-all-start.2) | async-done | bytes 2097184 | tf_op jit(solution)/shard_map/all_to_all | solution.py:161
  158.8 1.3 copy-done.1
  160.2 6.4 %shard_map.92.b_ref = f32[512,256]{1,0:T(8,128)} custom-call(bf16[512,2048]{1,0:T(8,128)(2,1)} %multiply_convert_fusion.q_ref.g_ref, bf16[2048,512]{1,0:T(8,128)(2,1)} %bitcast.34, bf16[2048,512]{1,0:T(8,128)(2,1)} %bitcast.35, f32[8,2048]{1,0:T(8,128)} %fusion.1.bias_ref, f32[2048,1]{1,0:T(8,128)} %copy.33.live_ref), custom_call_target="tpu_custom_call" | custom-call | tf_op jit(solution)/shard_map/pallas_call | solution.py:52
  166.6 5.0 %shard_map.93 = bf16[512,1024]{1,0:T(8,128)(2,1)} custom-call(f32[512,768]{1,0:T(8,128)} %shard_map.91.a_ref, f32[512,256]{1,0:T(8,128)} %shard_map.92.b_ref, bf16[512,2048]{1,0:T(8,128)(2,1)} %multiply_convert_fusion.q_ref.g_ref, bf16[1024,1024]{1,0:T(8,128)(2,1)} %w_ref.1), custom_call_target="tpu_custom_call" | custom-call | tf_op jit(solution)/shard_map/pallas_call | solution.py:82
  171.7 1.5 reshape.120
  173.1 0.0 copy-start.3
  173.1 23.5 %all_to_all.31 = bf16[128,4,1024]{2,1,0:T(4,128)(2,1)S(1)} all-to-all(bf16[128,4,1024]{2,1,0:T(4,128)(2,1)S(1)} %reshape.120), channel_id=1, replica_groups=mesh['req'=16,'cache'=8] {'req','cache'}, dimensions={0} | all-to-all | bytes 2097152 | tf_op jit(solution)/shard_map/all_to_all | solution.py:174
  196.6 0.3 reshape.121
  196.9 0.0 copy-done.3
  196.9 1.3 fusion.2
  (11 shorter events, 0.1 us)
Async XLA Ops:
  0.0 54.6 %copy-start = (f32[8,128]{1,0:T(8,128)S(1)}, f32[8,128]{1,0:T(8,128)}, u32[]{:S(2)}) copy-start(f32[8,128]{1,0:T(8,128)} %param.17) | copy-start | bytes 12292
  7.2 31.9 %all-to-all-start = ((bf16[128,4,1152]{2,1,0:T(4,128)(2,1)}), bf16[128,4,1152]{2,1,0:T(4,128)(2,1)S(1)}, u32[]{:S(2)}, u32[]{:S(2)}) async-start(bf16[128,4,1152]{2,1,0:T(4,128)(2,1)} %fusion.3), calls=%async_computation | async-start | bytes 2359296 | tf_op jit(solution)/shard_map/all_to_all | solution.py:135
  25.5 20.1 %copy-start.4 = (s32[1,128]{1,0:T(1,128)S(1)}, s32[1,128]{1,0:T(1,128)}, u32[]{:S(2)}) copy-start(s32[1,128]{1,0:T(1,128)} %param.12) | copy-start | bytes 1540
  39.1 82.5 %all-to-all-start.1 = ((bf16[1,128,1,16,1536]{4,3,2,0,1:T(8,128)(2,1)}), bf16[1,128,1,16,1536]{4,3,2,0,1:T(8,128)(2,1)}, u32[]{:S(2)}, u32[]{:S(2)}) async-start(bf16[1,128,1,16,1536]{4,3,2,0,1:T(8,128)(2,1)} %pad_maximum_fusion), calls=%async_computation.1 | async-start | bytes 12582912 | tf_op jit(solution)/shard_map/all_to_all | solution.py:137
  51.6 4.1 %copy-start.2 = (f32[512,1024]{1,0:T(8,128)S(1)}, f32[512,1024]{1,0:T(8,128)}, u32[]{:S(2)}) copy-start(f32[512,1024]{1,0:T(8,128)} %reshape.122) | copy-start | bytes 6291460
  121.6 37.2 %all-to-all-start.2 = ((bf16[1,128,1,16,512]{4,3,2,0,1:T(8,128)(2,1)}), bf16[1,128,1,16,512]{4,3,2,0,1:T(8,128)(2,1)S(1)}, u32[]{:S(2)}, u32[]{:S(2)}) async-start(bf16[1,128,1,16,512]{4,3,2,0,1:T(8,128)(2,1)} %pad_maximum_fusion.1), calls=%async_computation.2 | async-start | bytes 4194304 | tf_op jit(solution)/shard_map/all_to_all | solution.py:161
  158.8 1.4 copy-start.1
  173.1 23.8 %copy-start.3 = (bf16[256,1024]{1,0:T(8,128)(2,1)S(1)}, bf16[256,1024]{1,0:T(8,128)(2,1)}, u32[]{:S(2)}) copy-start(bf16[256,1024]{1,0:T(8,128)(2,1)} %param.9) | copy-start | bytes 1572868

commit v18 on v13

--- a/solution.py
+++ b/solution.py
@@ -109,9 +109,11 @@
     event_count = devices * per_owner * block_ev
 
     target = cand_req[:, 0]
-    onehot = (target[:, None] == jnp.arange(devices, dtype=jnp.int32)[None, :]).astype(jnp.int32)
-    earlier = jnp.cumsum(onehot, axis=0) - onehot
-    slot_rank = jnp.sum(earlier * onehot, axis=1)
+    onehot = (target[:, None] == jnp.arange(devices, dtype=jnp.int32)[None, :]).astype(jnp.bfloat16)
+    row_ids = jnp.arange(row_count, dtype=jnp.int32)
+    before = (row_ids[None, :] < row_ids[:, None]).astype(jnp.bfloat16)
+    earlier = jnp.dot(before, onehot, preferred_element_type=jnp.float32)
+    slot_rank = jnp.sum(earlier * onehot.astype(jnp.float32), axis=1).astype(jnp.int32)
     flat_slot = target * capacity + slot_rank
     slot_ids = jnp.arange(devices * capacity, dtype=jnp.int32)
     slot_table = (flat_slot[:, None] == slot_ids[None, :]).astype(cand_x.dtype)

time: 198 us -> 197 us (level)
  no operation moved by 1% of the time
where the time goes in v18:
time: 197 us
  waiting for transfers between devices  89.1 us (45%)
  starting transfers between devices  24.5 us (12%)
  Pallas kernels  23.5 us (12%)
  blocking collectives  23.5 us (12%)
  local copies, waits for them, and re-layouts  13.6 us (7%)
  matrix products  11.3 us (6%)
  other arithmetic  10.3 us (5%)
    all_to_all x1, waiting for transfers between devices, shards(): lax.all_to_all(kv_first, axes, split_axis=1, concat_axis=0, tiled=True)  59.5 us
    all_to_all x1, blocking collectives, shards(): lax.all_to_all(update, axes, split_axis=0, concat_axis=0, tiled=True)  23.5 us
    pallas_call x2, Pallas kernels, attend(): pl.pallas_call(kernel, grid=(head_count,), in_specs=[pl.BlockSpec((slot_c...  18.5 us
    all_to_all x1, waiting for transfers between devices, shards(): lax.all_to_all(kv_second, axes, split_axis=1, concat_axis=0, tiled=True)  16 us
    all_to_all x1, waiting for transfers between devices, shards(): lax.all_to_all(send, axes, split_axis=0, concat_axis=0, tiled=True)  13.6 us
    all_to_all x1, starting transfers between devices, shards(): lax.all_to_all(send, axes, split_axis=0, concat_axis=0, tiled=True)  11.5 us
    all_to_all x1, starting transfers between devices, shards(): lax.all_to_all(kv_second, axes, split_axis=1, concat_axis=0, tiled=True)  7.14 us
    dot_general x1, matrix products, prepare(): jnp.dot(normed, w_proj, preferred_element_type=jnp.float32)  6.42 us
  transfers between devices with their start and end apart: 3, of which 3 were waited for; matrix products, arithmetic and copies ran while one was open for 13% of the time, Pallas kernels for 6%

profile of v18, /device:TPU:1, one launch (start us, length us, event | category | flops | bytes accessed | tf_op | source)
XLA Modules:
  0.0 196.6 jit_solution(11807953898185934463)
XLA Ops:
  0.0 0.0 copy-start
  0.0 0.7 convert_element_type.77
  0.7 0.2 copy.21
  0.9 1.0 fusion.4
  1.9 0.7 multiply_add_fusion
  2.6 1.6 convolution_convert_fusion
  4.2 0.4 reshape.107
  4.6 1.6 fusion.3
  6.2 11.5 %all-to-all-start = ((bf16[128,4,1152]{2,1,0:T(4,128)(2,1)}), bf16[128,4,1152]{2,1,0:T(4,128)(2,1)S(1)}, u32[]{:S(2)}, u32[]{:S(2)}) async-start(bf16[128,4,1152]{2,1,0:T(4,128)(2,1)} %fusion.3), calls=%async_computation | async-start | bytes 2359296 | tf_op jit(solution)/shard_map/all_to_all | solution.py:137
  17.7 3.3 %fusion.15 = (bf16[1,128,1,16,768]{4,3,2,0,1:T(8,128)(2,1)S(1)}, bf16[1,128,1,16,768]{4,3,2,0,1:T(8,128)(2,1)S(1)}) fusion(bf16[1,128,1,16,2048]{4,3,2,0,1:T(8,128)(2,1)} %bitcast.22), kind=kLoop, calls=%fused_computation.39 | loop fusion | bytes 12582912 | tf_op jit(solution)/shard_map/slice | solution.py:132
  21.0 3.5 %pad_maximum_fusion = bf16[1,128,1,16,1536]{4,3,2,0,1:T(8,128)(2,1)} fusion(bf16[1,128,1,16,768]{4,3,2,0,1:T(8,128)(2,1)S(1)} %get-tuple-element.22, bf16[1,128,1,16,768]{4,3,2,0,1:T(8,128)(2,1)S(1)} %get-tuple-element.21), kind=kLoop, calls=%fused_computation | loop fusion | flops 12582912 | bytes 12582912 | tf_op jit(solution)/shard_map/concatenate | solution.py:131
  24.5 0.0 copy-start.4
  24.5 13.6 %all-to-all-done = bf16[128,4,1152]{2,1,0:T(4,128)(2,1)S(1)} async-done(((bf16[128,4,1152]{2,1,0:T(4,128)(2,1)}), bf16[128,4,1152]{2,1,0:T(4,128)(2,1)S(1)}, u32[]{:S(2)}, u32[]{:S(2)}) %all-to-all-start) | async-done | bytes 1179680 | tf_op jit(solution)/shard_map/all_to_all | solution.py:137
  38.1 5.8 %all-to-all-start.1 = ((bf16[1,128,1,16,1536]{4,3,2,0,1:T(8,128)(2,1)}), bf16[1,128,1,16,1536]{4,3,2,0,1:T(8,128)(2,1)}, u32[]{:S(2)}, u32[]{:S(2)}) async-start(bf16[1,128,1,16,1536]{4,3,2,0,1:T(8,128)(2,1)} %pad_maximum_fusion), calls=%async_computation.1 | async-start | bytes 12582912 | tf_op jit(solution)/shard_map/all_to_all | solution.py:139
  44.6 0.0 copy-done.4
  44.6 0.1 select_reduce_fusion
  44.7 0.1 fusion.13
  44.8 0.1 reshape.114
  44.9 1.7 fusion.14
  46.6 1.6 pad_maximum_fusion.1
  48.2 0.6 slice_convert_fusion
  48.9 1.7 reshape.112
  50.6 0.0 copy-start.2
  50.6 0.5 convert_reduce_fusion
  51.1 0.7 div.13
  51.8 0.8 multiply_reduce_fusion
  52.6 0.7 rsqrt.12
  53.3 0.1 slice_convert_fusion.1
  53.4 0.3 reshape.113
  53.6 0.0 copy-done
  53.6 1.1 fusion.1.bias_ref
  54.7 0.0 copy-done.2
  54.7 6.4 %multiply_convert_fusion.q_ref.g_ref = bf16[512,2048]{1,0:T(8,128)(2,1)} fusion(bf16[1024,2048]{1,0:T(8,128)(2,1)} %param.15, f32[512,1024]{1,0:T(8,128)S(1)} %copy-done.2, f32[512]{0:T(512)} %rsqrt.12, f32[512]{0:T(512)} %div.13), kind=kOutput, calls=%fused_computation.1 | convolution fusion | flops 2154299392 | bytes 8392704 | tf_op jit(solution)/shard_map/dot_general | solution.py:21
  61.1 59.5 %all-to-all-done.1 = bf16[1,128,1,16,1536]{4,3,2,0,1:T(8,128)(2,1)} async-done(((bf16[1,128,1,16,1536]{4,3,2,0,1:T(8,128)(2,1)}), bf16[1,128,1,16,1536]{4,3,2,0,1:T(8,128)(2,1)}, u32[]{:S(2)}, u32[]{:S(2)}) %all-to-all-start.1) | async-done | bytes 6291488 | tf_op jit(solution)/shard_map/all_to_all | solution.py:139
  120.6 7.1 %all-to-all-start.2 = ((bf16[1,128,1,16,512]{4,3,2,0,1:T(8,128)(2,1)}), bf16[1,128,1,16,512]{4,3,2,0,1:T(8,128)(2,1)S(1)}, u32[]{:S(2)}, u32[]{:S(2)}) async-start(bf16[1,128,1,16,512]{4,3,2,0,1:T(8,128)(2,1)} %pad_maximum_fusion.1), calls=%async_computation.2 | async-start | bytes 4194304 | tf_op jit(solution)/shard_map/all_to_all | solution.py:163
  127.8 1.5 copy.26.live_ref
  129.3 12.7 %shard_map.91.a_ref = f32[512,768]{1,0:T(8,128)} custom-call(bf16[512,2048]{1,0:T(8,128)(2,1)} %multiply_convert_fusion.q_ref.g_ref, bf16[2048,1536]{1,0:T(8,128)(2,1)} %bitcast.12.k_ref.v_ref, bf16[2048,1536]{1,0:T(8,128)(2,1)} %bitcast.12.k_ref.v_ref, f32[8,2048]{1,0:T(8,128)} %fusion.1.bias_ref, f32[2048,1]{1,0:T(8,128)} %copy.26.live_ref), custom_call_target="tpu_custom_call" | custom-call | tf_op jit(solution)/shard_map/pallas_call | solution.py:52
  141.9 16.0 %all-to-all-done.2 = bf16[1,128,1,16,512]{4,3,2,0,1:T(8,128)(2,1)S(1)} async-done(((bf16[1,128,1,16,512]{4,3,2,0,1:T(8,128)(2,1)}), bf16[1,128,1,16,512]{4,3,2,0,1:T(8,128)(2,1)S(1)}, u32[]{:S(2)}, u32[]{:S(2)}) %all-to-all-start.2) | async-done | bytes 2097184 | tf_op jit(solution)/shard_map/all_to_all | solution.py:163
  157.9 0.0 copy-start.1
  157.9 1.3 copy-done.1
  159.2 5.9 %shard_map.92.b_ref = f32[512,256]{1,0:T(8,128)} custom-call(bf16[512,2048]{1,0:T(8,128)(2,1)} %multiply_convert_fusion.q_ref.g_ref, bf16[2048,512]{1,0:T(8,128)(2,1)} %bitcast.20, bf16[2048,512]{1,0:T(8,128)(2,1)} %bitcast.21, f32[8,2048]{1,0:T(8,128)} %fusion.1.bias_ref, f32[2048,1]{1,0:T(8,128)} %copy.26.live_ref), custom_call_target="tpu_custom_call" | custom-call | tf_op jit(solution)/shard_map/pallas_call | solution.py:52
  165.1 5.0 %shard_map.93 = bf16[512,1024]{1,0:T(8,128)(2,1)} custom-call(f32[512,768]{1,0:T(8,128)} %shard_map.91.a_ref, f32[512,256]{1,0:T(8,128)} %shard_map.92.b_ref, bf16[512,2048]{1,0:T(8,128)(2,1)} %multiply_convert_fusion.q_ref.g_ref, bf16[1024,1024]{1,0:T(8,128)(2,1)} %w_ref.1), custom_call_target="tpu_custom_call" | custom-call | tf_op jit(solution)/shard_map/pallas_call | solution.py:82
  170.1 1.5 reshape.110
  171.6 0.0 copy-start.3
  171.6 23.5 %all_to_all.31 = bf16[128,4,1024]{2,1,0:T(4,128)(2,1)S(1)} all-to-all(bf16[128,4,1024]{2,1,0:T(4,128)(2,1)S(1)} %reshape.110), channel_id=1, replica_groups=mesh['req'=16,'cache'=8] {'req','cache'}, dimensions={0} | all-to-all | bytes 2097152 | tf_op jit(solution)/shard_map/all_to_all | solution.py:176
  195.1 0.3 reshape.111
  195.3 0.0 copy-done.3
  195.3 1.3 fusion.2
  (4 shorter events, 0.0 us)
Async XLA Ops:
  0.0 53.6 %copy-start = (f32[8,128]{1,0:T(8,128)S(1)}, f32[8,128]{1,0:T(8,128)}, u32[]{:S(2)}) copy-start(f32[8,128]{1,0:T(8,128)} %param.17) | copy-start | bytes 12292
  6.2 31.9 %all-to-all-start = ((bf16[128,4,1152]{2,1,0:T(4,128)(2,1)}), bf16[128,4,1152]{2,1,0:T(4,128)(2,1)S(1)}, u32[]{:S(2)}, u32[]{:S(2)}) async-start(bf16[128,4,1152]{2,1,0:T(4,128)(2,1)} %fusion.3), calls=%async_computation | async-start | bytes 2359296 | tf_op jit(solution)/shard_map/all_to_all | solution.py:137
  24.5 20.1 %copy-start.4 = (s32[1,128]{1,0:T(1,128)S(1)}, s32[1,128]{1,0:T(1,128)}, u32[]{:S(2)}) copy-start(s32[1,128]{1,0:T(1,128)} %param.12) | copy-start | bytes 1540
  38.1 82.5 %all-to-all-start.1 = ((bf16[1,128,1,16,1536]{4,3,2,0,1:T(8,128)(2,1)}), bf16[1,128,1,16,1536]{4,3,2,0,1:T(8,128)(2,1)}, u32[]{:S(2)}, u32[]{:S(2)}) async-start(bf16[1,128,1,16,1536]{4,3,2,0,1:T(8,128)(2,1)} %pad_maximum_fusion), calls=%async_computation.1 | async-start | bytes 12582912 | tf_op jit(solution)/shard_map/all_to_all | solution.py:139
  50.6 4.1 %copy-start.2 = (f32[512,1024]{1,0:T(8,128)S(1)}, f32[512,1024]{1,0:T(8,128)}, u32[]{:S(2)}) copy-start(f32[512,1024]{1,0:T(8,128)} %reshape.112) | copy-start | bytes 6291460
  120.6 37.2 %all-to-all-start.2 = ((bf16[1,128,1,16,512]{4,3,2,0,1:T(8,128)(2,1)}), bf16[1,128,1,16,512]{4,3,2,0,1:T(8,128)(2,1)S(1)}, u32[]{:S(2)}, u32[]{:S(2)}) async-start(bf16[1,128,1,16,512]{4,3,2,0,1:T(8,128)(2,1)} %pad_maximum_fusion.1), calls=%async_computation.2 | async-start | bytes 4194304 | tf_op jit(solution)/shard_map/all_to_all | solution.py:163
  157.9 1.3 copy-start.1
  171.6 23.7 %copy-start.3 = (bf16[256,1024]{1,0:T(8,128)(2,1)S(1)}, bf16[256,1024]{1,0:T(8,128)(2,1)}, u32[]{:S(2)}) copy-start(bf16[256,1024]{1,0:T(8,128)(2,1)} %param.9) | copy-start | bytes 1572868

commit v19 on v18

--- a/solution.py
+++ b/solution.py
@@ -71,7 +71,8 @@
     spread = jnp.mean(centred * centred, axis=-1, keepdims=True)
     normal = centred * lax.rsqrt(spread + 1e-05)
     hidden = (normal * g_ref[...].astype(jnp.float32)).astype(jnp.bfloat16)
-    o_ref[...] = jnp.dot(hidden, w_ref[...], preferred_element_type=jnp.float32).astype(o_ref.dtype)
+    result = jnp.dot(hidden, w_ref[...], preferred_element_type=jnp.float32).astype(o_ref.dtype)
+    o_ref[...] = result.reshape(o_ref.shape)
 
 
 def finish(first_half, second_half, projected, w_out):
@@ -88,8 +89,8 @@
             pl.BlockSpec((tile, features), lambda i: (i, 0)),
             pl.BlockSpec(w_out.shape, lambda i: (0, 0)),
         ],
-        out_specs=pl.BlockSpec((tile, w_out.shape[1]), lambda i: (i, 0)),
-        out_shape=jax.ShapeDtypeStruct((slot_count, w_out.shape[1]), jnp.bfloat16),
+        out_specs=pl.BlockSpec((tile // 4, 4, w_out.shape[1]), lambda i: (i, 0, 0)),
+        out_shape=jax.ShapeDtypeStruct((slot_count // 4, 4, w_out.shape[1]), jnp.bfloat16),
     )(first_half, second_half, projected, w_out)
 
 

time: 197 us -> 197 us (level)
  no operation moved by 1% of the time
where the time goes in v19:
time: 197 us; the launch traced here: 196 us
  waiting for transfers between devices  89.1 us (45%)
  starting transfers between devices  24.5 us (12%)
  blocking collectives  24.3 us (12%)
  Pallas kernels  23.6 us (12%)
  local copies, waits for them, and re-layouts  12.1 us (6%)
  matrix products  11.3 us (6%)
  other arithmetic  10.3 us (5%)
    all_to_all x1, waiting for transfers between devices, shards(): lax.all_to_all(kv_first, axes, split_axis=1, concat_axis=0, tiled=True)  59.5 us
    all_to_all x1, blocking collectives, shards(): lax.all_to_all(update, axes, split_axis=0, concat_axis=0, tiled=True)  24.3 us
    pallas_call x2, Pallas kernels, attend(): pl.pallas_call(kernel, grid=(head_count,), in_specs=[pl.BlockSpec((slot_c...  18.5 us
    all_to_all x1, waiting for transfers between devices, shards(): lax.all_to_all(kv_second, axes, split_axis=1, concat_axis=0, tiled=True)  16 us
    all_to_all x1, waiting for transfers between devices, shards(): lax.all_to_all(send, axes, split_axis=0, concat_axis=0, tiled=True)  13.6 us
    all_to_all x1, starting transfers between devices, shards(): lax.all_to_all(send, axes, split_axis=0, concat_axis=0, tiled=True)  11.5 us
    all_to_all x1, starting transfers between devices, shards(): lax.all_to_all(kv_second, axes, split_axis=1, concat_axis=0, tiled=True)  7.14 us
    dot_general x1, matrix products, prepare(): jnp.dot(normed, w_proj, preferred_element_type=jnp.float32)  6.42 us
  transfers between devices with their start and end apart: 3, of which 3 were waited for; matrix products, arithmetic and copies ran while one was open for 13% of the time, Pallas kernels for 6%

profile of v19, /device:TPU:1, one launch (start us, length us, event | category | flops | bytes accessed | tf_op | source)
XLA Modules:
  0.0 196.0 jit_solution(12470214794114786489)
XLA Ops:
  0.0 0.0 copy-start
  0.0 0.7 convert_element_type.77
  0.7 0.2 copy.21
  0.9 1.0 fusion.4
  1.9 0.7 multiply_add_fusion
  2.6 1.6 convolution_convert_fusion
  4.2 0.4 reshape.104
  4.6 1.6 fusion.3
  6.2 11.5 %all-to-all-start = ((bf16[128,4,1152]{2,1,0:T(4,128)(2,1)}), bf16[128,4,1152]{2,1,0:T(4,128)(2,1)S(1)}, u32[]{:S(2)}, u32[]{:S(2)}) async-start(bf16[128,4,1152]{2,1,0:T(4,128)(2,1)} %fusion.3), calls=%async_computation | async-start | bytes 2359296 | tf_op jit(solution)/shard_map/all_to_all | solution.py:138
  17.7 3.3 %fusion.15 = (bf16[1,128,1,16,768]{4,3,2,0,1:T(8,128)(2,1)S(1)}, bf16[1,128,1,16,768]{4,3,2,0,1:T(8,128)(2,1)S(1)}) fusion(bf16[1,128,1,16,2048]{4,3,2,0,1:T(8,128)(2,1)} %bitcast.22), kind=kLoop, calls=%fused_computation.39 | loop fusion | bytes 12582912 | tf_op jit(solution)/shard_map/slice | solution.py:133
  21.0 3.5 %pad_maximum_fusion = bf16[1,128,1,16,1536]{4,3,2,0,1:T(8,128)(2,1)} fusion(bf16[1,128,1,16,768]{4,3,2,0,1:T(8,128)(2,1)S(1)} %get-tuple-element.22, bf16[1,128,1,16,768]{4,3,2,0,1:T(8,128)(2,1)S(1)} %get-tuple-element.21), kind=kLoop, calls=%fused_computation | loop fusion | flops 12582912 | bytes 12582912 | tf_op jit(solution)/shard_map/concatenate | solution.py:132
  24.5 0.0 copy-start.4
  24.5 13.6 %all-to-all-done = bf16[128,4,1152]{2,1,0:T(4,128)(2,1)S(1)} async-done(((bf16[128,4,1152]{2,1,0:T(4,128)(2,1)}), bf16[128,4,1152]{2,1,0:T(4,128)(2,1)S(1)}, u32[]{:S(2)}, u32[]{:S(2)}) %all-to-all-start) | async-done | bytes 1179680 | tf_op jit(solution)/shard_map/all_to_all | solution.py:138
  38.1 5.8 %all-to-all-start.1 = ((bf16[1,128,1,16,1536]{4,3,2,0,1:T(8,128)(2,1)}), bf16[1,128,1,16,1536]{4,3,2,0,1:T(8,128)(2,1)}, u32[]{:S(2)}, u32[]{:S(2)}) async-start(bf16[1,128,1,16,1536]{4,3,2,0,1:T(8,128)(2,1)} %pad_maximum_fusion), calls=%async_computation.1 | async-start | bytes 12582912 | tf_op jit(solution)/shard_map/all_to_all | solution.py:140
  44.6 0.0 copy-done.4
  44.6 0.1 select_reduce_fusion
  44.7 0.1 fusion.13
  44.8 0.1 reshape.110
  44.9 1.7 fusion.14
  46.6 1.6 pad_maximum_fusion.1
  48.2 0.6 slice_convert_fusion
  48.9 1.7 reshape.108
  50.6 0.0 copy-start.2
  50.6 0.5 convert_reduce_fusion
  51.1 0.7 div.13
  51.8 0.8 multiply_reduce_fusion
  52.6 0.7 rsqrt.12
  53.3 0.1 slice_convert_fusion.1
  53.4 0.3 reshape.109
  53.6 0.0 copy-done
  53.6 1.1 fusion.1.bias_ref
  54.7 0.0 copy-done.2
  54.7 6.4 %multiply_convert_fusion.q_ref.g_ref = bf16[512,2048]{1,0:T(8,128)(2,1)} fusion(bf16[1024,2048]{1,0:T(8,128)(2,1)} %param.15, f32[512,1024]{1,0:T(8,128)S(1)} %copy-done.2, f32[512]{0:T(512)} %rsqrt.12, f32[512]{0:T(512)} %div.13), kind=kOutput, calls=%fused_computation.1 | convolution fusion | flops 2154299392 | bytes 8392704 | tf_op jit(solution)/shard_map/dot_general | solution.py:21
  61.1 59.5 %all-to-all-done.1 = bf16[1,128,1,16,1536]{4,3,2,0,1:T(8,128)(2,1)} async-done(((bf16[1,128,1,16,1536]{4,3,2,0,1:T(8,128)(2,1)}), bf16[1,128,1,16,1536]{4,3,2,0,1:T(8,128)(2,1)}, u32[]{:S(2)}, u32[]{:S(2)}) %all-to-all-start.1) | async-done | bytes 6291488 | tf_op jit(solution)/shard_map/all_to_all | solution.py:140
  120.6 7.1 %all-to-all-start.2 = ((bf16[1,128,1,16,512]{4,3,2,0,1:T(8,128)(2,1)}), bf16[1,128,1,16,512]{4,3,2,0,1:T(8,128)(2,1)S(1)}, u32[]{:S(2)}, u32[]{:S(2)}) async-start(bf16[1,128,1,16,512]{4,3,2,0,1:T(8,128)(2,1)} %pad_maximum_fusion.1), calls=%async_computation.2 | async-start | bytes 4194304 | tf_op jit(solution)/shard_map/all_to_all | solution.py:164
  127.8 1.5 copy.26.live_ref
  129.3 12.7 %shard_map.91.a_ref = f32[512,768]{1,0:T(8,128)} custom-call(bf16[512,2048]{1,0:T(8,128)(2,1)} %multiply_convert_fusion.q_ref.g_ref, bf16[2048,1536]{1,0:T(8,128)(2,1)} %bitcast.12.k_ref.v_ref, bf16[2048,1536]{1,0:T(8,128)(2,1)} %bitcast.12.k_ref.v_ref, f32[8,2048]{1,0:T(8,128)} %fusion.1.bias_ref, f32[2048,1]{1,0:T(8,128)} %copy.26.live_ref), custom_call_target="tpu_custom_call" | custom-call | tf_op jit(solution)/shard_map/pallas_call | solution.py:52
  141.9 16.0 %all-to-all-done.2 = bf16[1,128,1,16,512]{4,3,2,0,1:T(8,128)(2,1)S(1)} async-done(((bf16[1,128,1,16,512]{4,3,2,0,1:T(8,128)(2,1)}), bf16[1,128,1,16,512]{4,3,2,0,1:T(8,128)(2,1)S(1)}, u32[]{:S(2)}, u32[]{:S(2)}) %all-to-all-start.2) | async-done | bytes 2097184 | tf_op jit(solution)/shard_map/all_to_all | solution.py:164
  157.9 0.0 copy-start.1
  157.9 1.3 copy-done.1
  159.2 5.9 %shard_map.92.b_ref = f32[512,256]{1,0:T(8,128)} custom-call(bf16[512,2048]{1,0:T(8,128)(2,1)} %multiply_convert_fusion.q_ref.g_ref, bf16[2048,512]{1,0:T(8,128)(2,1)} %bitcast.20, bf16[2048,512]{1,0:T(8,128)(2,1)} %bitcast.21, f32[8,2048]{1,0:T(8,128)} %fusion.1.bias_ref, f32[2048,1]{1,0:T(8,128)} %copy.26.live_ref), custom_call_target="tpu_custom_call" | custom-call | tf_op jit(solution)/shard_map/pallas_call | solution.py:52
  165.1 5.1 %shard_map.93 = bf16[128,4,1024]{2,1,0:T(4,128)(2,1)} custom-call(f32[512,768]{1,0:T(8,128)} %shard_map.91.a_ref, f32[512,256]{1,0:T(8,128)} %shard_map.92.b_ref, bf16[512,2048]{1,0:T(8,128)(2,1)} %multiply_convert_fusion.q_ref.g_ref, bf16[1024,1024]{1,0:T(8,128)(2,1)} %w_ref.1), custom_call_target="tpu_custom_call" | custom-call | tf_op jit(solution)/shard_map/pallas_call | solution.py:83
  170.1 0.0 copy-start.3
  170.1 24.3 %all_to_all.31 = bf16[128,4,1024]{2,1,0:T(4,128)(2,1)S(1)} all-to-all(bf16[128,4,1024]{2,1,0:T(4,128)(2,1)} %shard_map.93), channel_id=1, replica_groups=mesh['req'=16,'cache'=8] {'req','cache'}, dimensions={0} | all-to-all | bytes 2097152 | tf_op jit(solution)/shard_map/all_to_all | solution.py:177
  194.5 0.3 reshape.107
  194.7 0.0 copy-done.3
  194.8 1.3 fusion.2
  (4 shorter events, 0.0 us)
Async XLA Ops:
  0.0 53.6 %copy-start = (f32[8,128]{1,0:T(8,128)S(1)}, f32[8,128]{1,0:T(8,128)}, u32[]{:S(2)}) copy-start(f32[8,128]{1,0:T(8,128)} %param.17) | copy-start | bytes 12292
  6.2 31.9 %all-to-all-start = ((bf16[128,4,1152]{2,1,0:T(4,128)(2,1)}), bf16[128,4,1152]{2,1,0:T(4,128)(2,1)S(1)}, u32[]{:S(2)}, u32[]{:S(2)}) async-start(bf16[128,4,1152]{2,1,0:T(4,128)(2,1)} %fusion.3), calls=%async_computation | async-start | bytes 2359296 | tf_op jit(solution)/shard_map/all_to_all | solution.py:138
  24.5 20.1 %copy-start.4 = (s32[1,128]{1,0:T(1,128)S(1)}, s32[1,128]{1,0:T(1,128)}, u32[]{:S(2)}) copy-start(s32[1,128]{1,0:T(1,128)} %param.12) | copy-start | bytes 1540
  38.1 82.5 %all-to-all-start.1 = ((bf16[1,128,1,16,1536]{4,3,2,0,1:T(8,128)(2,1)}), bf16[1,128,1,16,1536]{4,3,2,0,1:T(8,128)(2,1)}, u32[]{:S(2)}, u32[]{:S(2)}) async-start(bf16[1,128,1,16,1536]{4,3,2,0,1:T(8,128)(2,1)} %pad_maximum_fusion), calls=%async_computation.1 | async-start | bytes 12582912 | tf_op jit(solution)/shard_map/all_to_all | solution.py:140
  50.6 4.1 %copy-start.2 = (f32[512,1024]{1,0:T(8,128)S(1)}, f32[512,1024]{1,0:T(8,128)}, u32[]{:S(2)}) copy-start(f32[512,1024]{1,0:T(8,128)} %reshape.108) | copy-start | bytes 6291460
  120.6 37.2 %all-to-all-start.2 = ((bf16[1,128,1,16,512]{4,3,2,0,1:T(8,128)(2,1)}), bf16[1,128,1,16,512]{4,3,2,0,1:T(8,128)(2,1)S(1)}, u32[]{:S(2)}, u32[]{:S(2)}) async-start(bf16[1,128,1,16,512]{4,3,2,0,1:T(8,128)(2,1)} %pad_maximum_fusion.1), calls=%async_computation.2 | async-start | bytes 4194304 | tf_op jit(solution)/shard_map/all_to_all | solution.py:164
  157.9 1.3 copy-start.1
  170.1 24.6 %copy-start.3 = (bf16[256,1024]{1,0:T(8,128)(2,1)S(1)}, bf16[256,1024]{1,0:T(8,128)(2,1)}, u32[]{:S(2)}) copy-start(bf16[256,1024]{1,0:T(8,128)(2,1)} %param.9) | copy-start | bytes 1572868
